TPU v7x, 256 devices: a whole 4x4x8 slice. The times are simulated.
256 devices in a mesh: dp: 16 (over z, core), expert: 16 (over x, y).
Axes of the slice: x: 4, y: 4, z: 8, core: 2. Of those that a mesh axis runs over, the one named last changes fastest.
Arguments:
- hidden_in: bfloat16 [16384, 2048], P(('dp', 'expert')), parts along dimension 0, may hold values from -6 to 6
- route_ids: int32 [16384, 8], P(('dp', 'expert')), parts along dimension 0, may hold values from 0 to 15, all different within a row; in each aligned block of 64 rows (0 to 63, 64 to 127, ...) at most 64 rows name the same one
- gates: float32 [16384, 8], P(('dp', 'expert')), parts along dimension 0, may hold values from 0.05 to 1
- w_in: bfloat16 [16, 2048, 1536], P('expert'), may hold values from -0.125 to 0.125
- w_out: bfloat16 [16, 768, 2048], P('expert'), may hold values from -0.21875 to 0.21875
Outputs:
- combined: bfloat16 [16384, 2048], P(('dp', 'expert')), parts along dimension 0
There are 16 independent parts, one for each index of `dp`. A program takes and returns all parts, laid end to end along the dimension named above; an argument that names none is the same for every part. Nothing has to cross between parts.
Inputs may be any that keep to these rules, and one draw needn't show every extreme that they name: `route_ids`: each row names 8 different experts. Among the rows of one device (aligned blocks of 64 rows) no expert is named by more than 64 rows, and in every draw some expert is named by exactly 64 rows of some block.
All inputs are finite; a program needn't handle non-finite values.
Results may differ from a plain program's by a relative error of at most 0.0085.
Values may be sent and summed in bfloat16 or wider, within the bound.
No kernel may reach another device: no remote copies, remote signals or barrier semaphores. Data moves between devices by JAX's collectives and lax.ppermute only.
A program may use at most 64 MiB of HBM per device.

v0:
```python
import jax
import jax.numpy as jnp
from jax import lax
from jax.sharding import PartitionSpec as P

SIDE = 4
PAD = 128


def shift(tree, axis, step):
    pairs = []
    for x in range(SIDE):
        for y in range(SIDE):
            if axis == "x":
                pairs.append((x * SIDE + y, ((x + step) % SIDE) * SIDE + y))
            else:
                pairs.append((x * SIDE + y, x * SIDE + (y + step) % SIDE))
    return lax.ppermute(tree, "expert", pairs)


def gather_ring(tree, axis):
    right = shift(tree, axis, -1)
    left = shift(tree, axis, 1)
    cut = jax.tree.leaves(tree)[0].shape[0] // 2
    far_a = shift(jax.tree.map(lambda v: v[:cut], left), axis, 1)
    far_b = shift(jax.tree.map(lambda v: v[cut:], right), axis, -1)
    far = jax.tree.map(lambda a, b: jnp.concatenate([a, b], axis=0), far_a, far_b)
    return jax.tree.map(lambda *vs: jnp.concatenate(vs, axis=0), tree, right, far, left)


def scatter_ring(parts, axis):
    cut = parts.shape[1] // 2
    got_a = shift(parts[2, :cut].astype(jnp.bfloat16), axis, 1)
    got_b = shift(parts[2, cut:].astype(jnp.bfloat16), axis, -1)
    to_right = jnp.concatenate([parts[1, :cut] + got_a.astype(jnp.float32), parts[1, cut:]], axis=0)
    to_left = jnp.concatenate([parts[3, :cut], parts[3, cut:] + got_b.astype(jnp.float32)], axis=0)
    from_left = shift(to_right.astype(jnp.bfloat16), axis, 1)
    from_right = shift(to_left.astype(jnp.bfloat16), axis, -1)
    return parts[0] + from_left.astype(jnp.float32) + from_right.astype(jnp.float32)


def expert_rows(rows, me, width, w_in, w_out):
    half = w_out.shape[0]
    count = SIDE * SIDE
    experts = jnp.arange(count, dtype=jnp.int32)
    high = rows[:, width:width + count].astype(jnp.float32)
    low = rows[:, width + count:width + 2 * count].astype(jnp.float32)
    mine = jnp.sum(jnp.where(experts[None, :] == me, high + low, jnp.float32(0.0)), axis=1)
    projected = jnp.dot(rows[:, :width], w_in, preferred_element_type=jnp.float32)
    inner = (jax.nn.silu(projected[:, :half]) * projected[:, half:]).astype(jnp.bfloat16)
    produced = jnp.dot(inner, w_out, preferred_element_type=jnp.float32).astype(jnp.bfloat16)
    return mine[:, None] * produced.astype(jnp.float32)


def body(hidden_in, route_ids, gates, w_in, w_out):
    assert lax.axis_size("expert") == SIDE * SIDE
    me = lax.axis_index("expert")
    count, width = hidden_in.shape
    experts = jnp.arange(SIDE * SIDE, dtype=jnp.int32)
    table = jnp.sum(
        jnp.where(route_ids[:, :, None] == experts, gates[:, :, None], jnp.float32(0.0)), axis=1
    )
    high = table.astype(jnp.bfloat16)
    low = (table - high.astype(jnp.float32)).astype(jnp.bfloat16)
    extra = jnp.zeros((count, PAD - 2 * SIDE * SIDE), jnp.bfloat16)
    payload = jnp.concatenate([hidden_in, high, low, extra], axis=1)
    split = count // 2
    orders = (("x", "y"), ("y", "x"))
    gathered = []
    for i, (first, second) in enumerate(orders):
        own = payload[i * split:(i + 1) * split]
        gathered.append(gather_ring(gather_ring(own, first), second))
    rows = jnp.concatenate(gathered, axis=0)
    weighted = expert_rows(rows, me, width, w_in[0], w_out[0])
    outs = []
    for i, (first, second) in enumerate(orders):
        part = weighted[i * 16 * split:(i + 1) * 16 * split].reshape(SIDE, SIDE * split, width)
        stage = scatter_ring(part, second).reshape(SIDE, split, width)
        outs.append(scatter_ring(stage, first))
    return jnp.concatenate(outs, axis=0).astype(jnp.bfloat16)


def solution(mesh):
    placed = (
        P(("dp", "expert"), None),
        P(("dp", "expert"), None),
        P(("dp", "expert"), None),
        P("expert", None, None),
        P("expert", None, None),
    )
    return jax.shard_map(
        body, mesh=mesh, in_specs=placed, out_specs=P(("dp", "expert"), None), check_vma=False
    )
```

profile of v0, /device:TPU:64, one launch (start us, length us, event | category | flops | bytes accessed | tf_op | source)
XLA Modules:
  0.0 137.3 jit_solution(11090389823463112007)
XLA Ops:
  4.4 1.7 %collective-permute-start = (bf16[32,2176]{1,0:T(8,128)(2,1)S(1)}, bf16[32,2176]{1,0:T(8,128)(2,1)S(1)}, u32[]{:S(2)}, u32[]{:S(2)}) collective-permute-start(bf16[32,2176]{1,0:T(8,128)(2,1)S(1)} %get-tuple-element.39), channel_id=1, source_target_pairs={{0,12},{1,13},{2,14},{3,15},{4,0},{5,1},{6,2},{7,3},{8,4},{9,5},{1... | collective-permute-start | bytes 417800 | tf_op jit(solution)/shard_map/ppermute | solution.py:18
  6.1 3.4 %collective-permute-done.1 = bf16[32,2176]{1,0:T(8,128)(2,1)S(1)} collective-permute-done((bf16[32,2176]{1,0:T(8,128)(2,1)S(1)}, bf16[32,2176]{1,0:T(8,128)(2,1)S(1)}, u32[]{:S(2)}, u32[]{:S(2)}) %collective-permute-start.1) | collective-permute-done | bytes 139296 | tf_op jit(solution)/shard_map/ppermute | solution.py:18
  9.8 3.0 %collective-permute-start.3 = (bf16[16,2176]{1,0:T(8,128)(2,1)S(1)}, bf16[16,2176]{1,0:T(8,128)(2,1)S(1)}, u32[]{:S(2)}, u32[]{:S(2)}) collective-permute-start(bf16[16,2176]{1,0:T(8,128)(2,1)S(1)} %slice.204), channel_id=1, source_target_pairs={{0,12},{1,13},{2,14},{3,15},{4,0},{5,1},{6,2},{7,3},{8,4},{9,5},{1... | collective-permute-start | bytes 208904 | tf_op jit(solution)/shard_map/ppermute | solution.py:18
  12.8 2.2 %collective-permute-done.2 = bf16[16,2176]{1,0:T(8,128)(2,1)S(1)} collective-permute-done((bf16[16,2176]{1,0:T(8,128)(2,1)S(1)}, bf16[16,2176]{1,0:T(8,128)(2,1)S(1)}, u32[]{:S(2)}, u32[]{:S(2)}) %collective-permute-start.2) | collective-permute-done | bytes 69664 | tf_op jit(solution)/shard_map/ppermute | solution.py:18
  16.8 1.7 %collective-permute-start.4 = (bf16[128,2176]{1,0:T(8,128)(2,1)S(1)}, bf16[128,2176]{1,0:T(8,128)(2,1)S(1)}, u32[]{:S(2)}, u32[]{:S(2)}) collective-permute-start(bf16[128,2176]{1,0:T(8,128)(2,1)S(1)} %get-tuple-element.44), channel_id=1, source_target_pairs={{0,3},{1,0},{2,1},{3,2},{4,7},{5,4},{6,5},{7,6},{8,11},{9,8},{10,9... | collective-permute-start | bytes 1671176 | tf_op jit(solution)/shard_map/ppermute | solution.py:18
  18.8 2.9 %collective-permute-start.8 = (bf16[32,2176]{1,0:T(8,128)(2,1)S(1)}, bf16[32,2176]{1,0:T(8,128)(2,1)S(1)}, u32[]{:S(2)}, u32[]{:S(2)}) collective-permute-start(bf16[32,2176]{1,0:T(8,128)(2,1)S(1)} %get-tuple-element.38), channel_id=1, source_target_pairs={{0,3},{1,0},{2,1},{3,2},{4,7},{5,4},{6,5},{7,6},{8,11},{9,8},{10,9... | collective-permute-start | bytes 417800 | tf_op jit(solution)/shard_map/ppermute | solution.py:18
  21.6 10.1 %collective-permute-done.9 = bf16[32,2176]{1,0:T(8,128)(2,1)S(1)} collective-permute-done((bf16[32,2176]{1,0:T(8,128)(2,1)S(1)}, bf16[32,2176]{1,0:T(8,128)(2,1)S(1)}, u32[]{:S(2)}, u32[]{:S(2)}) %collective-permute-start.9) | collective-permute-done | bytes 139296 | tf_op jit(solution)/shard_map/ppermute | solution.py:18
  32.5 2.6 %collective-permute-start.11 = (bf16[16,2176]{1,0:T(8,128)(2,1)S(1)}, bf16[16,2176]{1,0:T(8,128)(2,1)S(1)}, u32[]{:S(2)}, u32[]{:S(2)}) collective-permute-start(bf16[16,2176]{1,0:T(8,128)(2,1)S(1)} %slice.209), channel_id=1, source_target_pairs={{0,3},{1,0},{2,1},{3,2},{4,7},{5,4},{6,5},{7,6},{8,11},{9,8},{10,9... | collective-permute-start | bytes 208904 | tf_op jit(solution)/shard_map/ppermute | solution.py:18
  35.3 3.3 %collective-permute-start.7 = (bf16[64,2176]{1,0:T(8,128)(2,1)S(1)}, bf16[64,2176]{1,0:T(8,128)(2,1)S(1)}, u32[]{:S(2)}, u32[]{:S(2)}) collective-permute-start(bf16[64,2176]{1,0:T(8,128)(2,1)S(1)} %slice.206), channel_id=1, source_target_pairs={{0,3},{1,0},{2,1},{3,2},{4,7},{5,4},{6,5},{7,6},{8,11},{9,8},{10,9... | collective-permute-start | bytes 835592 | tf_op jit(solution)/shard_map/ppermute | solution.py:18
  38.6 4.4 %collective-permute-done.6 = bf16[64,2176]{1,0:T(8,128)(2,1)S(1)} collective-permute-done((bf16[64,2176]{1,0:T(8,128)(2,1)S(1)}, bf16[64,2176]{1,0:T(8,128)(2,1)S(1)}, u32[]{:S(2)}, u32[]{:S(2)}) %collective-permute-start.6) | collective-permute-done | bytes 278560 | tf_op jit(solution)/shard_map/ppermute | solution.py:18
  45.8 2.1 %copy-done.1 = bf16[1024,2176]{1,0:T(8,128)(2,1)} copy-done((bf16[1024,2176]{1,0:T(8,128)(2,1)}, bf16[1024,2176]{1,0:T(8,128)(2,1)S(1)}, u32[]{:S(2)}) %copy-start.1) | copy-done | bytes 4456472
  48.5 2.6 %collective-permute-start.12 = (bf16[128,2176]{1,0:T(8,128)(2,1)}, bf16[128,2176]{1,0:T(8,128)(2,1)}, u32[]{:S(2)}, u32[]{:S(2)}) collective-permute-start(bf16[128,2176]{1,0:T(8,128)(2,1)} %get-tuple-element.40), channel_id=1, source_target_pairs={{0,12},{1,13},{2,14},{3,15},{4,0},{5,1},{6,2},{7,3},{8,4},{9,5},{1... | collective-permute-start | bytes 1671176 | tf_op jit(solution)/shard_map/ppermute | solution.py:18
  51.1 8.9 %collective-permute-done.13 = bf16[128,2176]{1,0:T(8,128)(2,1)} collective-permute-done((bf16[128,2176]{1,0:T(8,128)(2,1)}, bf16[128,2176]{1,0:T(8,128)(2,1)}, u32[]{:S(2)}, u32[]{:S(2)}) %collective-permute-start.13) | collective-permute-done | bytes 557088 | tf_op jit(solution)/shard_map/ppermute | solution.py:18
  62.2 3.3 %collective-permute-start.15 = (bf16[64,2176]{1,0:T(8,128)(2,1)S(1)}, bf16[64,2176]{1,0:T(8,128)(2,1)S(1)}, u32[]{:S(2)}, u32[]{:S(2)}) collective-permute-start(bf16[64,2176]{1,0:T(8,128)(2,1)S(1)} %slice.211), channel_id=1, source_target_pairs={{0,12},{1,13},{2,14},{3,15},{4,0},{5,1},{6,2},{7,3},{8,4},{9,5},{1... | collective-permute-start | bytes 835592 | tf_op jit(solution)/shard_map/ppermute | solution.py:18
  65.5 1.9 %constant_dynamic-update-slice_fusion.13 = bf16[1024,2176]{1,0:T(8,128)(2,1)} fusion(bf16[1024,2176]{1,0:T(8,128)(2,1)} %copy-done.1, bf16[128,2176]{1,0:T(8,128)(2,1)} %collective-permute-done.12), kind=kLoop, calls=%fused_computation.83 | loop fusion | bytes 1114112
  70.4 1.9 %constant_dynamic-update-slice_fusion.10 = bf16[1024,2176]{1,0:T(8,128)(2,1)} fusion(bf16[1024,2176]{1,0:T(8,128)(2,1)} %constant_dynamic-update-slice_fusion.11, bf16[128,2176]{1,0:T(8,128)(2,1)} %collective-permute-done.13), kind=kLoop, calls=%fused_computation.80 | loop fusion | bytes 1114112 | tf_op jit(solution)/shard_map/concatenate | solution.py:73
  73.7 10.0 %fusion = f32[1024,1536]{1,0:T(8,128)S(1)} fusion(bf16[1,2048,1536]{2,1,0:T(8,128)(2,1)} %param.8, bf16[1024,2176]{1,0:T(8,128)(2,1)} %constant_dynamic-update-slice_fusion.10), kind=kOutput, calls=%fused_computation.1 | convolution fusion | flops 6442450944 | bytes 16777216 | tf_op jit(solution)/shard_map/dot_general | solution.py:49
  83.7 3.5 %convert_multiply_fusion = f32[1024,2048]{1,0:T(8,128)S(1)} fusion(f32[1024]{0:T(1024)S(1)} %select_reduce_fusion, bf16[1,768,2048]{2,1,0:T(8,128)(2,1)S(1)} %copy-done, f32[1024,1536]{1,0:T(8,128)S(1)} %fusion), kind=kOutput, calls=%fused_computation | convolution fusion | flops 3232235520 | bytes 17829888 | tf_op jit(solution)/shard_map/dot_general | solution.py:51
  90.0 2.5 %collective-permute-start.26 = (bf16[64,2048]{1,0:T(8,128)(2,1)S(1)}, bf16[64,2048]{1,0:T(8,128)(2,1)S(1)}, u32[]{:S(2)}, u32[]{:S(2)}) collective-permute-start(bf16[64,2048]{1,0:T(8,128)(2,1)S(1)} %get-tuple-element.20), channel_id=1, source_target_pairs={{0,12},{1,13},{2,14},{3,15},{4,0},{5,1},{6,2},{7,3},{8,4},{9,5},{1... | collective-permute-start | bytes 786440 | tf_op jit(solution)/shard_map/ppermute | solution.py:18
  93.2 3.0 %collective-permute-start.18 = (bf16[64,2048]{1,0:T(8,128)(2,1)S(1)}, bf16[64,2048]{1,0:T(8,128)(2,1)S(1)}, u32[]{:S(2)}, u32[]{:S(2)}) collective-permute-start(bf16[64,2048]{1,0:T(8,128)(2,1)S(1)} %get-tuple-element.16), channel_id=1, source_target_pairs={{0,3},{1,0},{2,1},{3,2},{4,7},{5,4},{6,5},{7,6},{8,11},{9,8},{10,9... | collective-permute-start | bytes 786440 | tf_op jit(solution)/shard_map/ppermute | solution.py:18
  96.8 2.4 %collective-permute-done.26 = bf16[64,2048]{1,0:T(8,128)(2,1)S(1)} collective-permute-done((bf16[64,2048]{1,0:T(8,128)(2,1)S(1)}, bf16[64,2048]{1,0:T(8,128)(2,1)S(1)}, u32[]{:S(2)}, u32[]{:S(2)}) %collective-permute-start.26) | collective-permute-done | bytes 262176 | tf_op jit(solution)/shard_map/ppermute | solution.py:18
  99.4 3.8 %collective-permute-start.27 = (bf16[128,2048]{1,0:T(8,128)(2,1)S(1)}, bf16[128,2048]{1,0:T(8,128)(2,1)S(1)}, u32[]{:S(2)}, u32[]{:S(2)}) collective-permute-start(bf16[128,2048]{1,0:T(8,128)(2,1)S(1)} %pad_maximum_fusion.3), channel_id=1, source_target_pairs={{0,12},{1,13},{2,14},{3,15},{4,0},{5,1},{6,2},{7,3},{8,4},{9,5},{1... | collective-permute-start | bytes 1572872 | tf_op jit(solution)/shard_map/ppermute | solution.py:18
  103.7 3.2 %collective-permute-start.19 = (bf16[128,2048]{1,0:T(8,128)(2,1)S(1)}, bf16[128,2048]{1,0:T(8,128)(2,1)S(1)}, u32[]{:S(2)}, u32[]{:S(2)}) collective-permute-start(bf16[128,2048]{1,0:T(8,128)(2,1)S(1)} %pad_maximum_fusion.1), channel_id=1, source_target_pairs={{0,3},{1,0},{2,1},{3,2},{4,7},{5,4},{6,5},{7,6},{8,11},{9,8},{10,9... | collective-permute-start | bytes 1572872 | tf_op jit(solution)/shard_map/ppermute | solution.py:18
  107.0 2.9 %collective-permute-done.27 = bf16[128,2048]{1,0:T(8,128)(2,1)S(1)} collective-permute-done((bf16[128,2048]{1,0:T(8,128)(2,1)S(1)}, bf16[128,2048]{1,0:T(8,128)(2,1)S(1)}, u32[]{:S(2)}, u32[]{:S(2)}) %collective-permute-start.27) | collective-permute-done | bytes 524320 | tf_op jit(solution)/shard_map/ppermute | solution.py:18
  109.8 4.6 %collective-permute-done.25 = bf16[128,2048]{1,0:T(8,128)(2,1)S(1)} collective-permute-done((bf16[128,2048]{1,0:T(8,128)(2,1)S(1)}, bf16[128,2048]{1,0:T(8,128)(2,1)S(1)}, u32[]{:S(2)}, u32[]{:S(2)}) %collective-permute-start.25) | collective-permute-done | bytes 524320 | tf_op jit(solution)/shard_map/ppermute | solution.py:18
  114.4 2.9 %collective-permute-done.17 = bf16[128,2048]{1,0:T(8,128)(2,1)S(1)} collective-permute-done((bf16[128,2048]{1,0:T(8,128)(2,1)S(1)}, bf16[128,2048]{1,0:T(8,128)(2,1)S(1)}, u32[]{:S(2)}, u32[]{:S(2)}) %collective-permute-start.17) | collective-permute-done | bytes 524320 | tf_op jit(solution)/shard_map/ppermute | solution.py:18
  118.0 3.2 %collective-permute-start.30 = (bf16[16,2048]{1,0:T(8,128)(2,1)S(1)}, bf16[16,2048]{1,0:T(8,128)(2,1)S(1)}, u32[]{:S(2)}, u32[]{:S(2)}) collective-permute-start(bf16[16,2048]{1,0:T(8,128)(2,1)S(1)} %get-tuple-element.32), channel_id=1, source_target_pairs={{0,3},{1,0},{2,1},{3,2},{4,7},{5,4},{6,5},{7,6},{8,11},{9,8},{10,9... | collective-permute-start | bytes 196616 | tf_op jit(solution)/shard_map/ppermute | solution.py:18
  121.9 2.7 %collective-permute-start.22 = (bf16[16,2048]{1,0:T(8,128)(2,1)S(1)}, bf16[16,2048]{1,0:T(8,128)(2,1)S(1)}, u32[]{:S(2)}, u32[]{:S(2)}) collective-permute-start(bf16[16,2048]{1,0:T(8,128)(2,1)S(1)} %get-tuple-element.28), channel_id=1, source_target_pairs={{0,12},{1,13},{2,14},{3,15},{4,0},{5,1},{6,2},{7,3},{8,4},{9,5},{1... | collective-permute-start | bytes 196616 | tf_op jit(solution)/shard_map/ppermute | solution.py:18
  124.7 2.1 %collective-permute-start.31 = (bf16[32,2048]{1,0:T(8,128)(2,1)S(1)}, bf16[32,2048]{1,0:T(8,128)(2,1)S(1)}, u32[]{:S(2)}, u32[]{:S(2)}) collective-permute-start(bf16[32,2048]{1,0:T(8,128)(2,1)S(1)} %pad_maximum_fusion.8), channel_id=1, source_target_pairs={{0,3},{1,0},{2,1},{3,2},{4,7},{5,4},{6,5},{7,6},{8,11},{9,8},{10,9... | collective-permute-start | bytes 393224 | tf_op jit(solution)/shard_map/ppermute | solution.py:18
  127.0 3.2 %collective-permute-start.23 = (bf16[32,2048]{1,0:T(8,128)(2,1)S(1)}, bf16[32,2048]{1,0:T(8,128)(2,1)S(1)}, u32[]{:S(2)}, u32[]{:S(2)}) collective-permute-start(bf16[32,2048]{1,0:T(8,128)(2,1)S(1)} %pad_maximum_fusion.6), channel_id=1, source_target_pairs={{0,12},{1,13},{2,14},{3,15},{4,0},{5,1},{6,2},{7,3},{8,4},{9,5},{1... | collective-permute-start | bytes 393224 | tf_op jit(solution)/shard_map/ppermute | solution.py:18
  130.4 2.7 %collective-permute-done.29 = bf16[32,2048]{1,0:T(8,128)(2,1)S(1)} collective-permute-done((bf16[32,2048]{1,0:T(8,128)(2,1)S(1)}, bf16[32,2048]{1,0:T(8,128)(2,1)S(1)}, u32[]{:S(2)}, u32[]{:S(2)}) %collective-permute-start.29) | collective-permute-done | bytes 131104 | tf_op jit(solution)/shard_map/ppermute | solution.py:18
  133.2 3.3 %collective-permute-done.21 = bf16[32,2048]{1,0:T(8,128)(2,1)S(1)} collective-permute-done((bf16[32,2048]{1,0:T(8,128)(2,1)S(1)}, bf16[32,2048]{1,0:T(8,128)(2,1)S(1)}, u32[]{:S(2)}, u32[]{:S(2)}) %collective-permute-start.21) | collective-permute-done | bytes 131104 | tf_op jit(solution)/shard_map/ppermute | solution.py:18
  (97 shorter events, 24.8 us)
Async XLA Ops:
  2.9 6.6 %collective-permute-start.1 = (bf16[32,2176]{1,0:T(8,128)(2,1)S(1)}, bf16[32,2176]{1,0:T(8,128)(2,1)S(1)}, u32[]{:S(2)}, u32[]{:S(2)}) collective-permute-start(bf16[32,2176]{1,0:T(8,128)(2,1)S(1)} %get-tuple-element.39), channel_id=1, source_target_pairs={{0,4},{1,5},{2,6},{3,7},{4,8},{5,9},{6,10},{7,11},{8,12},{9,13},{1... | collective-permute-start | bytes 417800 | tf_op jit(solution)/shard_map/ppermute | solution.py:18
  4.4 5.4 %collective-permute-start = (bf16[32,2176]{1,0:T(8,128)(2,1)S(1)}, bf16[32,2176]{1,0:T(8,128)(2,1)S(1)}, u32[]{:S(2)}, u32[]{:S(2)}) collective-permute-start(bf16[32,2176]{1,0:T(8,128)(2,1)S(1)} %get-tuple-element.39), channel_id=1, source_target_pairs={{0,12},{1,13},{2,14},{3,15},{4,0},{5,1},{6,2},{7,3},{8,4},{9,5},{1... | collective-permute-start | bytes 417800 | tf_op jit(solution)/shard_map/ppermute | solution.py:18
  9.5 5.5 %collective-permute-start.2 = (bf16[16,2176]{1,0:T(8,128)(2,1)S(1)}, bf16[16,2176]{1,0:T(8,128)(2,1)S(1)}, u32[]{:S(2)}, u32[]{:S(2)}) collective-permute-start(bf16[16,2176]{1,0:T(8,128)(2,1)S(1)} %slice.203), channel_id=1, source_target_pairs={{0,4},{1,5},{2,6},{3,7},{4,8},{5,9},{6,10},{7,11},{8,12},{9,13},{1... | collective-permute-start | bytes 208904 | tf_op jit(solution)/shard_map/ppermute | solution.py:18
  9.8 5.2 %collective-permute-start.3 = (bf16[16,2176]{1,0:T(8,128)(2,1)S(1)}, bf16[16,2176]{1,0:T(8,128)(2,1)S(1)}, u32[]{:S(2)}, u32[]{:S(2)}) collective-permute-start(bf16[16,2176]{1,0:T(8,128)(2,1)S(1)} %slice.204), channel_id=1, source_target_pairs={{0,12},{1,13},{2,14},{3,15},{4,0},{5,1},{6,2},{7,3},{8,4},{9,5},{1... | collective-permute-start | bytes 208904 | tf_op jit(solution)/shard_map/ppermute | solution.py:18
  15.1 20.0 %collective-permute-start.5 = (bf16[128,2176]{1,0:T(8,128)(2,1)S(1)}, bf16[128,2176]{1,0:T(8,128)(2,1)S(1)}, u32[]{:S(2)}, u32[]{:S(2)}) collective-permute-start(bf16[128,2176]{1,0:T(8,128)(2,1)S(1)} %get-tuple-element.44), channel_id=1, source_target_pairs={{0,1},{1,2},{2,3},{3,0},{4,5},{5,6},{6,7},{7,4},{8,9},{9,10},{10,1... | collective-permute-start | bytes 1671176 | tf_op jit(solution)/shard_map/ppermute | solution.py:18
  16.8 18.5 %collective-permute-start.4 = (bf16[128,2176]{1,0:T(8,128)(2,1)S(1)}, bf16[128,2176]{1,0:T(8,128)(2,1)S(1)}, u32[]{:S(2)}, u32[]{:S(2)}) collective-permute-start(bf16[128,2176]{1,0:T(8,128)(2,1)S(1)} %get-tuple-element.44), channel_id=1, source_target_pairs={{0,3},{1,0},{2,1},{3,2},{4,7},{5,4},{6,5},{7,6},{8,11},{9,8},{10,9... | collective-permute-start | bytes 1671176 | tf_op jit(solution)/shard_map/ppermute | solution.py:18
  18.4 13.4 %collective-permute-start.9 = (bf16[32,2176]{1,0:T(8,128)(2,1)S(1)}, bf16[32,2176]{1,0:T(8,128)(2,1)S(1)}, u32[]{:S(2)}, u32[]{:S(2)}) collective-permute-start(bf16[32,2176]{1,0:T(8,128)(2,1)S(1)} %get-tuple-element.38), channel_id=1, source_target_pairs={{0,1},{1,2},{2,3},{3,0},{4,5},{5,6},{6,7},{7,4},{8,9},{9,10},{10,1... | collective-permute-start | bytes 417800 | tf_op jit(solution)/shard_map/ppermute | solution.py:18
  18.8 13.7 %collective-permute-start.8 = (bf16[32,2176]{1,0:T(8,128)(2,1)S(1)}, bf16[32,2176]{1,0:T(8,128)(2,1)S(1)}, u32[]{:S(2)}, u32[]{:S(2)}) collective-permute-start(bf16[32,2176]{1,0:T(8,128)(2,1)S(1)} %get-tuple-element.38), channel_id=1, source_target_pairs={{0,3},{1,0},{2,1},{3,2},{4,7},{5,4},{6,5},{7,6},{8,11},{9,8},{10,9... | collective-permute-start | bytes 417800 | tf_op jit(solution)/shard_map/ppermute | solution.py:18
  31.8 12.0 %collective-permute-start.10 = (bf16[16,2176]{1,0:T(8,128)(2,1)S(1)}, bf16[16,2176]{1,0:T(8,128)(2,1)S(1)}, u32[]{:S(2)}, u32[]{:S(2)}) collective-permute-start(bf16[16,2176]{1,0:T(8,128)(2,1)S(1)} %slice.208), channel_id=1, source_target_pairs={{0,1},{1,2},{2,3},{3,0},{4,5},{5,6},{6,7},{7,4},{8,9},{9,10},{10,1... | collective-permute-start | bytes 208904 | tf_op jit(solution)/shard_map/ppermute | solution.py:18
  32.5 12.0 %collective-permute-start.11 = (bf16[16,2176]{1,0:T(8,128)(2,1)S(1)}, bf16[16,2176]{1,0:T(8,128)(2,1)S(1)}, u32[]{:S(2)}, u32[]{:S(2)}) collective-permute-start(bf16[16,2176]{1,0:T(8,128)(2,1)S(1)} %slice.209), channel_id=1, source_target_pairs={{0,3},{1,0},{2,1},{3,2},{4,7},{5,4},{6,5},{7,6},{8,11},{9,8},{10,9... | collective-permute-start | bytes 208904 | tf_op jit(solution)/shard_map/ppermute | solution.py:18
  35.2 7.8 %collective-permute-start.6 = (bf16[64,2176]{1,0:T(8,128)(2,1)S(1)}, bf16[64,2176]{1,0:T(8,128)(2,1)S(1)}, u32[]{:S(2)}, u32[]{:S(2)}) collective-permute-start(bf16[64,2176]{1,0:T(8,128)(2,1)S(1)} %slice.205), channel_id=1, source_target_pairs={{0,1},{1,2},{2,3},{3,0},{4,5},{5,6},{6,7},{7,4},{8,9},{9,10},{10,1... | collective-permute-start | bytes 835592 | tf_op jit(solution)/shard_map/ppermute | solution.py:18
  35.3 7.7 %collective-permute-start.7 = (bf16[64,2176]{1,0:T(8,128)(2,1)S(1)}, bf16[64,2176]{1,0:T(8,128)(2,1)S(1)}, u32[]{:S(2)}, u32[]{:S(2)}) collective-permute-start(bf16[64,2176]{1,0:T(8,128)(2,1)S(1)} %slice.206), channel_id=1, source_target_pairs={{0,3},{1,0},{2,1},{3,2},{4,7},{5,4},{6,5},{7,6},{8,11},{9,8},{10,9... | collective-permute-start | bytes 835592 | tf_op jit(solution)/shard_map/ppermute | solution.py:18
  47.8 12.1 %collective-permute-start.13 = (bf16[128,2176]{1,0:T(8,128)(2,1)}, bf16[128,2176]{1,0:T(8,128)(2,1)}, u32[]{:S(2)}, u32[]{:S(2)}) collective-permute-start(bf16[128,2176]{1,0:T(8,128)(2,1)} %get-tuple-element.40), channel_id=1, source_target_pairs={{0,4},{1,5},{2,6},{3,7},{4,8},{5,9},{6,10},{7,11},{8,12},{9,13},{1... | collective-permute-start | bytes 1671176 | tf_op jit(solution)/shard_map/ppermute | solution.py:18
  48.5 12.8 %collective-permute-start.12 = (bf16[128,2176]{1,0:T(8,128)(2,1)}, bf16[128,2176]{1,0:T(8,128)(2,1)}, u32[]{:S(2)}, u32[]{:S(2)}) collective-permute-start(bf16[128,2176]{1,0:T(8,128)(2,1)} %get-tuple-element.40), channel_id=1, source_target_pairs={{0,12},{1,13},{2,14},{3,15},{4,0},{5,1},{6,2},{7,3},{8,4},{9,5},{1... | collective-permute-start | bytes 1671176 | tf_op jit(solution)/shard_map/ppermute | solution.py:18
  60.9 8.0 %collective-permute-start.14 = (bf16[64,2176]{1,0:T(8,128)(2,1)S(1)}, bf16[64,2176]{1,0:T(8,128)(2,1)S(1)}, u32[]{:S(2)}, u32[]{:S(2)}) collective-permute-start(bf16[64,2176]{1,0:T(8,128)(2,1)S(1)} %slice.210), channel_id=1, source_target_pairs={{0,4},{1,5},{2,6},{3,7},{4,8},{5,9},{6,10},{7,11},{8,12},{9,13},{1... | collective-permute-start | bytes 835592 | tf_op jit(solution)/shard_map/ppermute | solution.py:18
  62.2 7.5 %collective-permute-start.15 = (bf16[64,2176]{1,0:T(8,128)(2,1)S(1)}, bf16[64,2176]{1,0:T(8,128)(2,1)S(1)}, u32[]{:S(2)}, u32[]{:S(2)}) collective-permute-start(bf16[64,2176]{1,0:T(8,128)(2,1)S(1)} %slice.211), channel_id=1, source_target_pairs={{0,12},{1,13},{2,14},{3,15},{4,0},{5,1},{6,2},{7,3},{8,4},{9,5},{1... | collective-permute-start | bytes 835592 | tf_op jit(solution)/shard_map/ppermute | solution.py:18
  88.7 8.0 %collective-permute-start.24 = (bf16[64,2048]{1,0:T(8,128)(2,1)S(1)}, bf16[64,2048]{1,0:T(8,128)(2,1)S(1)}, u32[]{:S(2)}, u32[]{:S(2)}) collective-permute-start(bf16[64,2048]{1,0:T(8,128)(2,1)S(1)} %get-tuple-element.19), channel_id=1, source_target_pairs={{0,4},{1,5},{2,6},{3,7},{4,8},{5,9},{6,10},{7,11},{8,12},{9,13},{1... | collective-permute-start | bytes 786440 | tf_op jit(solution)/shard_map/ppermute | solution.py:18
  90.0 9.2 %collective-permute-start.26 = (bf16[64,2048]{1,0:T(8,128)(2,1)S(1)}, bf16[64,2048]{1,0:T(8,128)(2,1)S(1)}, u32[]{:S(2)}, u32[]{:S(2)}) collective-permute-start(bf16[64,2048]{1,0:T(8,128)(2,1)S(1)} %get-tuple-element.20), channel_id=1, source_target_pairs={{0,12},{1,13},{2,14},{3,15},{4,0},{5,1},{6,2},{7,3},{8,4},{9,5},{1... | collective-permute-start | bytes 786440 | tf_op jit(solution)/shard_map/ppermute | solution.py:18
  92.9 10.6 %collective-permute-start.16 = (bf16[64,2048]{1,0:T(8,128)(2,1)S(1)}, bf16[64,2048]{1,0:T(8,128)(2,1)S(1)}, u32[]{:S(2)}, u32[]{:S(2)}) collective-permute-start(bf16[64,2048]{1,0:T(8,128)(2,1)S(1)} %get-tuple-element.15), channel_id=1, source_target_pairs={{0,1},{1,2},{2,3},{3,0},{4,5},{5,6},{6,7},{7,4},{8,9},{9,10},{10,1... | collective-permute-start | bytes 786440 | tf_op jit(solution)/shard_map/ppermute | solution.py:18
  93.2 10.3 %collective-permute-start.18 = (bf16[64,2048]{1,0:T(8,128)(2,1)S(1)}, bf16[64,2048]{1,0:T(8,128)(2,1)S(1)}, u32[]{:S(2)}, u32[]{:S(2)}) collective-permute-start(bf16[64,2048]{1,0:T(8,128)(2,1)S(1)} %get-tuple-element.16), channel_id=1, source_target_pairs={{0,3},{1,0},{2,1},{3,2},{4,7},{5,4},{6,5},{7,6},{8,11},{9,8},{10,9... | collective-permute-start | bytes 786440 | tf_op jit(solution)/shard_map/ppermute | solution.py:18
  99.4 10.5 %collective-permute-start.27 = (bf16[128,2048]{1,0:T(8,128)(2,1)S(1)}, bf16[128,2048]{1,0:T(8,128)(2,1)S(1)}, u32[]{:S(2)}, u32[]{:S(2)}) collective-permute-start(bf16[128,2048]{1,0:T(8,128)(2,1)S(1)} %pad_maximum_fusion.3), channel_id=1, source_target_pairs={{0,12},{1,13},{2,14},{3,15},{4,0},{5,1},{6,2},{7,3},{8,4},{9,5},{1... | collective-permute-start | bytes 1572872 | tf_op jit(solution)/shard_map/ppermute | solution.py:18
  103.2 11.3 %collective-permute-start.25 = (bf16[128,2048]{1,0:T(8,128)(2,1)S(1)}, bf16[128,2048]{1,0:T(8,128)(2,1)S(1)}, u32[]{:S(2)}, u32[]{:S(2)}) collective-permute-start(bf16[128,2048]{1,0:T(8,128)(2,1)S(1)} %pad_maximum_fusion.2), channel_id=1, source_target_pairs={{0,4},{1,5},{2,6},{3,7},{4,8},{5,9},{6,10},{7,11},{8,12},{9,13},{1... | collective-permute-start | bytes 1572872 | tf_op jit(solution)/shard_map/ppermute | solution.py:18
  103.7 10.8 %collective-permute-start.19 = (bf16[128,2048]{1,0:T(8,128)(2,1)S(1)}, bf16[128,2048]{1,0:T(8,128)(2,1)S(1)}, u32[]{:S(2)}, u32[]{:S(2)}) collective-permute-start(bf16[128,2048]{1,0:T(8,128)(2,1)S(1)} %pad_maximum_fusion.1), channel_id=1, source_target_pairs={{0,3},{1,0},{2,1},{3,2},{4,7},{5,4},{6,5},{7,6},{8,11},{9,8},{10,9... | collective-permute-start | bytes 1572872 | tf_op jit(solution)/shard_map/ppermute | solution.py:18
  106.9 10.5 %collective-permute-start.17 = (bf16[128,2048]{1,0:T(8,128)(2,1)S(1)}, bf16[128,2048]{1,0:T(8,128)(2,1)S(1)}, u32[]{:S(2)}, u32[]{:S(2)}) collective-permute-start(bf16[128,2048]{1,0:T(8,128)(2,1)S(1)} %pad_maximum_fusion), channel_id=1, source_target_pairs={{0,1},{1,2},{2,3},{3,0},{4,5},{5,6},{6,7},{7,4},{8,9},{9,10},{10,1... | collective-permute-start | bytes 1572872 | tf_op jit(solution)/shard_map/ppermute | solution.py:18
  117.9 6.7 %collective-permute-start.28 = (bf16[16,2048]{1,0:T(8,128)(2,1)S(1)}, bf16[16,2048]{1,0:T(8,128)(2,1)S(1)}, u32[]{:S(2)}, u32[]{:S(2)}) collective-permute-start(bf16[16,2048]{1,0:T(8,128)(2,1)S(1)} %get-tuple-element.31), channel_id=1, source_target_pairs={{0,1},{1,2},{2,3},{3,0},{4,5},{5,6},{6,7},{7,4},{8,9},{9,10},{10,1... | collective-permute-start | bytes 196616 | tf_op jit(solution)/shard_map/ppermute | solution.py:18
  118.0 6.6 %collective-permute-start.30 = (bf16[16,2048]{1,0:T(8,128)(2,1)S(1)}, bf16[16,2048]{1,0:T(8,128)(2,1)S(1)}, u32[]{:S(2)}, u32[]{:S(2)}) collective-permute-start(bf16[16,2048]{1,0:T(8,128)(2,1)S(1)} %get-tuple-element.32), channel_id=1, source_target_pairs={{0,3},{1,0},{2,1},{3,2},{4,7},{5,4},{6,5},{7,6},{8,11},{9,8},{10,9... | collective-permute-start | bytes 196616 | tf_op jit(solution)/shard_map/ppermute | solution.py:18
  121.3 5.6 %collective-permute-start.20 = (bf16[16,2048]{1,0:T(8,128)(2,1)S(1)}, bf16[16,2048]{1,0:T(8,128)(2,1)S(1)}, u32[]{:S(2)}, u32[]{:S(2)}) collective-permute-start(bf16[16,2048]{1,0:T(8,128)(2,1)S(1)} %get-tuple-element.27), channel_id=1, source_target_pairs={{0,4},{1,5},{2,6},{3,7},{4,8},{5,9},{6,10},{7,11},{8,12},{9,13},{1... | collective-permute-start | bytes 196616 | tf_op jit(solution)/shard_map/ppermute | solution.py:18
  121.9 5.0 %collective-permute-start.22 = (bf16[16,2048]{1,0:T(8,128)(2,1)S(1)}, bf16[16,2048]{1,0:T(8,128)(2,1)S(1)}, u32[]{:S(2)}, u32[]{:S(2)}) collective-permute-start(bf16[16,2048]{1,0:T(8,128)(2,1)S(1)} %get-tuple-element.28), channel_id=1, source_target_pairs={{0,12},{1,13},{2,14},{3,15},{4,0},{5,1},{6,2},{7,3},{8,4},{9,5},{1... | collective-permute-start | bytes 196616 | tf_op jit(solution)/shard_map/ppermute | solution.py:18
  124.7 5.7 %collective-permute-start.31 = (bf16[32,2048]{1,0:T(8,128)(2,1)S(1)}, bf16[32,2048]{1,0:T(8,128)(2,1)S(1)}, u32[]{:S(2)}, u32[]{:S(2)}) collective-permute-start(bf16[32,2048]{1,0:T(8,128)(2,1)S(1)} %pad_maximum_fusion.8), channel_id=1, source_target_pairs={{0,3},{1,0},{2,1},{3,2},{4,7},{5,4},{6,5},{7,6},{8,11},{9,8},{10,9... | collective-permute-start | bytes 393224 | tf_op jit(solution)/shard_map/ppermute | solution.py:18
  126.9 6.3 %collective-permute-start.29 = (bf16[32,2048]{1,0:T(8,128)(2,1)S(1)}, bf16[32,2048]{1,0:T(8,128)(2,1)S(1)}, u32[]{:S(2)}, u32[]{:S(2)}) collective-permute-start(bf16[32,2048]{1,0:T(8,128)(2,1)S(1)} %pad_maximum_fusion.7), channel_id=1, source_target_pairs={{0,1},{1,2},{2,3},{3,0},{4,5},{5,6},{6,7},{7,4},{8,9},{9,10},{10,1... | collective-permute-start | bytes 393224 | tf_op jit(solution)/shard_map/ppermute | solution.py:18
  127.0 6.1 %collective-permute-start.23 = (bf16[32,2048]{1,0:T(8,128)(2,1)S(1)}, bf16[32,2048]{1,0:T(8,128)(2,1)S(1)}, u32[]{:S(2)}, u32[]{:S(2)}) collective-permute-start(bf16[32,2048]{1,0:T(8,128)(2,1)S(1)} %pad_maximum_fusion.6), channel_id=1, source_target_pairs={{0,12},{1,13},{2,14},{3,15},{4,0},{5,1},{6,2},{7,3},{8,4},{9,5},{1... | collective-permute-start | bytes 393224 | tf_op jit(solution)/shard_map/ppermute | solution.py:18
  130.3 6.3 %collective-permute-start.21 = (bf16[32,2048]{1,0:T(8,128)(2,1)S(1)}, bf16[32,2048]{1,0:T(8,128)(2,1)S(1)}, u32[]{:S(2)}, u32[]{:S(2)}) collective-permute-start(bf16[32,2048]{1,0:T(8,128)(2,1)S(1)} %pad_maximum_fusion.5), channel_id=1, source_target_pairs={{0,4},{1,5},{2,6},{3,7},{4,8},{5,9},{6,10},{7,11},{8,12},{9,13},{1... | collective-permute-start | bytes 393224 | tf_op jit(solution)/shard_map/ppermute | solution.py:18
  (2 other events, 85.8 us)
where the time goes:
time: 139 us; the launch traced here: 137 us
  starting transfers between devices  53.1 us (38%)
  waiting for transfers between devices  50 us (36%)
  local copies, waits for them, and re-layouts  15.5 us (11%)
  matrix products  13.5 us (10%)
  other arithmetic  4.75 us (3%)
    ppermute x32, starting transfers between devices, shift(): return lax.ppermute(tree, 'expert', pairs)  53.1 us
    ppermute x32, waiting for transfers between devices, shift(): return lax.ppermute(tree, 'expert', pairs)  50 us
    dot_general x1, matrix products, expert_rows(): jnp.dot(rows[:, :width], w_in, preferred_element_type=jnp.float32)  10 us
    unnamed x19, local copies, waits for them, and re-layouts  8.33 us
    dot_general x1, matrix products, expert_rows(): jnp.dot(inner, w_out, preferred_element_type=jnp.float32)  3.5 us
  transfers between devices with their start and end apart: 32, of which 13 were waited for; matrix products, arithmetic and copies ran while one was open for 5% of the time, Pallas kernels for 0%

commit v1 on v0

--- a/solution.py
+++ b/solution.py
@@ -7,15 +7,19 @@
 PAD = 128
 
 
-def shift(tree, axis, step):
+def shift(tree, stage, step):
+    parts = lax.axis_size("dp")
     pairs = []
-    for x in range(SIDE):
-        for y in range(SIDE):
-            if axis == "x":
-                pairs.append((x * SIDE + y, ((x + step) % SIDE) * SIDE + y))
-            else:
-                pairs.append((x * SIDE + y, x * SIDE + (y + step) % SIDE))
-    return lax.ppermute(tree, "expert", pairs)
+    for d in range(parts):
+        along_x = (d + stage) % 2 == 0
+        for x in range(SIDE):
+            for y in range(SIDE):
+                if along_x:
+                    target = ((x + step) % SIDE) * SIDE + y
+                else:
+                    target = x * SIDE + (y + step) % SIDE
+                pairs.append((d * SIDE * SIDE + x * SIDE + y, d * SIDE * SIDE + target))
+    return lax.ppermute(tree, ("dp", "expert"), pairs)
 
 
 def gather_ring(tree, axis):
@@ -64,20 +68,11 @@
     low = (table - high.astype(jnp.float32)).astype(jnp.bfloat16)
     extra = jnp.zeros((count, PAD - 2 * SIDE * SIDE), jnp.bfloat16)
     payload = jnp.concatenate([hidden_in, high, low, extra], axis=1)
-    split = count // 2
-    orders = (("x", "y"), ("y", "x"))
-    gathered = []
-    for i, (first, second) in enumerate(orders):
-        own = payload[i * split:(i + 1) * split]
-        gathered.append(gather_ring(gather_ring(own, first), second))
-    rows = jnp.concatenate(gathered, axis=0)
+    rows = gather_ring(gather_ring(payload, 0), 1)
     weighted = expert_rows(rows, me, width, w_in[0], w_out[0])
-    outs = []
-    for i, (first, second) in enumerate(orders):
-        part = weighted[i * 16 * split:(i + 1) * 16 * split].reshape(SIDE, SIDE * split, width)
-        stage = scatter_ring(part, second).reshape(SIDE, split, width)
-        outs.append(scatter_ring(stage, first))
-    return jnp.concatenate(outs, axis=0).astype(jnp.bfloat16)
+    part = weighted.reshape(SIDE, SIDE * count, width)
+    stage = scatter_ring(part, 1).reshape(SIDE, count, width)
+    return scatter_ring(stage, 0).astype(jnp.bfloat16)
 
 
 def solution(mesh):

time: 139 us -> 117 us (0.84); the launches traced: 137 us -> 117 us
  starting transfers between devices: 53.1 us -> 26.8 us
  waiting for transfers between devices: 50 us -> 58.4 us
  matrix products: 13.5 us -> 11.9 us
    ppermute x32 -> x16, starting transfers between devices: 53.1 us -> 26.8 us  [shift(): return lax.ppermute(tree, ('dp', 'expert'), pairs)]
    ppermute x32 -> x16, waiting for transfers between devices: 50 us -> 58.4 us  [shift(): return lax.ppermute(tree, ('dp', 'expert'), pairs)]
    concatenate x1 -> x0, local copies, waits for them, and re-layouts: 1.91 us -> none  [body(): rows = jnp.concatenate(gathered, axis=0)]
    dot_general x1, matrix products: 10 us -> 8.43 us  [expert_rows(): jnp.dot(rows[:, :width], w_in, preferred_element_type=jnp.float32)]
    unnamed x19 -> x15, local copies, waits for them, and re-layouts: 8.33 us -> 9.3 us
  transfers between devices with their start and end apart: 32 -> 16, of which waited for: 13 -> 10; matrix products, arithmetic and copies ran while one was open for 5% -> 8% of each run, Pallas kernels for 0% -> 0%
where the time goes in v1:
time: 117 us
  waiting for transfers between devices  58.4 us (50%)
  starting transfers between devices  26.8 us (23%)
  local copies, waits for them, and re-layouts  15 us (13%)
  matrix products  11.9 us (10%)
  other arithmetic  4.82 us (4%)
    ppermute x16, waiting for transfers between devices, shift(): return lax.ppermute(tree, ('dp', 'expert'), pairs)  58.4 us
    ppermute x16, starting transfers between devices, shift(): return lax.ppermute(tree, ('dp', 'expert'), pairs)  26.8 us
    unnamed x15, local copies, waits for them, and re-layouts  9.3 us
    dot_general x1, matrix products, expert_rows(): jnp.dot(rows[:, :width], w_in, preferred_element_type=jnp.float32)  8.43 us
    dot_general x1, matrix products, expert_rows(): jnp.dot(inner, w_out, preferred_element_type=jnp.float32)  3.51 us
  transfers between devices with their start and end apart: 16, of which 10 were waited for; matrix products, arithmetic and copies ran while one was open for 8% of the time, Pallas kernels for 0%

profile of v1, /device:TPU:64, one launch (start us, length us, event | category | flops | bytes accessed | tf_op | source)
XLA Modules:
  0.0 117.2 jit_solution(10535812197908419794)
XLA Ops:
  1.1 1.0 concatenate.26
  2.1 1.6 %collective-permute-start.1 = (bf16[64,2176]{1,0:T(8,128)(2,1)S(1)}, bf16[64,2176]{1,0:T(8,128)(2,1)S(1)}, u32[]{:S(2)}, u32[]{:S(2)}) collective-permute-start(bf16[64,2176]{1,0:T(8,128)(2,1)S(1)} %concatenate.26), channel_id=1, source_target_pairs={{0,4},{1,5},{2,6},{3,7},{4,8},{5,9},{6,10},{7,11},{8,12},{9,13},{1... | collective-permute-start | bytes 835592 | tf_op jit(solution)/shard_map/ppermute | solution.py:22
  3.7 1.7 %collective-permute-start = (bf16[64,2176]{1,0:T(8,128)(2,1)S(1)}, bf16[64,2176]{1,0:T(8,128)(2,1)S(1)}, u32[]{:S(2)}, u32[]{:S(2)}) collective-permute-start(bf16[64,2176]{1,0:T(8,128)(2,1)S(1)} %concatenate.26), channel_id=1, source_target_pairs={{0,12},{1,13},{2,14},{3,15},{4,0},{5,1},{6,2},{7,3},{8,4},{9,5},{1... | collective-permute-start | bytes 835592 | tf_op jit(solution)/shard_map/ppermute | solution.py:22
  5.5 0.9 constant_dynamic-update-slice_fusion.4
  6.4 3.6 %collective-permute-done.1 = bf16[64,2176]{1,0:T(8,128)(2,1)S(1)} collective-permute-done((bf16[64,2176]{1,0:T(8,128)(2,1)S(1)}, bf16[64,2176]{1,0:T(8,128)(2,1)S(1)}, u32[]{:S(2)}, u32[]{:S(2)}) %collective-permute-start.1) | collective-permute-done | bytes 278560 | tf_op jit(solution)/shard_map/ppermute | solution.py:22
  10.4 3.0 %collective-permute-start.3 = (bf16[32,2176]{1,0:T(8,128)(2,1)S(1)}, bf16[32,2176]{1,0:T(8,128)(2,1)S(1)}, u32[]{:S(2)}, u32[]{:S(2)}) collective-permute-start(bf16[32,2176]{1,0:T(8,128)(2,1)S(1)} %slice.103), channel_id=1, source_target_pairs={{0,12},{1,13},{2,14},{3,15},{4,0},{5,1},{6,2},{7,3},{8,4},{9,5},{1... | collective-permute-start | bytes 417800 | tf_op jit(solution)/shard_map/ppermute | solution.py:22
  14.3 2.1 %collective-permute-done.2 = bf16[32,2176]{1,0:T(8,128)(2,1)S(1)} collective-permute-done((bf16[32,2176]{1,0:T(8,128)(2,1)S(1)}, bf16[32,2176]{1,0:T(8,128)(2,1)S(1)}, u32[]{:S(2)}, u32[]{:S(2)}) %collective-permute-start.2) | collective-permute-done | bytes 139296 | tf_op jit(solution)/shard_map/ppermute | solution.py:22
  17.8 0.9 constant_dynamic-update-slice_fusion
  18.7 1.6 %collective-permute-start.5 = (bf16[256,2176]{1,0:T(8,128)(2,1)}, bf16[256,2176]{1,0:T(8,128)(2,1)S(1)}, u32[]{:S(2)}, u32[]{:S(2)}) collective-permute-start(bf16[256,2176]{1,0:T(8,128)(2,1)} %get-tuple-element.19), channel_id=1, source_target_pairs={{0,1},{1,2},{2,3},{3,0},{4,5},{5,6},{6,7},{7,4},{8,9},{9,10},{10,1... | collective-permute-start | bytes 3342344 | tf_op jit(solution)/shard_map/ppermute | solution.py:22
  20.2 1.7 %collective-permute-start.4 = (bf16[256,2176]{1,0:T(8,128)(2,1)}, bf16[256,2176]{1,0:T(8,128)(2,1)}, u32[]{:S(2)}, u32[]{:S(2)}) collective-permute-start(bf16[256,2176]{1,0:T(8,128)(2,1)} %get-tuple-element.19), channel_id=1, source_target_pairs={{0,3},{1,0},{2,1},{3,2},{4,7},{5,4},{6,5},{7,6},{8,11},{9,8},{10,9... | collective-permute-start | bytes 3342344 | tf_op jit(solution)/shard_map/ppermute | solution.py:22
  21.9 13.7 %collective-permute-done.5 = bf16[256,2176]{1,0:T(8,128)(2,1)S(1)} collective-permute-done((bf16[256,2176]{1,0:T(8,128)(2,1)}, bf16[256,2176]{1,0:T(8,128)(2,1)S(1)}, u32[]{:S(2)}, u32[]{:S(2)}) %collective-permute-start.5) | collective-permute-done | bytes 1114144 | tf_op jit(solution)/shard_map/ppermute | solution.py:22
  35.6 1.0 copy-done.1
  36.6 0.9 slice.104
  37.9 1.2 %slice.105 = bf16[128,2176]{1,0:T(8,128)(2,1)S(1)} slice(bf16[256,2176]{1,0:T(8,128)(2,1)} %collective-permute-done.4), slice={[128:256], [0:2176]} | slice | bytes 1114112 | tf_op jit(solution)/shard_map/slice | solution.py:30
  39.2 3.1 %collective-permute-start.7 = (bf16[128,2176]{1,0:T(8,128)(2,1)S(1)}, bf16[128,2176]{1,0:T(8,128)(2,1)S(1)}, u32[]{:S(2)}, u32[]{:S(2)}) collective-permute-start(bf16[128,2176]{1,0:T(8,128)(2,1)S(1)} %slice.105), channel_id=1, source_target_pairs={{0,3},{1,0},{2,1},{3,2},{4,7},{5,4},{6,5},{7,6},{8,11},{9,8},{10,9... | collective-permute-start | bytes 1671176 | tf_op jit(solution)/shard_map/ppermute | solution.py:22
  42.3 2.3 %constant_dynamic-update-slice_fusion.8 = bf16[1024,2176]{1,0:T(8,128)(2,1)} fusion(bf16[1024,2176]{1,0:T(8,128)(2,1)} %get-tuple-element.20, bf16[256,2176]{1,0:T(8,128)(2,1)} %collective-permute-done.4), kind=kLoop, calls=%fused_computation.48 | loop fusion | bytes 2228224
  44.6 4.0 %collective-permute-done.6 = bf16[128,2176]{1,0:T(8,128)(2,1)} collective-permute-done((bf16[128,2176]{1,0:T(8,128)(2,1)}, bf16[128,2176]{1,0:T(8,128)(2,1)}, u32[]{:S(2)}, u32[]{:S(2)}) %collective-permute-start.6) | collective-permute-done | bytes 557088 | tf_op jit(solution)/shard_map/ppermute | solution.py:22
  48.6 1.9 %constant_dynamic-update-slice_fusion.7 = bf16[1024,2176]{1,0:T(8,128)(2,1)} fusion(bf16[1024,2176]{1,0:T(8,128)(2,1)} %constant_dynamic-update-slice_fusion.8, bf16[128,2176]{1,0:T(8,128)(2,1)} %collective-permute-done.6), kind=kLoop, calls=%fused_computation.47 | loop fusion | bytes 1114112
  51.3 1.1 constant_dynamic-update-slice_fusion.5
  52.4 1.3 %select_reduce_fusion = f32[1024]{0:T(1024)S(1)} fusion(bf16[1024,2176]{1,0:T(8,128)(2,1)} %constant_dynamic-update-slice_fusion.5, pred[16]{0:T(512)(128)(4,1)S(1)} %iota_compare_fusion.1), kind=kLoop, calls=%fused_computation.25 | loop fusion | flops 80896 | bytes 69648 | tf_op jit(solution)/shard_map/reduce_sum | solution.py:52
  53.8 8.4 %fusion = f32[1024,1536]{1,0:T(8,128)S(1)} fusion(bf16[1,2048,1536]{2,1,0:T(8,128)(2,1)S(1)} %copy-done.3, bf16[1024,2176]{1,0:T(8,128)(2,1)} %constant_dynamic-update-slice_fusion.5), kind=kOutput, calls=%fused_computation.1 | convolution fusion | flops 6442450944 | bytes 16777216 | tf_op jit(solution)/shard_map/dot_general | solution.py:53
  62.2 3.5 %convert_multiply_fusion = f32[1024,2048]{1,0:T(8,128)S(1)} fusion(f32[1024]{0:T(1024)S(1)} %select_reduce_fusion, bf16[1,768,2048]{2,1,0:T(8,128)(2,1)S(1)} %copy-done, f32[1024,1536]{1,0:T(8,128)S(1)} %fusion), kind=kOutput, calls=%fused_computation | convolution fusion | flops 3232235520 | bytes 17829888 | tf_op jit(solution)/shard_map/dot_general | solution.py:55
  66.8 3.2 %collective-permute-start.10 = (bf16[128,2048]{1,0:T(8,128)(2,1)S(1)}, bf16[128,2048]{1,0:T(8,128)(2,1)S(1)}, u32[]{:S(2)}, u32[]{:S(2)}) collective-permute-start(bf16[128,2048]{1,0:T(8,128)(2,1)S(1)} %get-tuple-element.10), channel_id=1, source_target_pairs={{0,3},{1,0},{2,1},{3,2},{4,7},{5,4},{6,5},{7,6},{8,11},{9,8},{10,9... | collective-permute-start | bytes 1572872 | tf_op jit(solution)/shard_map/ppermute | solution.py:22
  70.0 7.2 %collective-permute-done.8 = bf16[128,2048]{1,0:T(8,128)(2,1)S(1)} collective-permute-done((bf16[128,2048]{1,0:T(8,128)(2,1)S(1)}, bf16[128,2048]{1,0:T(8,128)(2,1)S(1)}, u32[]{:S(2)}, u32[]{:S(2)}) %collective-permute-start.8) | collective-permute-done | bytes 524320 | tf_op jit(solution)/shard_map/ppermute | solution.py:22
  77.5 3.3 %collective-permute-start.11 = (bf16[256,2048]{1,0:T(8,128)(2,1)S(1)}, bf16[256,2048]{1,0:T(8,128)(2,1)S(1)}, u32[]{:S(2)}, u32[]{:S(2)}) collective-permute-start(bf16[256,2048]{1,0:T(8,128)(2,1)S(1)} %pad_maximum_fusion.1), channel_id=1, source_target_pairs={{0,3},{1,0},{2,1},{3,2},{4,7},{5,4},{6,5},{7,6},{8,11},{9,8},{10,9... | collective-permute-start | bytes 3145736 | tf_op jit(solution)/shard_map/ppermute | solution.py:22
  81.0 12.1 %collective-permute-done.11 = bf16[256,2048]{1,0:T(8,128)(2,1)S(1)} collective-permute-done((bf16[256,2048]{1,0:T(8,128)(2,1)S(1)}, bf16[256,2048]{1,0:T(8,128)(2,1)S(1)}, u32[]{:S(2)}, u32[]{:S(2)}) %collective-permute-start.11) | collective-permute-done | bytes 1048608 | tf_op jit(solution)/shard_map/ppermute | solution.py:22
  93.1 5.3 %collective-permute-done.9 = bf16[256,2048]{1,0:T(8,128)(2,1)S(1)} collective-permute-done((bf16[256,2048]{1,0:T(8,128)(2,1)S(1)}, bf16[256,2048]{1,0:T(8,128)(2,1)S(1)}, u32[]{:S(2)}, u32[]{:S(2)}) %collective-permute-start.9) | collective-permute-done | bytes 1048608 | tf_op jit(solution)/shard_map/ppermute | solution.py:22
  99.2 3.2 %collective-permute-start.14 = (bf16[32,2048]{1,0:T(8,128)(2,1)S(1)}, bf16[32,2048]{1,0:T(8,128)(2,1)S(1)}, u32[]{:S(2)}, u32[]{:S(2)}) collective-permute-start(bf16[32,2048]{1,0:T(8,128)(2,1)S(1)} %get-tuple-element.16), channel_id=1, source_target_pairs={{0,12},{1,13},{2,14},{3,15},{4,0},{5,1},{6,2},{7,3},{8,4},{9,5},{1... | collective-permute-start | bytes 393224 | tf_op jit(solution)/shard_map/ppermute | solution.py:22
  102.4 2.9 %collective-permute-done.12 = bf16[32,2048]{1,0:T(8,128)(2,1)S(1)} collective-permute-done((bf16[32,2048]{1,0:T(8,128)(2,1)S(1)}, bf16[32,2048]{1,0:T(8,128)(2,1)S(1)}, u32[]{:S(2)}, u32[]{:S(2)}) %collective-permute-start.12) | collective-permute-done | bytes 131104 | tf_op jit(solution)/shard_map/ppermute | solution.py:22
  105.4 3.3 %collective-permute-start.15 = (bf16[64,2048]{1,0:T(8,128)(2,1)S(1)}, bf16[64,2048]{1,0:T(8,128)(2,1)S(1)}, u32[]{:S(2)}, u32[]{:S(2)}) collective-permute-start(bf16[64,2048]{1,0:T(8,128)(2,1)S(1)} %pad_maximum_fusion.3), channel_id=1, source_target_pairs={{0,12},{1,13},{2,14},{3,15},{4,0},{5,1},{6,2},{7,3},{8,4},{9,5},{1... | collective-permute-start | bytes 786440 | tf_op jit(solution)/shard_map/ppermute | solution.py:22
  108.9 3.8 %collective-permute-done.15 = bf16[64,2048]{1,0:T(8,128)(2,1)S(1)} collective-permute-done((bf16[64,2048]{1,0:T(8,128)(2,1)S(1)}, bf16[64,2048]{1,0:T(8,128)(2,1)S(1)}, u32[]{:S(2)}, u32[]{:S(2)}) %collective-permute-start.15) | collective-permute-done | bytes 262176 | tf_op jit(solution)/shard_map/ppermute | solution.py:22
  112.6 3.8 %collective-permute-done.13 = bf16[64,2048]{1,0:T(8,128)(2,1)S(1)} collective-permute-done((bf16[64,2048]{1,0:T(8,128)(2,1)S(1)}, bf16[64,2048]{1,0:T(8,128)(2,1)S(1)}, u32[]{:S(2)}, u32[]{:S(2)}) %collective-permute-start.13) | collective-permute-done | bytes 262176 | tf_op jit(solution)/shard_map/ppermute | solution.py:22
  (43 shorter events, 8.2 us)
Async XLA Ops:
  0.0 62.2 %copy-start = (bf16[1,768,2048]{2,1,0:T(8,128)(2,1)S(1)}, bf16[1,768,2048]{2,1,0:T(8,128)(2,1)}, u32[]{:S(2)}) copy-start(bf16[1,768,2048]{2,1,0:T(8,128)(2,1)} %param.9) | copy-start | bytes 9437188
  2.1 7.8 %collective-permute-start.1 = (bf16[64,2176]{1,0:T(8,128)(2,1)S(1)}, bf16[64,2176]{1,0:T(8,128)(2,1)S(1)}, u32[]{:S(2)}, u32[]{:S(2)}) collective-permute-start(bf16[64,2176]{1,0:T(8,128)(2,1)S(1)} %concatenate.26), channel_id=1, source_target_pairs={{0,4},{1,5},{2,6},{3,7},{4,8},{5,9},{6,10},{7,11},{8,12},{9,13},{1... | collective-permute-start | bytes 835592 | tf_op jit(solution)/shard_map/ppermute | solution.py:22
  3.7 6.6 %collective-permute-start = (bf16[64,2176]{1,0:T(8,128)(2,1)S(1)}, bf16[64,2176]{1,0:T(8,128)(2,1)S(1)}, u32[]{:S(2)}, u32[]{:S(2)}) collective-permute-start(bf16[64,2176]{1,0:T(8,128)(2,1)S(1)} %concatenate.26), channel_id=1, source_target_pairs={{0,12},{1,13},{2,14},{3,15},{4,0},{5,1},{6,2},{7,3},{8,4},{9,5},{1... | collective-permute-start | bytes 835592 | tf_op jit(solution)/shard_map/ppermute | solution.py:22
  10.0 6.3 %collective-permute-start.2 = (bf16[32,2176]{1,0:T(8,128)(2,1)S(1)}, bf16[32,2176]{1,0:T(8,128)(2,1)S(1)}, u32[]{:S(2)}, u32[]{:S(2)}) collective-permute-start(bf16[32,2176]{1,0:T(8,128)(2,1)S(1)} %slice.102), channel_id=1, source_target_pairs={{0,4},{1,5},{2,6},{3,7},{4,8},{5,9},{6,10},{7,11},{8,12},{9,13},{1... | collective-permute-start | bytes 417800 | tf_op jit(solution)/shard_map/ppermute | solution.py:22
  10.4 6.7 %collective-permute-start.3 = (bf16[32,2176]{1,0:T(8,128)(2,1)S(1)}, bf16[32,2176]{1,0:T(8,128)(2,1)S(1)}, u32[]{:S(2)}, u32[]{:S(2)}) collective-permute-start(bf16[32,2176]{1,0:T(8,128)(2,1)S(1)} %slice.103), channel_id=1, source_target_pairs={{0,12},{1,13},{2,14},{3,15},{4,0},{5,1},{6,2},{7,3},{8,4},{9,5},{1... | collective-permute-start | bytes 417800 | tf_op jit(solution)/shard_map/ppermute | solution.py:22
  18.7 16.9 %collective-permute-start.5 = (bf16[256,2176]{1,0:T(8,128)(2,1)}, bf16[256,2176]{1,0:T(8,128)(2,1)S(1)}, u32[]{:S(2)}, u32[]{:S(2)}) collective-permute-start(bf16[256,2176]{1,0:T(8,128)(2,1)} %get-tuple-element.19), channel_id=1, source_target_pairs={{0,1},{1,2},{2,3},{3,0},{4,5},{5,6},{6,7},{7,4},{8,9},{9,10},{10,1... | collective-permute-start | bytes 3342344 | tf_op jit(solution)/shard_map/ppermute | solution.py:22
  20.2 17.7 %collective-permute-start.4 = (bf16[256,2176]{1,0:T(8,128)(2,1)}, bf16[256,2176]{1,0:T(8,128)(2,1)}, u32[]{:S(2)}, u32[]{:S(2)}) collective-permute-start(bf16[256,2176]{1,0:T(8,128)(2,1)} %get-tuple-element.19), channel_id=1, source_target_pairs={{0,3},{1,0},{2,1},{3,2},{4,7},{5,4},{6,5},{7,6},{8,11},{9,8},{10,9... | collective-permute-start | bytes 3342344 | tf_op jit(solution)/shard_map/ppermute | solution.py:22
  35.6 1.0 copy-start.1
  37.5 11.1 %collective-permute-start.6 = (bf16[128,2176]{1,0:T(8,128)(2,1)}, bf16[128,2176]{1,0:T(8,128)(2,1)}, u32[]{:S(2)}, u32[]{:S(2)}) collective-permute-start(bf16[128,2176]{1,0:T(8,128)(2,1)} %slice.104), channel_id=1, source_target_pairs={{0,1},{1,2},{2,3},{3,0},{4,5},{5,6},{6,7},{7,4},{8,9},{9,10},{10,1... | collective-permute-start | bytes 1671176 | tf_op jit(solution)/shard_map/ppermute | solution.py:22
  37.9 13.4 %copy-start.2 = (bf16[256,2176]{1,0:T(8,128)(2,1)S(1)}, bf16[256,2176]{1,0:T(8,128)(2,1)}, u32[]{:S(2)}) copy-start(bf16[256,2176]{1,0:T(8,128)(2,1)} %copy-done.1) | copy-start | bytes 3342340
  37.9 15.9 %copy-start.3 = (bf16[1,2048,1536]{2,1,0:T(8,128)(2,1)S(1)}, bf16[1,2048,1536]{2,1,0:T(8,128)(2,1)}, u32[]{:S(2)}) copy-start(bf16[1,2048,1536]{2,1,0:T(8,128)(2,1)} %param.8) | copy-start | bytes 18874372
  39.2 11.3 %collective-permute-start.7 = (bf16[128,2176]{1,0:T(8,128)(2,1)S(1)}, bf16[128,2176]{1,0:T(8,128)(2,1)S(1)}, u32[]{:S(2)}, u32[]{:S(2)}) collective-permute-start(bf16[128,2176]{1,0:T(8,128)(2,1)S(1)} %slice.105), channel_id=1, source_target_pairs={{0,3},{1,0},{2,1},{3,2},{4,7},{5,4},{6,5},{7,6},{8,11},{9,8},{10,9... | collective-permute-start | bytes 1671176 | tf_op jit(solution)/shard_map/ppermute | solution.py:22
  66.7 10.5 %collective-permute-start.8 = (bf16[128,2048]{1,0:T(8,128)(2,1)S(1)}, bf16[128,2048]{1,0:T(8,128)(2,1)S(1)}, u32[]{:S(2)}, u32[]{:S(2)}) collective-permute-start(bf16[128,2048]{1,0:T(8,128)(2,1)S(1)} %get-tuple-element.9), channel_id=1, source_target_pairs={{0,1},{1,2},{2,3},{3,0},{4,5},{5,6},{6,7},{7,4},{8,9},{9,10},{10,1... | collective-permute-start | bytes 1572872 | tf_op jit(solution)/shard_map/ppermute | solution.py:22
  66.8 10.4 %collective-permute-start.10 = (bf16[128,2048]{1,0:T(8,128)(2,1)S(1)}, bf16[128,2048]{1,0:T(8,128)(2,1)S(1)}, u32[]{:S(2)}, u32[]{:S(2)}) collective-permute-start(bf16[128,2048]{1,0:T(8,128)(2,1)S(1)} %get-tuple-element.10), channel_id=1, source_target_pairs={{0,3},{1,0},{2,1},{3,2},{4,7},{5,4},{6,5},{7,6},{8,11},{9,8},{10,9... | collective-permute-start | bytes 1572872 | tf_op jit(solution)/shard_map/ppermute | solution.py:22
  77.5 15.6 %collective-permute-start.11 = (bf16[256,2048]{1,0:T(8,128)(2,1)S(1)}, bf16[256,2048]{1,0:T(8,128)(2,1)S(1)}, u32[]{:S(2)}, u32[]{:S(2)}) collective-permute-start(bf16[256,2048]{1,0:T(8,128)(2,1)S(1)} %pad_maximum_fusion.1), channel_id=1, source_target_pairs={{0,3},{1,0},{2,1},{3,2},{4,7},{5,4},{6,5},{7,6},{8,11},{9,8},{10,9... | collective-permute-start | bytes 3145736 | tf_op jit(solution)/shard_map/ppermute | solution.py:22
  80.9 17.5 %collective-permute-start.9 = (bf16[256,2048]{1,0:T(8,128)(2,1)S(1)}, bf16[256,2048]{1,0:T(8,128)(2,1)S(1)}, u32[]{:S(2)}, u32[]{:S(2)}) collective-permute-start(bf16[256,2048]{1,0:T(8,128)(2,1)S(1)} %pad_maximum_fusion), channel_id=1, source_target_pairs={{0,1},{1,2},{2,3},{3,0},{4,5},{5,6},{6,7},{7,4},{8,9},{9,10},{10,1... | collective-permute-start | bytes 3145736 | tf_op jit(solution)/shard_map/ppermute | solution.py:22
  99.1 6.3 %collective-permute-start.12 = (bf16[32,2048]{1,0:T(8,128)(2,1)S(1)}, bf16[32,2048]{1,0:T(8,128)(2,1)S(1)}, u32[]{:S(2)}, u32[]{:S(2)}) collective-permute-start(bf16[32,2048]{1,0:T(8,128)(2,1)S(1)} %get-tuple-element.15), channel_id=1, source_target_pairs={{0,4},{1,5},{2,6},{3,7},{4,8},{5,9},{6,10},{7,11},{8,12},{9,13},{1... | collective-permute-start | bytes 393224 | tf_op jit(solution)/shard_map/ppermute | solution.py:22
  99.2 6.2 %collective-permute-start.14 = (bf16[32,2048]{1,0:T(8,128)(2,1)S(1)}, bf16[32,2048]{1,0:T(8,128)(2,1)S(1)}, u32[]{:S(2)}, u32[]{:S(2)}) collective-permute-start(bf16[32,2048]{1,0:T(8,128)(2,1)S(1)} %get-tuple-element.16), channel_id=1, source_target_pairs={{0,12},{1,13},{2,14},{3,15},{4,0},{5,1},{6,2},{7,3},{8,4},{9,5},{1... | collective-permute-start | bytes 393224 | tf_op jit(solution)/shard_map/ppermute | solution.py:22
  105.4 7.2 %collective-permute-start.15 = (bf16[64,2048]{1,0:T(8,128)(2,1)S(1)}, bf16[64,2048]{1,0:T(8,128)(2,1)S(1)}, u32[]{:S(2)}, u32[]{:S(2)}) collective-permute-start(bf16[64,2048]{1,0:T(8,128)(2,1)S(1)} %pad_maximum_fusion.3), channel_id=1, source_target_pairs={{0,12},{1,13},{2,14},{3,15},{4,0},{5,1},{6,2},{7,3},{8,4},{9,5},{1... | collective-permute-start | bytes 786440 | tf_op jit(solution)/shard_map/ppermute | solution.py:22
  108.8 7.7 %collective-permute-start.13 = (bf16[64,2048]{1,0:T(8,128)(2,1)S(1)}, bf16[64,2048]{1,0:T(8,128)(2,1)S(1)}, u32[]{:S(2)}, u32[]{:S(2)}) collective-permute-start(bf16[64,2048]{1,0:T(8,128)(2,1)S(1)} %pad_maximum_fusion.2), channel_id=1, source_target_pairs={{0,4},{1,5},{2,6},{3,7},{4,8},{5,9},{6,10},{7,11},{8,12},{9,13},{1... | collective-permute-start | bytes 786440 | tf_op jit(solution)/shard_map/ppermute | solution.py:22

commit v2 on v1

--- a/solution.py
+++ b/solution.py
@@ -32,15 +32,21 @@
     return jax.tree.map(lambda *vs: jnp.concatenate(vs, axis=0), tree, right, far, left)
 
 
-def scatter_ring(parts, axis):
-    cut = parts.shape[1] // 2
-    got_a = shift(parts[2, :cut].astype(jnp.bfloat16), axis, 1)
-    got_b = shift(parts[2, cut:].astype(jnp.bfloat16), axis, -1)
-    to_right = jnp.concatenate([parts[1, :cut] + got_a.astype(jnp.float32), parts[1, cut:]], axis=0)
-    to_left = jnp.concatenate([parts[3, :cut], parts[3, cut:] + got_b.astype(jnp.float32)], axis=0)
+def scatter_ring(own, right, far_a, far_b, left, axis):
+    got_a = shift(far_a.astype(jnp.bfloat16), axis, 1)
+    got_b = shift(far_b.astype(jnp.bfloat16), axis, -1)
+    cut = far_a.shape[0]
+    to_right = jnp.concatenate([right[:cut] + got_a.astype(jnp.float32), right[cut:]], axis=0)
+    to_left = jnp.concatenate([left[:cut], left[cut:] + got_b.astype(jnp.float32)], axis=0)
     from_left = shift(to_right.astype(jnp.bfloat16), axis, 1)
     from_right = shift(to_left.astype(jnp.bfloat16), axis, -1)
-    return parts[0] + from_left.astype(jnp.float32) + from_right.astype(jnp.float32)
+    return own + from_left.astype(jnp.float32) + from_right.astype(jnp.float32)
+
+
+def split_four(block):
+    n = block.shape[0] // SIDE
+    cut = n // 2
+    return block[:n], block[n:2 * n], block[2 * n:2 * n + cut], block[2 * n + cut:3 * n], block[3 * n:]
 
 
 def expert_rows(rows, me, width, w_in, w_out):
@@ -68,11 +74,15 @@
     low = (table - high.astype(jnp.float32)).astype(jnp.bfloat16)
     extra = jnp.zeros((count, PAD - 2 * SIDE * SIDE), jnp.bfloat16)
     payload = jnp.concatenate([hidden_in, high, low, extra], axis=1)
-    rows = gather_ring(gather_ring(payload, 0), 1)
-    weighted = expert_rows(rows, me, width, w_in[0], w_out[0])
-    part = weighted.reshape(SIDE, SIDE * count, width)
-    stage = scatter_ring(part, 1).reshape(SIDE, count, width)
-    return scatter_ring(stage, 0).astype(jnp.bfloat16)
+    first = gather_ring(payload, 0)
+    right = shift(first, 1, -1)
+    left = shift(first, 1, 1)
+    cut = first.shape[0] // 2
+    far_a = shift(left[:cut], 1, 1)
+    far_b = shift(right[cut:], 1, -1)
+    pieces = [expert_rows(p, me, width, w_in[0], w_out[0]) for p in (first, right, far_a, far_b, left)]
+    stage = scatter_ring(*pieces, 1)
+    return scatter_ring(*split_four(stage), 0).astype(jnp.bfloat16)
 
 
 def solution(mesh):

time: 117 us -> 104 us (0.89); the launches traced: 117 us -> 102 us
  waiting for transfers between devices: 58.4 us -> 46.3 us
  local copies, waits for them, and re-layouts: 15 us -> 7.31 us
  matrix products: 11.9 us -> 17.2 us
    ppermute x16, waiting for transfers between devices: 58.4 us -> 46.3 us  [shift(): return lax.ppermute(tree, ('dp', 'expert'), pairs)]
    unnamed x15 -> x10, local copies, waits for them, and re-layouts: 9.3 us -> 2.8 us
    dot_general x1 -> x5, matrix products: 8.43 us -> 12.9 us  [expert_rows(): jnp.dot(rows[:, :width], w_in, preferred_element_type=jnp.float32)]
    slice x0 -> x5, local copies, waits for them, and re-layouts: none -> 2.5 us  [the longest x1 1.24 us: body(): far_b = shift(right[cut:], 1, -1)]
    concatenate x2 -> x1, local copies, waits for them, and re-layouts: 1.98 us -> 0.73 us  [gather_ring(): jnp.concatenate(vs, axis=0)]
    slice x2 -> x1, local copies, waits for them, and re-layouts: 1.26 us -> 0.01 us  [gather_ring(): far_b = shift(jax.tree.map(lambda v: v[cut:], right), axis, -1)]
    dot_general x1 -> x5, matrix products: 3.51 us -> 4.33 us  [expert_rows(): jnp.dot(inner, w_out, preferred_element_type=jnp.float32)]
  transfers between devices with their start and end apart: 16 -> 16, of which waited for: 10 -> 9; matrix products, arithmetic and copies ran while one was open for 8% -> 22% of each run, Pallas kernels for 0% -> 0%
where the time goes in v2:
time: 104 us; the launch traced here: 102 us
  waiting for transfers between devices  46.3 us (45%)
  starting transfers between devices  27.2 us (26%)
  matrix products  17.2 us (17%)
  local copies, waits for them, and re-layouts  7.31 us (7%)
  other arithmetic  4.17 us (4%)
    ppermute x16, waiting for transfers between devices, shift(): return lax.ppermute(tree, ('dp', 'expert'), pairs)  46.3 us
    ppermute x16, starting transfers between devices, shift(): return lax.ppermute(tree, ('dp', 'expert'), pairs)  27.2 us
    dot_general x5, matrix products, expert_rows(): jnp.dot(rows[:, :width], w_in, preferred_element_type=jnp.float32)  12.9 us
    dot_general x5, matrix products, expert_rows(): jnp.dot(inner, w_out, preferred_element_type=jnp.float32)  4.33 us
    unnamed x10, local copies, waits for them, and re-layouts  2.8 us
  transfers between devices with their start and end apart: 16, of which 9 were waited for; matrix products, arithmetic and copies ran while one was open for 22% of the time, Pallas kernels for 0%

profile of v2, /device:TPU:64, one launch (start us, length us, event | category | flops | bytes accessed | tf_op | source)
XLA Modules:
  0.0 102.5 jit_solution(4020175609876568703)
XLA Ops:
  0.0 0.9 select_reduce_fusion.5
  1.1 1.1 %concatenate.22 = bf16[64,2176]{1,0:T(8,128)(2,1)S(1)} concatenate(bf16[64,2048]{1,0:T(8,128)(2,1)} %param.5, bf16[64,16]{1,0:T(8,128)(2,1)S(1)} %copy.8, bf16[64,16]{1,0:T(8,128)(2,1)S(1)} %copy.9, bf16[64,96]{1,0:T(8,128)(2,1)S(1)} %broadcast_in_dim.67), dimensions={1} | concatenate | bytes 557056 | tf_op jit(solution)/shard_map/concatenate | solution.py:76
  2.1 2.8 %collective-permute-start = (bf16[64,2176]{1,0:T(8,128)(2,1)S(1)}, bf16[64,2176]{1,0:T(8,128)(2,1)S(1)}, u32[]{:S(2)}, u32[]{:S(2)}) collective-permute-start(bf16[64,2176]{1,0:T(8,128)(2,1)S(1)} %concatenate.22), channel_id=1, source_target_pairs={{0,12},{1,13},{2,14},{3,15},{4,0},{5,1},{6,2},{7,3},{8,4},{9,5},{1... | collective-permute-start | bytes 835592 | tf_op jit(solution)/shard_map/ppermute | solution.py:22
  5.7 7.0 %collective-permute-done.1 = bf16[64,2176]{1,0:T(8,128)(2,1)S(1)} collective-permute-done((bf16[64,2176]{1,0:T(8,128)(2,1)S(1)}, bf16[64,2176]{1,0:T(8,128)(2,1)S(1)}, u32[]{:S(2)}, u32[]{:S(2)}) %collective-permute-start.1) | collective-permute-done | bytes 278560 | tf_op jit(solution)/shard_map/ppermute | solution.py:22
  12.9 3.3 %collective-permute-start.3 = (bf16[32,2176]{1,0:T(8,128)(2,1)S(1)}, bf16[32,2176]{1,0:T(8,128)(2,1)S(1)}, u32[]{:S(2)}, u32[]{:S(2)}) collective-permute-start(bf16[32,2176]{1,0:T(8,128)(2,1)S(1)} %slice.173), channel_id=1, source_target_pairs={{0,12},{1,13},{2,14},{3,15},{4,0},{5,1},{6,2},{7,3},{8,4},{9,5},{1... | collective-permute-start | bytes 417800 | tf_op jit(solution)/shard_map/ppermute | solution.py:22
  16.9 2.2 %collective-permute-done.2 = bf16[32,2176]{1,0:T(8,128)(2,1)S(1)} collective-permute-done((bf16[32,2176]{1,0:T(8,128)(2,1)S(1)}, bf16[32,2176]{1,0:T(8,128)(2,1)S(1)}, u32[]{:S(2)}, u32[]{:S(2)}) %collective-permute-start.2) | collective-permute-done | bytes 139296 | tf_op jit(solution)/shard_map/ppermute | solution.py:22
  21.2 1.6 %collective-permute-start.5 = (bf16[256,2176]{1,0:T(8,128)(2,1)}, bf16[256,2176]{1,0:T(8,128)(2,1)}, u32[]{:S(2)}, u32[]{:S(2)}) collective-permute-start(bf16[256,2176]{1,0:T(8,128)(2,1)} %constant_dynamic-update-slice_fusion), channel_id=1, source_target_pairs={{0,1},{1,2},{2,3},{3,0},{4,5},{5,6},{6,7},{7,4},{8,9},{9,10},{10,1... | collective-permute-start | bytes 3342344 | tf_op jit(solution)/shard_map/ppermute | solution.py:22
  22.7 1.7 %collective-permute-start.4 = (bf16[256,2176]{1,0:T(8,128)(2,1)}, bf16[256,2176]{1,0:T(8,128)(2,1)}, u32[]{:S(2)}, u32[]{:S(2)}) collective-permute-start(bf16[256,2176]{1,0:T(8,128)(2,1)} %constant_dynamic-update-slice_fusion), channel_id=1, source_target_pairs={{0,3},{1,0},{2,1},{3,2},{4,7},{5,4},{6,5},{7,6},{8,11},{9,8},{10,9... | collective-permute-start | bytes 3342344 | tf_op jit(solution)/shard_map/ppermute | solution.py:22
  24.4 13.8 %collective-permute-done.5 = bf16[256,2176]{1,0:T(8,128)(2,1)} collective-permute-done((bf16[256,2176]{1,0:T(8,128)(2,1)}, bf16[256,2176]{1,0:T(8,128)(2,1)}, u32[]{:S(2)}, u32[]{:S(2)}) %collective-permute-start.5) | collective-permute-done | bytes 1114144 | tf_op jit(solution)/shard_map/ppermute | solution.py:22
  38.2 1.1 %slice.185 = bf16[128,2176]{1,0:T(8,128)(2,1)S(1)} slice(bf16[256,2176]{1,0:T(8,128)(2,1)} %collective-permute-done.5), slice={[0:128], [0:2176]} | slice | bytes 1114112 | tf_op jit(solution)/shard_map/slice | solution.py:81
  39.7 1.2 %slice.199 = bf16[128,2176]{1,0:T(8,128)(2,1)S(1)} slice(bf16[256,2176]{1,0:T(8,128)(2,1)} %collective-permute-done.4), slice={[128:256], [0:2176]} | slice | bytes 1114112 | tf_op jit(solution)/shard_map/slice | solution.py:82
  41.0 3.1 %collective-permute-start.9 = (bf16[128,2176]{1,0:T(8,128)(2,1)S(1)}, bf16[128,2176]{1,0:T(8,128)(2,1)S(1)}, u32[]{:S(2)}, u32[]{:S(2)}) collective-permute-start(bf16[128,2176]{1,0:T(8,128)(2,1)S(1)} %slice.199), channel_id=1, source_target_pairs={{0,3},{1,0},{2,1},{3,2},{4,7},{5,4},{6,5},{7,6},{8,11},{9,8},{10,9... | collective-permute-start | bytes 1671176 | tf_op jit(solution)/shard_map/ppermute | solution.py:22
  44.1 4.9 %fusion.6 = f32[256,1536]{1,0:T(8,128)S(1)} fusion(bf16[1,2048,1536]{2,1,0:T(8,128)(2,1)} %param.8, bf16[256,2176]{1,0:T(8,128)(2,1)} %collective-permute-done.4), kind=kOutput, calls=%fused_computation.6 | convolution fusion | flops 1610612736 | bytes 8912896 | tf_op jit(solution)/shard_map/dot_general | solution.py:59
  49.1 3.0 %fusion.2 = f32[256,1536]{1,0:T(8,128)S(1)} fusion(bf16[1,2048,1536]{2,1,0:T(8,128)(2,1)S(1)} %bitcast.57, bf16[256,2176]{1,0:T(8,128)(2,1)} %collective-permute-done.5), kind=kOutput, calls=%fused_computation.2 | convolution fusion | flops 1610612736 | bytes 8912896 | tf_op jit(solution)/shard_map/dot_general | solution.py:59
  52.1 1.4 %select_reduce_fusion.1 = (f32[256]{0:T(256)S(1)}, f32[256]{0:T(256)S(1)}, f32[256]{0:T(256)S(1)}) fusion(bf16[256,2176]{1,0:T(8,128)(2,1)} %collective-permute-done.4, pred[16]{0:T(512)(128)(4,1)S(1)} %iota_compare_fusion.1, bf16[256,2176]{1,0:T(8,128)(2,1)} %collective-permute-done.5, bf16[256,2176]{1,0:T(8,128)(2,1)} %constant_dynamic-update-slice_fusion), kind=kLoop, calls=%fused_computation.76 | loop fusion | flops 60672 | bytes 52240 | tf_op jit(solution)/shard_map/reduce_sum | solution.py:58
  53.4 1.0 %fusion.35 = f32[256,2048]{1,0:T(8,128)S(1)} fusion(bf16[1,768,2048]{2,1,0:T(8,128)(2,1)S(1)} %copy-done, f32[256]{0:T(256)S(1)} %get-tuple-element.7, f32[256,1536]{1,0:T(8,128)S(1)} %fusion.6), kind=kOutput, calls=%fused_computation.25 | convolution fusion | flops 808058880 | bytes 6816768 | tf_op jit(solution)/shard_map/dot_general | solution.py:61
  54.5 1.0 fusion.44
  55.7 1.0 fusion.4
  57.6 1.0 fusion
  59.2 3.3 %collective-permute-start.10 = (bf16[128,2048]{1,0:T(8,128)(2,1)S(1)}, bf16[128,2048]{1,0:T(8,128)(2,1)S(1)}, u32[]{:S(2)}, u32[]{:S(2)}) collective-permute-start(bf16[128,2048]{1,0:T(8,128)(2,1)S(1)} %fusion.68), channel_id=1, source_target_pairs={{0,3},{1,0},{2,1},{3,2},{4,7},{5,4},{6,5},{7,6},{8,11},{9,8},{10,9... | collective-permute-start | bytes 1572872 | tf_op jit(solution)/shard_map/ppermute | solution.py:22
  62.5 5.5 %collective-permute-done.7 = bf16[128,2048]{1,0:T(8,128)(2,1)S(1)} collective-permute-done((bf16[128,2048]{1,0:T(8,128)(2,1)S(1)}, bf16[128,2048]{1,0:T(8,128)(2,1)S(1)}, u32[]{:S(2)}, u32[]{:S(2)}) %collective-permute-start.7) | collective-permute-done | bytes 524320 | tf_op jit(solution)/shard_map/ppermute | solution.py:22
  68.3 0.9 collective-permute-done.10
  69.4 4.0 %collective-permute-start.11 = (bf16[256,2048]{1,0:T(8,128)(2,1)S(1)}, bf16[256,2048]{1,0:T(8,128)(2,1)S(1)}, u32[]{:S(2)}, u32[]{:S(2)}) collective-permute-start(bf16[256,2048]{1,0:T(8,128)(2,1)S(1)} %pad_maximum_fusion.1), channel_id=1, source_target_pairs={{0,3},{1,0},{2,1},{3,2},{4,7},{5,4},{6,5},{7,6},{8,11},{9,8},{10,9... | collective-permute-start | bytes 3145736 | tf_op jit(solution)/shard_map/ppermute | solution.py:22
  73.4 3.0 %fusion.8 = f32[256,1536]{1,0:T(8,128)S(1)} fusion(bf16[1,2048,1536]{2,1,0:T(8,128)(2,1)S(1)} %bitcast.57, bf16[256,2176]{1,0:T(8,128)(2,1)} %constant_dynamic-update-slice_fusion), kind=kOutput, calls=%fused_computation.8 | convolution fusion | flops 1610612736 | bytes 8912896 | tf_op jit(solution)/shard_map/dot_general | solution.py:59
  76.4 1.0 fusion.26
  77.4 6.8 %collective-permute-done.8 = bf16[256,2048]{1,0:T(8,128)(2,1)S(1)} collective-permute-done((bf16[256,2048]{1,0:T(8,128)(2,1)S(1)}, bf16[256,2048]{1,0:T(8,128)(2,1)S(1)}, u32[]{:S(2)}, u32[]{:S(2)}) %collective-permute-start.8) | collective-permute-done | bytes 1048608 | tf_op jit(solution)/shard_map/ppermute | solution.py:22
  84.3 2.9 %collective-permute-done.11 = bf16[256,2048]{1,0:T(8,128)(2,1)S(1)} collective-permute-done((bf16[256,2048]{1,0:T(8,128)(2,1)S(1)}, bf16[256,2048]{1,0:T(8,128)(2,1)S(1)}, u32[]{:S(2)}, u32[]{:S(2)}) %collective-permute-start.11) | collective-permute-done | bytes 1048608 | tf_op jit(solution)/shard_map/ppermute | solution.py:22
  87.8 3.2 %collective-permute-start.14 = (bf16[32,2048]{1,0:T(8,128)(2,1)S(1)}, bf16[32,2048]{1,0:T(8,128)(2,1)S(1)}, u32[]{:S(2)}, u32[]{:S(2)}) collective-permute-start(bf16[32,2048]{1,0:T(8,128)(2,1)S(1)} %get-tuple-element.17), channel_id=1, source_target_pairs={{0,12},{1,13},{2,14},{3,15},{4,0},{5,1},{6,2},{7,3},{8,4},{9,5},{1... | collective-permute-start | bytes 393224 | tf_op jit(solution)/shard_map/ppermute | solution.py:22
  91.0 2.9 %collective-permute-done.12 = bf16[32,2048]{1,0:T(8,128)(2,1)S(1)} collective-permute-done((bf16[32,2048]{1,0:T(8,128)(2,1)S(1)}, bf16[32,2048]{1,0:T(8,128)(2,1)S(1)}, u32[]{:S(2)}, u32[]{:S(2)}) %collective-permute-start.12) | collective-permute-done | bytes 131104 | tf_op jit(solution)/shard_map/ppermute | solution.py:22
  94.4 3.0 %collective-permute-start.15 = (bf16[64,2048]{1,0:T(8,128)(2,1)S(1)}, bf16[64,2048]{1,0:T(8,128)(2,1)S(1)}, u32[]{:S(2)}, u32[]{:S(2)}) collective-permute-start(bf16[64,2048]{1,0:T(8,128)(2,1)S(1)} %pad_maximum_fusion.3), channel_id=1, source_target_pairs={{0,12},{1,13},{2,14},{3,15},{4,0},{5,1},{6,2},{7,3},{8,4},{9,5},{1... | collective-permute-start | bytes 786440 | tf_op jit(solution)/shard_map/ppermute | solution.py:22
  97.5 4.2 %collective-permute-done.13 = bf16[64,2048]{1,0:T(8,128)(2,1)S(1)} collective-permute-done((bf16[64,2048]{1,0:T(8,128)(2,1)S(1)}, bf16[64,2048]{1,0:T(8,128)(2,1)S(1)}, u32[]{:S(2)}, u32[]{:S(2)}) %collective-permute-start.13) | collective-permute-done | bytes 262176 | tf_op jit(solution)/shard_map/ppermute | solution.py:22
  101.7 0.8 fusion.80
  (47 shorter events, 7.5 us)
Async XLA Ops:
  0.0 53.4 %copy-start = (bf16[1,768,2048]{2,1,0:T(8,128)(2,1)S(1)}, bf16[1,768,2048]{2,1,0:T(8,128)(2,1)}, u32[]{:S(2)}) copy-start(bf16[1,768,2048]{2,1,0:T(8,128)(2,1)} %param.9) | copy-start | bytes 9437188
  2.1 10.7 %collective-permute-start = (bf16[64,2176]{1,0:T(8,128)(2,1)S(1)}, bf16[64,2176]{1,0:T(8,128)(2,1)S(1)}, u32[]{:S(2)}, u32[]{:S(2)}) collective-permute-start(bf16[64,2176]{1,0:T(8,128)(2,1)S(1)} %concatenate.22), channel_id=1, source_target_pairs={{0,12},{1,13},{2,14},{3,15},{4,0},{5,1},{6,2},{7,3},{8,4},{9,5},{1... | collective-permute-start | bytes 835592 | tf_op jit(solution)/shard_map/ppermute | solution.py:22
  5.0 7.8 %collective-permute-start.1 = (bf16[64,2176]{1,0:T(8,128)(2,1)S(1)}, bf16[64,2176]{1,0:T(8,128)(2,1)S(1)}, u32[]{:S(2)}, u32[]{:S(2)}) collective-permute-start(bf16[64,2176]{1,0:T(8,128)(2,1)S(1)} %concatenate.22), channel_id=1, source_target_pairs={{0,4},{1,5},{2,6},{3,7},{4,8},{5,9},{6,10},{7,11},{8,12},{9,13},{1... | collective-permute-start | bytes 835592 | tf_op jit(solution)/shard_map/ppermute | solution.py:22
  12.8 6.3 %collective-permute-start.2 = (bf16[32,2176]{1,0:T(8,128)(2,1)S(1)}, bf16[32,2176]{1,0:T(8,128)(2,1)S(1)}, u32[]{:S(2)}, u32[]{:S(2)}) collective-permute-start(bf16[32,2176]{1,0:T(8,128)(2,1)S(1)} %slice.172), channel_id=1, source_target_pairs={{0,4},{1,5},{2,6},{3,7},{4,8},{5,9},{6,10},{7,11},{8,12},{9,13},{1... | collective-permute-start | bytes 417800 | tf_op jit(solution)/shard_map/ppermute | solution.py:22
  12.9 6.9 %collective-permute-start.3 = (bf16[32,2176]{1,0:T(8,128)(2,1)S(1)}, bf16[32,2176]{1,0:T(8,128)(2,1)S(1)}, u32[]{:S(2)}, u32[]{:S(2)}) collective-permute-start(bf16[32,2176]{1,0:T(8,128)(2,1)S(1)} %slice.173), channel_id=1, source_target_pairs={{0,12},{1,13},{2,14},{3,15},{4,0},{5,1},{6,2},{7,3},{8,4},{9,5},{1... | collective-permute-start | bytes 417800 | tf_op jit(solution)/shard_map/ppermute | solution.py:22
  21.2 17.0 %collective-permute-start.5 = (bf16[256,2176]{1,0:T(8,128)(2,1)}, bf16[256,2176]{1,0:T(8,128)(2,1)}, u32[]{:S(2)}, u32[]{:S(2)}) collective-permute-start(bf16[256,2176]{1,0:T(8,128)(2,1)} %constant_dynamic-update-slice_fusion), channel_id=1, source_target_pairs={{0,1},{1,2},{2,3},{3,0},{4,5},{5,6},{6,7},{7,4},{8,9},{9,10},{10,1... | collective-permute-start | bytes 3342344 | tf_op jit(solution)/shard_map/ppermute | solution.py:22
  22.7 17.0 %collective-permute-start.4 = (bf16[256,2176]{1,0:T(8,128)(2,1)}, bf16[256,2176]{1,0:T(8,128)(2,1)}, u32[]{:S(2)}, u32[]{:S(2)}) collective-permute-start(bf16[256,2176]{1,0:T(8,128)(2,1)} %constant_dynamic-update-slice_fusion), channel_id=1, source_target_pairs={{0,3},{1,0},{2,1},{3,2},{4,7},{5,4},{6,5},{7,6},{8,11},{9,8},{10,9... | collective-permute-start | bytes 3342344 | tf_op jit(solution)/shard_map/ppermute | solution.py:22
  39.3 16.4 %collective-permute-start.6 = (bf16[128,2176]{1,0:T(8,128)(2,1)S(1)}, bf16[128,2176]{1,0:T(8,128)(2,1)S(1)}, u32[]{:S(2)}, u32[]{:S(2)}) collective-permute-start(bf16[128,2176]{1,0:T(8,128)(2,1)S(1)} %slice.185), channel_id=1, source_target_pairs={{0,1},{1,2},{2,3},{3,0},{4,5},{5,6},{6,7},{7,4},{8,9},{9,10},{10,1... | collective-permute-start | bytes 1671176 | tf_op jit(solution)/shard_map/ppermute | solution.py:22
  39.7 9.3 %slice-start = ((s8[6291456]{0:T(1024)(128)(4,1)}), s8[4194304]{0:T(1024)(128)(4,1)S(1)}, s32[]{:S(2)}) async-start(s8[6291456]{0:T(1024)(128)(4,1)} %bitcast.56), calls=%async_computation | async-start | bytes 8388608
  41.0 8.1 %slice-start.1 = ((s8[6291456]{0:T(1024)(128)(4,1)}), s8[2097152]{0:T(1024)(128)(4,1)S(1)}, s32[]{:S(2)}) async-start(s8[6291456]{0:T(1024)(128)(4,1)} %bitcast.56), calls=%async_computation.1 | async-start | bytes 4194304
  41.0 15.7 %collective-permute-start.9 = (bf16[128,2176]{1,0:T(8,128)(2,1)S(1)}, bf16[128,2176]{1,0:T(8,128)(2,1)S(1)}, u32[]{:S(2)}, u32[]{:S(2)}) collective-permute-start(bf16[128,2176]{1,0:T(8,128)(2,1)S(1)} %slice.199), channel_id=1, source_target_pairs={{0,3},{1,0},{2,1},{3,2},{4,7},{5,4},{6,5},{7,6},{8,11},{9,8},{10,9... | collective-permute-start | bytes 1671176 | tf_op jit(solution)/shard_map/ppermute | solution.py:22
  57.5 10.5 %collective-permute-start.7 = (bf16[128,2048]{1,0:T(8,128)(2,1)S(1)}, bf16[128,2048]{1,0:T(8,128)(2,1)S(1)}, u32[]{:S(2)}, u32[]{:S(2)}) collective-permute-start(bf16[128,2048]{1,0:T(8,128)(2,1)S(1)} %fusion.56), channel_id=1, source_target_pairs={{0,1},{1,2},{2,3},{3,0},{4,5},{5,6},{6,7},{7,4},{8,9},{9,10},{10,1... | collective-permute-start | bytes 1572872 | tf_op jit(solution)/shard_map/ppermute | solution.py:22
  59.2 10.0 %collective-permute-start.10 = (bf16[128,2048]{1,0:T(8,128)(2,1)S(1)}, bf16[128,2048]{1,0:T(8,128)(2,1)S(1)}, u32[]{:S(2)}, u32[]{:S(2)}) collective-permute-start(bf16[128,2048]{1,0:T(8,128)(2,1)S(1)} %fusion.68), channel_id=1, source_target_pairs={{0,3},{1,0},{2,1},{3,2},{4,7},{5,4},{6,5},{7,6},{8,11},{9,8},{10,9... | collective-permute-start | bytes 1572872 | tf_op jit(solution)/shard_map/ppermute | solution.py:22
  68.2 16.1 %collective-permute-start.8 = (bf16[256,2048]{1,0:T(8,128)(2,1)S(1)}, bf16[256,2048]{1,0:T(8,128)(2,1)S(1)}, u32[]{:S(2)}, u32[]{:S(2)}) collective-permute-start(bf16[256,2048]{1,0:T(8,128)(2,1)S(1)} %pad_maximum_fusion), channel_id=1, source_target_pairs={{0,1},{1,2},{2,3},{3,0},{4,5},{5,6},{6,7},{7,4},{8,9},{9,10},{10,1... | collective-permute-start | bytes 3145736 | tf_op jit(solution)/shard_map/ppermute | solution.py:22
  69.4 17.7 %collective-permute-start.11 = (bf16[256,2048]{1,0:T(8,128)(2,1)S(1)}, bf16[256,2048]{1,0:T(8,128)(2,1)S(1)}, u32[]{:S(2)}, u32[]{:S(2)}) collective-permute-start(bf16[256,2048]{1,0:T(8,128)(2,1)S(1)} %pad_maximum_fusion.1), channel_id=1, source_target_pairs={{0,3},{1,0},{2,1},{3,2},{4,7},{5,4},{6,5},{7,6},{8,11},{9,8},{10,9... | collective-permute-start | bytes 3145736 | tf_op jit(solution)/shard_map/ppermute | solution.py:22
  87.7 6.3 %collective-permute-start.12 = (bf16[32,2048]{1,0:T(8,128)(2,1)S(1)}, bf16[32,2048]{1,0:T(8,128)(2,1)S(1)}, u32[]{:S(2)}, u32[]{:S(2)}) collective-permute-start(bf16[32,2048]{1,0:T(8,128)(2,1)S(1)} %get-tuple-element.16), channel_id=1, source_target_pairs={{0,4},{1,5},{2,6},{3,7},{4,8},{5,9},{6,10},{7,11},{8,12},{9,13},{1... | collective-permute-start | bytes 393224 | tf_op jit(solution)/shard_map/ppermute | solution.py:22
  87.8 6.2 %collective-permute-start.14 = (bf16[32,2048]{1,0:T(8,128)(2,1)S(1)}, bf16[32,2048]{1,0:T(8,128)(2,1)S(1)}, u32[]{:S(2)}, u32[]{:S(2)}) collective-permute-start(bf16[32,2048]{1,0:T(8,128)(2,1)S(1)} %get-tuple-element.17), channel_id=1, source_target_pairs={{0,12},{1,13},{2,14},{3,15},{4,0},{5,1},{6,2},{7,3},{8,4},{9,5},{1... | collective-permute-start | bytes 393224 | tf_op jit(solution)/shard_map/ppermute | solution.py:22
  94.0 7.7 %collective-permute-start.13 = (bf16[64,2048]{1,0:T(8,128)(2,1)S(1)}, bf16[64,2048]{1,0:T(8,128)(2,1)S(1)}, u32[]{:S(2)}, u32[]{:S(2)}) collective-permute-start(bf16[64,2048]{1,0:T(8,128)(2,1)S(1)} %pad_maximum_fusion.2), channel_id=1, source_target_pairs={{0,4},{1,5},{2,6},{3,7},{4,8},{5,9},{6,10},{7,11},{8,12},{9,13},{1... | collective-permute-start | bytes 786440 | tf_op jit(solution)/shard_map/ppermute | solution.py:22
  94.4 7.3 %collective-permute-start.15 = (bf16[64,2048]{1,0:T(8,128)(2,1)S(1)}, bf16[64,2048]{1,0:T(8,128)(2,1)S(1)}, u32[]{:S(2)}, u32[]{:S(2)}) collective-permute-start(bf16[64,2048]{1,0:T(8,128)(2,1)S(1)} %pad_maximum_fusion.3), channel_id=1, source_target_pairs={{0,12},{1,13},{2,14},{3,15},{4,0},{5,1},{6,2},{7,3},{8,4},{9,5},{1... | collective-permute-start | bytes 786440 | tf_op jit(solution)/shard_map/ppermute | solution.py:22

commit v3 on v2

--- a/solution.py
+++ b/solution.py
@@ -49,20 +49,25 @@
     return block[:n], block[n:2 * n], block[2 * n:2 * n + cut], block[2 * n + cut:3 * n], block[3 * n:]
 
 
-def expert_rows(rows, me, width, w_in, w_out):
-    half = w_out.shape[0]
+def gate_column(rows, me, width):
     count = SIDE * SIDE
     experts = jnp.arange(count, dtype=jnp.int32)
     high = rows[:, width:width + count].astype(jnp.float32)
     low = rows[:, width + count:width + 2 * count].astype(jnp.float32)
-    mine = jnp.sum(jnp.where(experts[None, :] == me, high + low, jnp.float32(0.0)), axis=1)
+    return jnp.sum(jnp.where(experts[None, :] == me, high + low, jnp.float32(0.0)), axis=1)
+
+
+def expert_rows(rows, me, width, w_in, w_out, mine=None):
+    half = w_out.shape[0]
+    if mine is None:
+        mine = gate_column(rows, me, width)
     projected = jnp.dot(rows[:, :width], w_in, preferred_element_type=jnp.float32)
     inner = (jax.nn.silu(projected[:, :half]) * projected[:, half:]).astype(jnp.bfloat16)
     produced = jnp.dot(inner, w_out, preferred_element_type=jnp.float32).astype(jnp.bfloat16)
     return mine[:, None] * produced.astype(jnp.float32)
 
 
-def body(hidden_in, route_ids, gates, w_in, w_out):
+def layer(hidden_in, route_ids, gates, w_in, w_out):
     assert lax.axis_size("expert") == SIDE * SIDE
     me = lax.axis_index("expert")
     count, width = hidden_in.shape
@@ -75,12 +80,14 @@
     extra = jnp.zeros((count, PAD - 2 * SIDE * SIDE), jnp.bfloat16)
     payload = jnp.concatenate([hidden_in, high, low, extra], axis=1)
     first = gather_ring(payload, 0)
+    first, mine_first = lax.optimization_barrier((first, gate_column(first, me, width)))
     right = shift(first, 1, -1)
     left = shift(first, 1, 1)
     cut = first.shape[0] // 2
     far_a = shift(left[:cut], 1, 1)
     far_b = shift(right[cut:], 1, -1)
-    pieces = [expert_rows(p, me, width, w_in[0], w_out[0]) for p in (first, right, far_a, far_b, left)]
+    pieces = [expert_rows(first, me, width, w_in[0], w_out[0], mine_first)]
+    pieces += [expert_rows(p, me, width, w_in[0], w_out[0]) for p in (right, far_a, far_b, left)]
     stage = scatter_ring(*pieces, 1)
     return scatter_ring(*split_four(stage), 0).astype(jnp.bfloat16)
 
@@ -94,5 +101,5 @@
         P("expert", None, None),
     )
     return jax.shard_map(
-        body, mesh=mesh, in_specs=placed, out_specs=P(("dp", "expert"), None), check_vma=False
+        layer, mesh=mesh, in_specs=placed, out_specs=P(("dp", "expert"), None), check_vma=False
     )

time: 104 us -> 99.7 us (0.959)
  matrix products: 17.2 us -> 14.5 us
  local copies, waits for them, and re-layouts: 7.31 us -> 5.36 us
    dot_general x5, matrix products: 12.9 us -> 10.2 us  [expert_rows(): jnp.dot(rows[:, :width], w_in, preferred_element_type=jnp.float32)]
    slice x2, local copies, waits for them, and re-layouts: 2.34 us -> 0.08 us  [the longest x1 0.04 us: layer(): far_a = shift(left[:cut], 1, 1)]
    unnamed x10, local copies, waits for them, and re-layouts: 2.8 us -> 1.05 us
    reduce_sum x3 -> x4, other arithmetic: 2.4 us -> 1.45 us  [the longest x1 0.87 us: layer(): jnp.sum(jnp.where(route_ids[:, :, None] == experts, gates[:, :, None], jn...]
  transfers between devices with their start and end apart: 16 -> 16, of which waited for: 9 -> 11; matrix products, arithmetic and copies ran while one was open for 22% -> 18% of each run, Pallas kernels for 0% -> 0%
where the time goes in v3:
time: 99.7 us; the launch traced here: 98.2 us
  waiting for transfers between devices  47.1 us (47%)
  starting transfers between devices  27.6 us (28%)
  matrix products  14.5 us (15%)
  local copies, waits for them, and re-layouts  5.36 us (5%)
  other arithmetic  3.32 us (3%)
    ppermute x16, waiting for transfers between devices, shift(): return lax.ppermute(tree, ('dp', 'expert'), pairs)  47.1 us
    ppermute x16, starting transfers between devices, shift(): return lax.ppermute(tree, ('dp', 'expert'), pairs)  27.6 us
    dot_general x5, matrix products, expert_rows(): jnp.dot(rows[:, :width], w_in, preferred_element_type=jnp.float32)  10.2 us
    dot_general x5, matrix products, expert_rows(): jnp.dot(inner, w_out, preferred_element_type=jnp.float32)  4.29 us
  transfers between devices with their start and end apart: 16, of which 11 were waited for; matrix products, arithmetic and copies ran while one was open for 18% of the time, Pallas kernels for 0%

profile of v3, /device:TPU:64, one launch (start us, length us, event | category | flops | bytes accessed | tf_op | source)
XLA Modules:
  0.0 98.2 jit_solution(6877324889393571827)
XLA Ops:
  1.1 1.1 %concatenate.22 = bf16[64,2176]{1,0:T(8,128)(2,1)S(1)} concatenate(bf16[64,2048]{1,0:T(8,128)(2,1)} %param.5, bf16[64,16]{1,0:T(8,128)(2,1)S(1)} %copy.8, bf16[64,16]{1,0:T(8,128)(2,1)S(1)} %copy.9, bf16[64,96]{1,0:T(8,128)(2,1)S(1)} %broadcast_in_dim.66), dimensions={1} | concatenate | bytes 557056 | tf_op jit(solution)/shard_map/concatenate | solution.py:81
  2.1 2.8 %collective-permute-start = (bf16[64,2176]{1,0:T(8,128)(2,1)S(1)}, bf16[64,2176]{1,0:T(8,128)(2,1)}, u32[]{:S(2)}, u32[]{:S(2)}) collective-permute-start(bf16[64,2176]{1,0:T(8,128)(2,1)S(1)} %concatenate.22), channel_id=1, source_target_pairs={{0,12},{1,13},{2,14},{3,15},{4,0},{5,1},{6,2},{7,3},{8,4},{9,5},{1... | collective-permute-start | bytes 835592 | tf_op jit(solution)/shard_map/ppermute | solution.py:22
  5.0 7.8 %collective-permute-done.1 = bf16[64,2176]{1,0:T(8,128)(2,1)} collective-permute-done((bf16[64,2176]{1,0:T(8,128)(2,1)S(1)}, bf16[64,2176]{1,0:T(8,128)(2,1)}, u32[]{:S(2)}, u32[]{:S(2)}) %collective-permute-start.1) | collective-permute-done | bytes 278560 | tf_op jit(solution)/shard_map/ppermute | solution.py:22
  12.8 0.9 slice.172
  13.9 0.9 slice.173
  14.8 3.3 %collective-permute-start.3 = (bf16[32,2176]{1,0:T(8,128)(2,1)S(1)}, bf16[32,2176]{1,0:T(8,128)(2,1)S(1)}, u32[]{:S(2)}, u32[]{:S(2)}) collective-permute-start(bf16[32,2176]{1,0:T(8,128)(2,1)S(1)} %slice.173), channel_id=1, source_target_pairs={{0,12},{1,13},{2,14},{3,15},{4,0},{5,1},{6,2},{7,3},{8,4},{9,5},{1... | collective-permute-start | bytes 417800 | tf_op jit(solution)/shard_map/ppermute | solution.py:22
  18.1 1.0 constant_dynamic-update-slice_fusion.3
  19.1 1.0 %collective-permute-done.2 = bf16[32,2176]{1,0:T(8,128)(2,1)S(1)} collective-permute-done((bf16[32,2176]{1,0:T(8,128)(2,1)S(1)}, bf16[32,2176]{1,0:T(8,128)(2,1)S(1)}, u32[]{:S(2)}, u32[]{:S(2)}) %collective-permute-start.2) | collective-permute-done | bytes 139296 | tf_op jit(solution)/shard_map/ppermute | solution.py:22
  20.7 1.0 %constant_dynamic-update-slice_fusion = bf16[256,2176]{1,0:T(8,128)(2,1)S(1)} fusion(bf16[256,2176]{1,0:T(8,128)(2,1)S(1)} %constant_dynamic-update-slice_fusion.1, bf16[64,2176]{1,0:T(8,128)(2,1)} %collective-permute-done.1), kind=kLoop, calls=%fused_computation.81 | loop fusion | bytes 557056 | tf_op jit(solution)/shard_map/concatenate | solution.py:32
  21.9 1.9 %collective-permute-start.5 = (bf16[256,2176]{1,0:T(8,128)(2,1)S(1)}, bf16[256,2176]{1,0:T(8,128)(2,1)S(1)}, u32[]{:S(2)}, u32[]{:S(2)}) collective-permute-start(bf16[256,2176]{1,0:T(8,128)(2,1)S(1)} %constant_dynamic-update-slice_fusion), channel_id=1, source_target_pairs={{0,1},{1,2},{2,3},{3,0},{4,5},{5,6},{6,7},{7,4},{8,9},{9,10},{10,1... | collective-permute-start | bytes 3342344 | tf_op jit(solution)/shard_map/ppermute | solution.py:22
  23.8 1.4 %collective-permute-start.4 = (bf16[256,2176]{1,0:T(8,128)(2,1)S(1)}, bf16[256,2176]{1,0:T(8,128)(2,1)S(1)}, u32[]{:S(2)}, u32[]{:S(2)}) collective-permute-start(bf16[256,2176]{1,0:T(8,128)(2,1)S(1)} %constant_dynamic-update-slice_fusion), channel_id=1, source_target_pairs={{0,3},{1,0},{2,1},{3,2},{4,7},{5,4},{6,5},{7,6},{8,11},{9,8},{10,9... | collective-permute-start | bytes 3342344 | tf_op jit(solution)/shard_map/ppermute | solution.py:22
  25.2 13.5 %collective-permute-done.5 = bf16[256,2176]{1,0:T(8,128)(2,1)S(1)} collective-permute-done((bf16[256,2176]{1,0:T(8,128)(2,1)S(1)}, bf16[256,2176]{1,0:T(8,128)(2,1)S(1)}, u32[]{:S(2)}, u32[]{:S(2)}) %collective-permute-start.5) | collective-permute-done | bytes 1114144 | tf_op jit(solution)/shard_map/ppermute | solution.py:22
  39.5 2.7 %collective-permute-start.9 = (bf16[128,2176]{1,0:T(8,128)(2,1)S(1)}, bf16[128,2176]{1,0:T(8,128)(2,1)S(1)}, u32[]{:S(2)}, u32[]{:S(2)}) collective-permute-start(bf16[128,2176]{1,0:T(8,128)(2,1)S(1)} %slice.198), channel_id=1, source_target_pairs={{0,3},{1,0},{2,1},{3,2},{4,7},{5,4},{6,5},{7,6},{8,11},{9,8},{10,9... | collective-permute-start | bytes 1671176 | tf_op jit(solution)/shard_map/ppermute | solution.py:22
  42.4 4.7 %fusion.6 = f32[256,1536]{1,0:T(8,128)S(1)} fusion(bf16[1,2048,1536]{2,1,0:T(8,128)(2,1)} %param.8, bf16[256,2176]{1,0:T(8,128)(2,1)S(1)} %collective-permute-done.4), kind=kOutput, calls=%fused_computation.6 | convolution fusion | flops 1610612736 | bytes 8912896 | tf_op jit(solution)/shard_map/dot_general | solution.py:64
  47.1 1.8 %fusion.2 = f32[256,1536]{1,0:T(8,128)S(1)} fusion(bf16[1,2048,1536]{2,1,0:T(8,128)(2,1)S(1)} %bitcast.55, bf16[256,2176]{1,0:T(8,128)(2,1)S(1)} %collective-permute-done.5), kind=kOutput, calls=%fused_computation.2 | convolution fusion | flops 1610612736 | bytes 8912896 | tf_op jit(solution)/shard_map/dot_general | solution.py:64
  48.9 1.0 %fusion.32 = f32[256,2048]{1,0:T(8,128)S(1)} fusion(bf16[1,768,2048]{2,1,0:T(8,128)(2,1)S(1)} %copy-done, f32[256]{0:T(256)S(1)} %get-tuple-element.11, f32[256,1536]{1,0:T(8,128)S(1)} %fusion.6), kind=kOutput, calls=%fused_computation.24 | convolution fusion | flops 808058880 | bytes 6816768 | tf_op jit(solution)/shard_map/dot_general | solution.py:66
  50.0 1.0 %fusion.41 = f32[256,2048]{1,0:T(8,128)S(1)} fusion(bf16[1,768,2048]{2,1,0:T(8,128)(2,1)S(1)} %copy-done, f32[256]{0:T(256)S(1)} %get-tuple-element.12, f32[256,1536]{1,0:T(8,128)S(1)} %fusion.2), kind=kOutput, calls=%fused_computation.27 | convolution fusion | flops 808058880 | bytes 6816768 | tf_op jit(solution)/shard_map/dot_general | solution.py:66
  51.1 1.0 %fusion.4 = f32[128,1536]{1,0:T(8,128)S(1)} fusion(bf16[1,2048,1536]{2,1,0:T(8,128)(2,1)S(1)} %bitcast.55, bf16[128,2176]{1,0:T(8,128)(2,1)S(1)} %collective-permute-done.6), kind=kOutput, calls=%fused_computation.4 | convolution fusion | flops 805306368 | bytes 7602176 | tf_op jit(solution)/shard_map/dot_general | solution.py:64
  53.2 1.0 %fusion = f32[128,1536]{1,0:T(8,128)S(1)} fusion(bf16[1,2048,1536]{2,1,0:T(8,128)(2,1)S(1)} %bitcast.55, bf16[128,2176]{1,0:T(8,128)(2,1)S(1)} %collective-permute-done.9), kind=kOutput, calls=%fused_computation | convolution fusion | flops 805306368 | bytes 7602176 | tf_op jit(solution)/shard_map/dot_general | solution.py:64
  54.9 3.3 %collective-permute-start.10 = (bf16[128,2048]{1,0:T(8,128)(2,1)S(1)}, bf16[128,2048]{1,0:T(8,128)(2,1)S(1)}, u32[]{:S(2)}, u32[]{:S(2)}) collective-permute-start(bf16[128,2048]{1,0:T(8,128)(2,1)S(1)} %fusion.65), channel_id=1, source_target_pairs={{0,3},{1,0},{2,1},{3,2},{4,7},{5,4},{6,5},{7,6},{8,11},{9,8},{10,9... | collective-permute-start | bytes 1572872 | tf_op jit(solution)/shard_map/ppermute | solution.py:22
  58.1 5.5 %collective-permute-done.7 = bf16[128,2048]{1,0:T(8,128)(2,1)S(1)} collective-permute-done((bf16[128,2048]{1,0:T(8,128)(2,1)S(1)}, bf16[128,2048]{1,0:T(8,128)(2,1)S(1)}, u32[]{:S(2)}, u32[]{:S(2)}) %collective-permute-start.7) | collective-permute-done | bytes 524320 | tf_op jit(solution)/shard_map/ppermute | solution.py:22
  63.9 0.9 collective-permute-done.10
  65.0 3.8 %collective-permute-start.11 = (bf16[256,2048]{1,0:T(8,128)(2,1)S(1)}, bf16[256,2048]{1,0:T(8,128)(2,1)S(1)}, u32[]{:S(2)}, u32[]{:S(2)}) collective-permute-start(bf16[256,2048]{1,0:T(8,128)(2,1)S(1)} %pad_maximum_fusion.1), channel_id=1, source_target_pairs={{0,3},{1,0},{2,1},{3,2},{4,7},{5,4},{6,5},{7,6},{8,11},{9,8},{10,9... | collective-permute-start | bytes 3145736 | tf_op jit(solution)/shard_map/ppermute | solution.py:22
  68.8 1.8 %fusion.8 = f32[256,1536]{1,0:T(8,128)S(1)} fusion(bf16[1,2048,1536]{2,1,0:T(8,128)(2,1)S(1)} %bitcast.55, bf16[256,2176]{1,0:T(8,128)(2,1)S(1)} %constant_dynamic-update-slice_fusion), kind=kOutput, calls=%fused_computation.8 | convolution fusion | flops 1610612736 | bytes 8912896 | tf_op jit(solution)/shard_map/dot_general | solution.py:64
  70.6 1.0 %fusion.23 = f32[256,2048]{1,0:T(8,128)S(1)} fusion(bf16[1,768,2048]{2,1,0:T(8,128)(2,1)S(1)} %copy-done, f32[256,1536]{1,0:T(8,128)S(1)} %fusion.8), kind=kOutput, calls=%fused_computation.21 | convolution fusion | flops 807534592 | bytes 6815744 | tf_op jit(solution)/shard_map/dot_general | solution.py:66
  71.6 8.3 %collective-permute-done.8 = bf16[256,2048]{1,0:T(8,128)(2,1)S(1)} collective-permute-done((bf16[256,2048]{1,0:T(8,128)(2,1)S(1)}, bf16[256,2048]{1,0:T(8,128)(2,1)S(1)}, u32[]{:S(2)}, u32[]{:S(2)}) %collective-permute-start.8) | collective-permute-done | bytes 1048608 | tf_op jit(solution)/shard_map/ppermute | solution.py:22
  79.9 2.2 %collective-permute-done.11 = bf16[256,2048]{1,0:T(8,128)(2,1)S(1)} collective-permute-done((bf16[256,2048]{1,0:T(8,128)(2,1)S(1)}, bf16[256,2048]{1,0:T(8,128)(2,1)S(1)}, u32[]{:S(2)}, u32[]{:S(2)}) %collective-permute-start.11) | collective-permute-done | bytes 1048608 | tf_op jit(solution)/shard_map/ppermute | solution.py:22
  82.9 3.7 %collective-permute-start.14 = (bf16[32,2048]{1,0:T(8,128)(2,1)S(1)}, bf16[32,2048]{1,0:T(8,128)(2,1)S(1)}, u32[]{:S(2)}, u32[]{:S(2)}) collective-permute-start(bf16[32,2048]{1,0:T(8,128)(2,1)S(1)} %get-tuple-element.20), channel_id=1, source_target_pairs={{0,12},{1,13},{2,14},{3,15},{4,0},{5,1},{6,2},{7,3},{8,4},{9,5},{1... | collective-permute-start | bytes 393224 | tf_op jit(solution)/shard_map/ppermute | solution.py:22
  86.6 2.9 %collective-permute-done.12 = bf16[32,2048]{1,0:T(8,128)(2,1)S(1)} collective-permute-done((bf16[32,2048]{1,0:T(8,128)(2,1)S(1)}, bf16[32,2048]{1,0:T(8,128)(2,1)S(1)}, u32[]{:S(2)}, u32[]{:S(2)}) %collective-permute-start.12) | collective-permute-done | bytes 131104 | tf_op jit(solution)/shard_map/ppermute | solution.py:22
  89.5 1.5 %collective-permute-start.13 = (bf16[64,2048]{1,0:T(8,128)(2,1)S(1)}, bf16[64,2048]{1,0:T(8,128)(2,1)S(1)}, u32[]{:S(2)}, u32[]{:S(2)}) collective-permute-start(bf16[64,2048]{1,0:T(8,128)(2,1)S(1)} %pad_maximum_fusion.2), channel_id=1, source_target_pairs={{0,4},{1,5},{2,6},{3,7},{4,8},{5,9},{6,10},{7,11},{8,12},{9,13},{1... | collective-permute-start | bytes 786440 | tf_op jit(solution)/shard_map/ppermute | solution.py:22
  91.0 2.0 %collective-permute-start.15 = (bf16[64,2048]{1,0:T(8,128)(2,1)S(1)}, bf16[64,2048]{1,0:T(8,128)(2,1)S(1)}, u32[]{:S(2)}, u32[]{:S(2)}) collective-permute-start(bf16[64,2048]{1,0:T(8,128)(2,1)S(1)} %pad_maximum_fusion.3), channel_id=1, source_target_pairs={{0,12},{1,13},{2,14},{3,15},{4,0},{5,1},{6,2},{7,3},{8,4},{9,5},{1... | collective-permute-start | bytes 786440 | tf_op jit(solution)/shard_map/ppermute | solution.py:22
  93.0 4.2 %collective-permute-done.13 = bf16[64,2048]{1,0:T(8,128)(2,1)S(1)} collective-permute-done((bf16[64,2048]{1,0:T(8,128)(2,1)S(1)}, bf16[64,2048]{1,0:T(8,128)(2,1)S(1)}, u32[]{:S(2)}, u32[]{:S(2)}) %collective-permute-start.13) | collective-permute-done | bytes 262176 | tf_op jit(solution)/shard_map/ppermute | solution.py:22
  (48 shorter events, 7.1 us)
Async XLA Ops:
  0.0 48.9 %copy-start = (bf16[1,768,2048]{2,1,0:T(8,128)(2,1)S(1)}, bf16[1,768,2048]{2,1,0:T(8,128)(2,1)}, u32[]{:S(2)}) copy-start(bf16[1,768,2048]{2,1,0:T(8,128)(2,1)} %param.9) | copy-start | bytes 9437188
  2.1 11.7 %collective-permute-start = (bf16[64,2176]{1,0:T(8,128)(2,1)S(1)}, bf16[64,2176]{1,0:T(8,128)(2,1)}, u32[]{:S(2)}, u32[]{:S(2)}) collective-permute-start(bf16[64,2176]{1,0:T(8,128)(2,1)S(1)} %concatenate.22), channel_id=1, source_target_pairs={{0,12},{1,13},{2,14},{3,15},{4,0},{5,1},{6,2},{7,3},{8,4},{9,5},{1... | collective-permute-start | bytes 835592 | tf_op jit(solution)/shard_map/ppermute | solution.py:22
  5.0 7.9 %collective-permute-start.1 = (bf16[64,2176]{1,0:T(8,128)(2,1)S(1)}, bf16[64,2176]{1,0:T(8,128)(2,1)}, u32[]{:S(2)}, u32[]{:S(2)}) collective-permute-start(bf16[64,2176]{1,0:T(8,128)(2,1)S(1)} %concatenate.22), channel_id=1, source_target_pairs={{0,4},{1,5},{2,6},{3,7},{4,8},{5,9},{6,10},{7,11},{8,12},{9,13},{1... | collective-permute-start | bytes 835592 | tf_op jit(solution)/shard_map/ppermute | solution.py:22
  13.8 6.3 %collective-permute-start.2 = (bf16[32,2176]{1,0:T(8,128)(2,1)S(1)}, bf16[32,2176]{1,0:T(8,128)(2,1)S(1)}, u32[]{:S(2)}, u32[]{:S(2)}) collective-permute-start(bf16[32,2176]{1,0:T(8,128)(2,1)S(1)} %slice.172), channel_id=1, source_target_pairs={{0,4},{1,5},{2,6},{3,7},{4,8},{5,9},{6,10},{7,11},{8,12},{9,13},{1... | collective-permute-start | bytes 417800 | tf_op jit(solution)/shard_map/ppermute | solution.py:22
  14.8 5.9 %collective-permute-start.3 = (bf16[32,2176]{1,0:T(8,128)(2,1)S(1)}, bf16[32,2176]{1,0:T(8,128)(2,1)S(1)}, u32[]{:S(2)}, u32[]{:S(2)}) collective-permute-start(bf16[32,2176]{1,0:T(8,128)(2,1)S(1)} %slice.173), channel_id=1, source_target_pairs={{0,12},{1,13},{2,14},{3,15},{4,0},{5,1},{6,2},{7,3},{8,4},{9,5},{1... | collective-permute-start | bytes 417800 | tf_op jit(solution)/shard_map/ppermute | solution.py:22
  21.9 16.8 %collective-permute-start.5 = (bf16[256,2176]{1,0:T(8,128)(2,1)S(1)}, bf16[256,2176]{1,0:T(8,128)(2,1)S(1)}, u32[]{:S(2)}, u32[]{:S(2)}) collective-permute-start(bf16[256,2176]{1,0:T(8,128)(2,1)S(1)} %constant_dynamic-update-slice_fusion), channel_id=1, source_target_pairs={{0,1},{1,2},{2,3},{3,0},{4,5},{5,6},{6,7},{7,4},{8,9},{9,10},{10,1... | collective-permute-start | bytes 3342344 | tf_op jit(solution)/shard_map/ppermute | solution.py:22
  23.8 15.6 %collective-permute-start.4 = (bf16[256,2176]{1,0:T(8,128)(2,1)S(1)}, bf16[256,2176]{1,0:T(8,128)(2,1)S(1)}, u32[]{:S(2)}, u32[]{:S(2)}) collective-permute-start(bf16[256,2176]{1,0:T(8,128)(2,1)S(1)} %constant_dynamic-update-slice_fusion), channel_id=1, source_target_pairs={{0,3},{1,0},{2,1},{3,2},{4,7},{5,4},{6,5},{7,6},{8,11},{9,8},{10,9... | collective-permute-start | bytes 3342344 | tf_op jit(solution)/shard_map/ppermute | solution.py:22
  38.7 12.4 %collective-permute-start.6 = (bf16[128,2176]{1,0:T(8,128)(2,1)S(1)}, bf16[128,2176]{1,0:T(8,128)(2,1)S(1)}, u32[]{:S(2)}, u32[]{:S(2)}) collective-permute-start(bf16[128,2176]{1,0:T(8,128)(2,1)S(1)} %slice.184), channel_id=1, source_target_pairs={{0,1},{1,2},{2,3},{3,0},{4,5},{5,6},{6,7},{7,4},{8,9},{9,10},{10,1... | collective-permute-start | bytes 1671176 | tf_op jit(solution)/shard_map/ppermute | solution.py:22
  39.4 7.7 %slice-start = ((s8[6291456]{0:T(1024)(128)(4,1)}), s8[4194304]{0:T(1024)(128)(4,1)S(1)}, s32[]{:S(2)}) async-start(s8[6291456]{0:T(1024)(128)(4,1)} %bitcast.54), calls=%async_computation | async-start | bytes 8388608
  39.5 12.7 %collective-permute-start.9 = (bf16[128,2176]{1,0:T(8,128)(2,1)S(1)}, bf16[128,2176]{1,0:T(8,128)(2,1)S(1)}, u32[]{:S(2)}, u32[]{:S(2)}) collective-permute-start(bf16[128,2176]{1,0:T(8,128)(2,1)S(1)} %slice.198), channel_id=1, source_target_pairs={{0,3},{1,0},{2,1},{3,2},{4,7},{5,4},{6,5},{7,6},{8,11},{9,8},{10,9... | collective-permute-start | bytes 1671176 | tf_op jit(solution)/shard_map/ppermute | solution.py:22
  42.4 4.7 %slice-start.1 = ((s8[6291456]{0:T(1024)(128)(4,1)}), s8[2097152]{0:T(1024)(128)(4,1)S(1)}, s32[]{:S(2)}) async-start(s8[6291456]{0:T(1024)(128)(4,1)} %bitcast.54), calls=%async_computation.1 | async-start | bytes 4194304
  53.0 10.6 %collective-permute-start.7 = (bf16[128,2048]{1,0:T(8,128)(2,1)S(1)}, bf16[128,2048]{1,0:T(8,128)(2,1)S(1)}, u32[]{:S(2)}, u32[]{:S(2)}) collective-permute-start(bf16[128,2048]{1,0:T(8,128)(2,1)S(1)} %fusion.53), channel_id=1, source_target_pairs={{0,1},{1,2},{2,3},{3,0},{4,5},{5,6},{6,7},{7,4},{8,9},{9,10},{10,1... | collective-permute-start | bytes 1572872 | tf_op jit(solution)/shard_map/ppermute | solution.py:22
  54.9 10.0 %collective-permute-start.10 = (bf16[128,2048]{1,0:T(8,128)(2,1)S(1)}, bf16[128,2048]{1,0:T(8,128)(2,1)S(1)}, u32[]{:S(2)}, u32[]{:S(2)}) collective-permute-start(bf16[128,2048]{1,0:T(8,128)(2,1)S(1)} %fusion.65), channel_id=1, source_target_pairs={{0,3},{1,0},{2,1},{3,2},{4,7},{5,4},{6,5},{7,6},{8,11},{9,8},{10,9... | collective-permute-start | bytes 1572872 | tf_op jit(solution)/shard_map/ppermute | solution.py:22
  63.8 16.1 %collective-permute-start.8 = (bf16[256,2048]{1,0:T(8,128)(2,1)S(1)}, bf16[256,2048]{1,0:T(8,128)(2,1)S(1)}, u32[]{:S(2)}, u32[]{:S(2)}) collective-permute-start(bf16[256,2048]{1,0:T(8,128)(2,1)S(1)} %pad_maximum_fusion), channel_id=1, source_target_pairs={{0,1},{1,2},{2,3},{3,0},{4,5},{5,6},{6,7},{7,4},{8,9},{9,10},{10,1... | collective-permute-start | bytes 3145736 | tf_op jit(solution)/shard_map/ppermute | solution.py:22
  65.0 17.1 %collective-permute-start.11 = (bf16[256,2048]{1,0:T(8,128)(2,1)S(1)}, bf16[256,2048]{1,0:T(8,128)(2,1)S(1)}, u32[]{:S(2)}, u32[]{:S(2)}) collective-permute-start(bf16[256,2048]{1,0:T(8,128)(2,1)S(1)} %pad_maximum_fusion.1), channel_id=1, source_target_pairs={{0,3},{1,0},{2,1},{3,2},{4,7},{5,4},{6,5},{7,6},{8,11},{9,8},{10,9... | collective-permute-start | bytes 3145736 | tf_op jit(solution)/shard_map/ppermute | solution.py:22
  82.8 6.6 %collective-permute-start.12 = (bf16[32,2048]{1,0:T(8,128)(2,1)S(1)}, bf16[32,2048]{1,0:T(8,128)(2,1)S(1)}, u32[]{:S(2)}, u32[]{:S(2)}) collective-permute-start(bf16[32,2048]{1,0:T(8,128)(2,1)S(1)} %get-tuple-element.19), channel_id=1, source_target_pairs={{0,4},{1,5},{2,6},{3,7},{4,8},{5,9},{6,10},{7,11},{8,12},{9,13},{1... | collective-permute-start | bytes 393224 | tf_op jit(solution)/shard_map/ppermute | solution.py:22
  82.9 6.6 %collective-permute-start.14 = (bf16[32,2048]{1,0:T(8,128)(2,1)S(1)}, bf16[32,2048]{1,0:T(8,128)(2,1)S(1)}, u32[]{:S(2)}, u32[]{:S(2)}) collective-permute-start(bf16[32,2048]{1,0:T(8,128)(2,1)S(1)} %get-tuple-element.20), channel_id=1, source_target_pairs={{0,12},{1,13},{2,14},{3,15},{4,0},{5,1},{6,2},{7,3},{8,4},{9,5},{1... | collective-permute-start | bytes 393224 | tf_op jit(solution)/shard_map/ppermute | solution.py:22
  89.5 7.7 %collective-permute-start.13 = (bf16[64,2048]{1,0:T(8,128)(2,1)S(1)}, bf16[64,2048]{1,0:T(8,128)(2,1)S(1)}, u32[]{:S(2)}, u32[]{:S(2)}) collective-permute-start(bf16[64,2048]{1,0:T(8,128)(2,1)S(1)} %pad_maximum_fusion.2), channel_id=1, source_target_pairs={{0,4},{1,5},{2,6},{3,7},{4,8},{5,9},{6,10},{7,11},{8,12},{9,13},{1... | collective-permute-start | bytes 786440 | tf_op jit(solution)/shard_map/ppermute | solution.py:22
  91.0 6.5 %collective-permute-start.15 = (bf16[64,2048]{1,0:T(8,128)(2,1)S(1)}, bf16[64,2048]{1,0:T(8,128)(2,1)S(1)}, u32[]{:S(2)}, u32[]{:S(2)}) collective-permute-start(bf16[64,2048]{1,0:T(8,128)(2,1)S(1)} %pad_maximum_fusion.3), channel_id=1, source_target_pairs={{0,12},{1,13},{2,14},{3,15},{4,0},{5,1},{6,2},{7,3},{8,4},{9,5},{1... | collective-permute-start | bytes 786440 | tf_op jit(solution)/shard_map/ppermute | solution.py:22

commit v4 on v3

--- a/solution.py
+++ b/solution.py
@@ -22,16 +22,6 @@
     return lax.ppermute(tree, ("dp", "expert"), pairs)
 
 
-def gather_ring(tree, axis):
-    right = shift(tree, axis, -1)
-    left = shift(tree, axis, 1)
-    cut = jax.tree.leaves(tree)[0].shape[0] // 2
-    far_a = shift(jax.tree.map(lambda v: v[:cut], left), axis, 1)
-    far_b = shift(jax.tree.map(lambda v: v[cut:], right), axis, -1)
-    far = jax.tree.map(lambda a, b: jnp.concatenate([a, b], axis=0), far_a, far_b)
-    return jax.tree.map(lambda *vs: jnp.concatenate(vs, axis=0), tree, right, far, left)
-
-
 def scatter_ring(own, right, far_a, far_b, left, axis):
     got_a = shift(far_a.astype(jnp.bfloat16), axis, 1)
     got_b = shift(far_b.astype(jnp.bfloat16), axis, -1)
@@ -43,10 +33,18 @@
     return own + from_left.astype(jnp.float32) + from_right.astype(jnp.float32)
 
 
-def split_four(block):
-    n = block.shape[0] // SIDE
-    cut = n // 2
-    return block[:n], block[n:2 * n], block[2 * n:2 * n + cut], block[2 * n + cut:3 * n], block[3 * n:]
+def gather_direct(block, stage):
+    right = shift(block, stage, -1)
+    far = shift(block, stage, 2)
+    left = shift(block, stage, 1)
+    return jnp.concatenate([block, right, far, left], axis=0)
+
+
+def scatter_direct(parts, stage):
+    from_left = shift(parts[1].astype(jnp.bfloat16), stage, 1)
+    from_far = shift(parts[2].astype(jnp.bfloat16), stage, 2)
+    from_right = shift(parts[3].astype(jnp.bfloat16), stage, -1)
+    return parts[0] + from_left.astype(jnp.float32) + from_far.astype(jnp.float32) + from_right.astype(jnp.float32)
 
 
 def gate_column(rows, me, width):
@@ -79,7 +77,7 @@
     low = (table - high.astype(jnp.float32)).astype(jnp.bfloat16)
     extra = jnp.zeros((count, PAD - 2 * SIDE * SIDE), jnp.bfloat16)
     payload = jnp.concatenate([hidden_in, high, low, extra], axis=1)
-    first = gather_ring(payload, 0)
+    first = gather_direct(payload, 0)
     first, mine_first = lax.optimization_barrier((first, gate_column(first, me, width)))
     right = shift(first, 1, -1)
     left = shift(first, 1, 1)
@@ -89,7 +87,7 @@
     pieces = [expert_rows(first, me, width, w_in[0], w_out[0], mine_first)]
     pieces += [expert_rows(p, me, width, w_in[0], w_out[0]) for p in (right, far_a, far_b, left)]
     stage = scatter_ring(*pieces, 1)
-    return scatter_ring(*split_four(stage), 0).astype(jnp.bfloat16)
+    return scatter_direct(stage.reshape(SIDE, count, width), 0).astype(jnp.bfloat16)
 
 
 def solution(mesh):

time: 99.7 us -> 94.2 us (0.945)
  starting transfers between devices: 27.6 us -> 21.9 us
  local copies, waits for them, and re-layouts: 5.36 us -> 1.54 us
  waiting for transfers between devices: 47.1 us -> 50.6 us
  other arithmetic: 3.32 us -> 4.45 us
    ppermute x16 -> x14, starting transfers between devices: 27.6 us -> 21.9 us  [shift(): return lax.ppermute(tree, ('dp', 'expert'), pairs)]
    ppermute x16 -> x14, waiting for transfers between devices: 47.1 us -> 50.6 us  [shift(): return lax.ppermute(tree, ('dp', 'expert'), pairs)]
    slice x3 -> x1, local copies, waits for them, and re-layouts: 1.87 us -> 0.07 us  [scatter_direct(): from_left = shift(parts[1].astype(jnp.bfloat16), stage, 1)]
    concatenate x0 -> x1, other arithmetic: none -> 1.2 us  [gather_direct(): return jnp.concatenate([block, right, far, left], axis=0)]
    unnamed x10 -> x6, local copies, waits for them, and re-layouts: 1.05 us -> 0.01 us
  transfers between devices with their start and end apart: 16 -> 14, of which waited for: 11 -> 10; matrix products, arithmetic and copies ran while one was open for 18% -> 16% of each run, Pallas kernels for 0% -> 0%
where the time goes in v4:
time: 94.2 us; the launch traced here: 93.4 us
  waiting for transfers between devices  50.6 us (54%)
  starting transfers between devices  21.9 us (23%)
  matrix products  14.6 us (15%)
  other arithmetic  4.45 us (5%)
  local copies, waits for them, and re-layouts  1.54 us (2%)
    ppermute x14, waiting for transfers between devices, shift(): return lax.ppermute(tree, ('dp', 'expert'), pairs)  50.6 us
    ppermute x14, starting transfers between devices, shift(): return lax.ppermute(tree, ('dp', 'expert'), pairs)  21.9 us
    dot_general x5, matrix products, expert_rows(): jnp.dot(rows[:, :width], w_in, preferred_element_type=jnp.float32)  10.2 us
    dot_general x5, matrix products, expert_rows(): jnp.dot(inner, w_out, preferred_element_type=jnp.float32)  4.34 us
  transfers between devices with their start and end apart: 14, of which 10 were waited for; matrix products, arithmetic and copies ran while one was open for 16% of the time, Pallas kernels for 0%

profile of v4, /device:TPU:64, one launch (start us, length us, event | category | flops | bytes accessed | tf_op | source)
XLA Modules:
  0.0 93.4 jit_solution(17592655618238757508)
XLA Ops:
  0.0 0.9 select_reduce_fusion.5
  1.1 1.1 %concatenate.14 = bf16[64,2176]{1,0:T(8,128)(2,1)S(1)} concatenate(bf16[64,2048]{1,0:T(8,128)(2,1)} %param.5, bf16[64,16]{1,0:T(8,128)(2,1)S(1)} %copy.8, bf16[64,16]{1,0:T(8,128)(2,1)S(1)} %copy.9, bf16[64,96]{1,0:T(8,128)(2,1)S(1)} %broadcast_in_dim.66), dimensions={1} | concatenate | bytes 557056 | tf_op jit(solution)/shard_map/concatenate | solution.py:79
  2.1 2.8 %collective-permute-start = (bf16[64,2176]{1,0:T(8,128)(2,1)S(1)}, bf16[64,2176]{1,0:T(8,128)(2,1)}, u32[]{:S(2)}, u32[]{:S(2)}) collective-permute-start(bf16[64,2176]{1,0:T(8,128)(2,1)S(1)} %concatenate.14), channel_id=1, source_target_pairs={{0,12},{1,13},{2,14},{3,15},{4,0},{5,1},{6,2},{7,3},{8,4},{9,5},{1... | collective-permute-start | bytes 835592 | tf_op jit(solution)/shard_map/ppermute | solution.py:22
  5.0 0.8 collective-permute-start.1
  5.8 0.9 collective-permute-start.2
  6.7 5.4 %collective-permute-done = bf16[64,2176]{1,0:T(8,128)(2,1)} collective-permute-done((bf16[64,2176]{1,0:T(8,128)(2,1)S(1)}, bf16[64,2176]{1,0:T(8,128)(2,1)}, u32[]{:S(2)}, u32[]{:S(2)}) %collective-permute-start) | collective-permute-done | bytes 278560 | tf_op jit(solution)/shard_map/ppermute | solution.py:22
  12.1 1.2 %collective-permute-done.1 = bf16[64,2176]{1,0:T(8,128)(2,1)} collective-permute-done((bf16[64,2176]{1,0:T(8,128)(2,1)S(1)}, bf16[64,2176]{1,0:T(8,128)(2,1)}, u32[]{:S(2)}, u32[]{:S(2)}) %collective-permute-start.1) | collective-permute-done | bytes 278560 | tf_op jit(solution)/shard_map/ppermute | solution.py:22
  13.2 2.9 %collective-permute-done.2 = bf16[64,2176]{1,0:T(8,128)(2,1)} collective-permute-done((bf16[64,2176]{1,0:T(8,128)(2,1)S(1)}, bf16[64,2176]{1,0:T(8,128)(2,1)}, u32[]{:S(2)}, u32[]{:S(2)}) %collective-permute-start.2) | collective-permute-done | bytes 278560 | tf_op jit(solution)/shard_map/ppermute | solution.py:22
  16.1 1.2 %pad_maximum_fusion = bf16[256,2176]{1,0:T(8,128)(2,1)S(1)} fusion(bf16[64,2176]{1,0:T(8,128)(2,1)} %collective-permute-done.2, bf16[64,2176]{1,0:T(8,128)(2,1)} %collective-permute-done.1, bf16[64,2176]{1,0:T(8,128)(2,1)} %collective-permute-done, bf16[64,2176]{1,0:T(8,128)(2,1)S(1)} %concatenate.14), kind=kLoop, calls=%fused_computation.38 | loop fusion | flops 4456448 | bytes 2228224 | tf_op jit(solution)/shard_map/concatenate | solution.py:40
  17.5 1.7 %collective-permute-start.4 = (bf16[256,2176]{1,0:T(8,128)(2,1)S(1)}, bf16[256,2176]{1,0:T(8,128)(2,1)S(1)}, u32[]{:S(2)}, u32[]{:S(2)}) collective-permute-start(bf16[256,2176]{1,0:T(8,128)(2,1)S(1)} %pad_maximum_fusion), channel_id=1, source_target_pairs={{0,1},{1,2},{2,3},{3,0},{4,5},{5,6},{6,7},{7,4},{8,9},{9,10},{10,1... | collective-permute-start | bytes 3342344 | tf_op jit(solution)/shard_map/ppermute | solution.py:22
  19.2 1.7 %collective-permute-start.3 = (bf16[256,2176]{1,0:T(8,128)(2,1)S(1)}, bf16[256,2176]{1,0:T(8,128)(2,1)S(1)}, u32[]{:S(2)}, u32[]{:S(2)}) collective-permute-start(bf16[256,2176]{1,0:T(8,128)(2,1)S(1)} %pad_maximum_fusion), channel_id=1, source_target_pairs={{0,3},{1,0},{2,1},{3,2},{4,7},{5,4},{6,5},{7,6},{8,11},{9,8},{10,9... | collective-permute-start | bytes 3342344 | tf_op jit(solution)/shard_map/ppermute | solution.py:22
  20.8 13.5 %collective-permute-done.4 = bf16[256,2176]{1,0:T(8,128)(2,1)S(1)} collective-permute-done((bf16[256,2176]{1,0:T(8,128)(2,1)S(1)}, bf16[256,2176]{1,0:T(8,128)(2,1)S(1)}, u32[]{:S(2)}, u32[]{:S(2)}) %collective-permute-start.4) | collective-permute-done | bytes 1114144 | tf_op jit(solution)/shard_map/ppermute | solution.py:22
  34.8 2.9 %collective-permute-start.8 = (bf16[128,2176]{1,0:T(8,128)(2,1)S(1)}, bf16[128,2176]{1,0:T(8,128)(2,1)S(1)}, u32[]{:S(2)}, u32[]{:S(2)}) collective-permute-start(bf16[128,2176]{1,0:T(8,128)(2,1)S(1)} %slice.173), channel_id=1, source_target_pairs={{0,3},{1,0},{2,1},{3,2},{4,7},{5,4},{6,5},{7,6},{8,11},{9,8},{10,9... | collective-permute-start | bytes 1671176 | tf_op jit(solution)/shard_map/ppermute | solution.py:22
  38.0 4.7 %fusion.6 = f32[256,1536]{1,0:T(8,128)S(1)} fusion(bf16[1,2048,1536]{2,1,0:T(8,128)(2,1)} %param.8, bf16[256,2176]{1,0:T(8,128)(2,1)S(1)} %collective-permute-done.3), kind=kOutput, calls=%fused_computation.6 | convolution fusion | flops 1610612736 | bytes 8912896 | tf_op jit(solution)/shard_map/dot_general | solution.py:62
  42.8 1.8 %fusion.2 = f32[256,1536]{1,0:T(8,128)S(1)} fusion(bf16[1,2048,1536]{2,1,0:T(8,128)(2,1)S(1)} %bitcast.57, bf16[256,2176]{1,0:T(8,128)(2,1)S(1)} %collective-permute-done.4), kind=kOutput, calls=%fused_computation.2 | convolution fusion | flops 1610612736 | bytes 8912896 | tf_op jit(solution)/shard_map/dot_general | solution.py:62
  44.6 1.0 %fusion.35 = f32[256,2048]{1,0:T(8,128)S(1)} fusion(bf16[1,768,2048]{2,1,0:T(8,128)(2,1)S(1)} %copy-done, f32[256]{0:T(256)S(1)} %get-tuple-element.11, f32[256,1536]{1,0:T(8,128)S(1)} %fusion.6), kind=kOutput, calls=%fused_computation.25 | convolution fusion | flops 808058880 | bytes 6816768 | tf_op jit(solution)/shard_map/dot_general | solution.py:64
  45.6 1.0 %fusion.44 = f32[256,2048]{1,0:T(8,128)S(1)} fusion(bf16[1,768,2048]{2,1,0:T(8,128)(2,1)S(1)} %copy-done, f32[256]{0:T(256)S(1)} %get-tuple-element.12, f32[256,1536]{1,0:T(8,128)S(1)} %fusion.2), kind=kOutput, calls=%fused_computation.28 | convolution fusion | flops 808058880 | bytes 6816768 | tf_op jit(solution)/shard_map/dot_general | solution.py:64
  46.8 1.0 %fusion.4 = f32[128,1536]{1,0:T(8,128)S(1)} fusion(bf16[1,2048,1536]{2,1,0:T(8,128)(2,1)S(1)} %bitcast.57, bf16[128,2176]{1,0:T(8,128)(2,1)S(1)} %collective-permute-done.5), kind=kOutput, calls=%fused_computation.4 | convolution fusion | flops 805306368 | bytes 7602176 | tf_op jit(solution)/shard_map/dot_general | solution.py:62
  48.0 0.6 fusion.56
  48.9 1.0 %fusion = f32[128,1536]{1,0:T(8,128)S(1)} fusion(bf16[1,2048,1536]{2,1,0:T(8,128)(2,1)S(1)} %bitcast.57, bf16[128,2176]{1,0:T(8,128)(2,1)S(1)} %collective-permute-done.8), kind=kOutput, calls=%fused_computation | convolution fusion | flops 805306368 | bytes 7602176 | tf_op jit(solution)/shard_map/dot_general | solution.py:62
  50.5 3.3 %collective-permute-start.9 = (bf16[128,2048]{1,0:T(8,128)(2,1)S(1)}, bf16[128,2048]{1,0:T(8,128)(2,1)S(1)}, u32[]{:S(2)}, u32[]{:S(2)}) collective-permute-start(bf16[128,2048]{1,0:T(8,128)(2,1)S(1)} %fusion.68), channel_id=1, source_target_pairs={{0,3},{1,0},{2,1},{3,2},{4,7},{5,4},{6,5},{7,6},{8,11},{9,8},{10,9... | collective-permute-start | bytes 1572872 | tf_op jit(solution)/shard_map/ppermute | solution.py:22
  53.8 5.5 %collective-permute-done.6 = bf16[128,2048]{1,0:T(8,128)(2,1)S(1)} collective-permute-done((bf16[128,2048]{1,0:T(8,128)(2,1)S(1)}, bf16[128,2048]{1,0:T(8,128)(2,1)S(1)}, u32[]{:S(2)}, u32[]{:S(2)}) %collective-permute-start.6) | collective-permute-done | bytes 524320 | tf_op jit(solution)/shard_map/ppermute | solution.py:22
  59.5 0.9 %collective-permute-done.9 = bf16[128,2048]{1,0:T(8,128)(2,1)S(1)} collective-permute-done((bf16[128,2048]{1,0:T(8,128)(2,1)S(1)}, bf16[128,2048]{1,0:T(8,128)(2,1)S(1)}, u32[]{:S(2)}, u32[]{:S(2)}) %collective-permute-start.9) | collective-permute-done | bytes 524320 | tf_op jit(solution)/shard_map/ppermute | solution.py:22
  60.7 3.8 %collective-permute-start.10 = (bf16[256,2048]{1,0:T(8,128)(2,1)S(1)}, bf16[256,2048]{1,0:T(8,128)(2,1)S(1)}, u32[]{:S(2)}, u32[]{:S(2)}) collective-permute-start(bf16[256,2048]{1,0:T(8,128)(2,1)S(1)} %pad_maximum_fusion.2), channel_id=1, source_target_pairs={{0,3},{1,0},{2,1},{3,2},{4,7},{5,4},{6,5},{7,6},{8,11},{9,8},{10,9... | collective-permute-start | bytes 3145736 | tf_op jit(solution)/shard_map/ppermute | solution.py:22
  64.4 1.8 %fusion.8 = f32[256,1536]{1,0:T(8,128)S(1)} fusion(bf16[1,2048,1536]{2,1,0:T(8,128)(2,1)S(1)} %bitcast.57, bf16[256,2176]{1,0:T(8,128)(2,1)S(1)} %pad_maximum_fusion), kind=kOutput, calls=%fused_computation.8 | convolution fusion | flops 1610612736 | bytes 8912896 | tf_op jit(solution)/shard_map/dot_general | solution.py:62
  66.2 1.1 %fusion.26 = f32[256,2048]{1,0:T(8,128)S(1)} fusion(bf16[1,768,2048]{2,1,0:T(8,128)(2,1)S(1)} %copy-done, f32[256]{0:T(256)S(1)} %select_reduce_fusion.2, f32[256,1536]{1,0:T(8,128)S(1)} %fusion.8), kind=kOutput, calls=%fused_computation.22 | convolution fusion | flops 808058880 | bytes 6816768 | tf_op jit(solution)/shard_map/dot_general | solution.py:64
  67.3 8.2 %collective-permute-done.7 = bf16[256,2048]{1,0:T(8,128)(2,1)S(1)} collective-permute-done((bf16[256,2048]{1,0:T(8,128)(2,1)S(1)}, bf16[256,2048]{1,0:T(8,128)(2,1)S(1)}, u32[]{:S(2)}, u32[]{:S(2)}) %collective-permute-start.7) | collective-permute-done | bytes 1048608 | tf_op jit(solution)/shard_map/ppermute | solution.py:22
  75.5 5.0 %collective-permute-done.10 = bf16[256,2048]{1,0:T(8,128)(2,1)S(1)} collective-permute-done((bf16[256,2048]{1,0:T(8,128)(2,1)S(1)}, bf16[256,2048]{1,0:T(8,128)(2,1)S(1)}, u32[]{:S(2)}, u32[]{:S(2)}) %collective-permute-start.10) | collective-permute-done | bytes 1048608 | tf_op jit(solution)/shard_map/ppermute | solution.py:22
  81.4 3.1 %collective-permute-start.13 = (bf16[64,2048]{1,0:T(8,128)(2,1)S(1)}, bf16[64,2048]{1,0:T(8,128)(2,1)S(1)}, u32[]{:S(2)}, u32[]{:S(2)}) collective-permute-start(bf16[64,2048]{1,0:T(8,128)(2,1)S(1)} %get-tuple-element.18), channel_id=1, source_target_pairs={{0,12},{1,13},{2,14},{3,15},{4,0},{5,1},{6,2},{7,3},{8,4},{9,5},{1... | collective-permute-start | bytes 786440 | tf_op jit(solution)/shard_map/ppermute | solution.py:22
  84.5 7.2 %collective-permute-done.11 = bf16[64,2048]{1,0:T(8,128)(2,1)S(1)} collective-permute-done((bf16[64,2048]{1,0:T(8,128)(2,1)S(1)}, bf16[64,2048]{1,0:T(8,128)(2,1)S(1)}, u32[]{:S(2)}, u32[]{:S(2)}) %collective-permute-start.11) | collective-permute-done | bytes 262176 | tf_op jit(solution)/shard_map/ppermute | solution.py:22
  91.6 0.9 collective-permute-done.13
  92.5 0.8 fusion.81
  (35 shorter events, 3.6 us)
Async XLA Ops:
  0.0 44.6 %copy-start = (bf16[1,768,2048]{2,1,0:T(8,128)(2,1)S(1)}, bf16[1,768,2048]{2,1,0:T(8,128)(2,1)}, u32[]{:S(2)}) copy-start(bf16[1,768,2048]{2,1,0:T(8,128)(2,1)} %param.9) | copy-start | bytes 9437188
  2.1 9.9 %collective-permute-start = (bf16[64,2176]{1,0:T(8,128)(2,1)S(1)}, bf16[64,2176]{1,0:T(8,128)(2,1)}, u32[]{:S(2)}, u32[]{:S(2)}) collective-permute-start(bf16[64,2176]{1,0:T(8,128)(2,1)S(1)} %concatenate.14), channel_id=1, source_target_pairs={{0,12},{1,13},{2,14},{3,15},{4,0},{5,1},{6,2},{7,3},{8,4},{9,5},{1... | collective-permute-start | bytes 835592 | tf_op jit(solution)/shard_map/ppermute | solution.py:22
  5.0 8.3 %collective-permute-start.1 = (bf16[64,2176]{1,0:T(8,128)(2,1)S(1)}, bf16[64,2176]{1,0:T(8,128)(2,1)}, u32[]{:S(2)}, u32[]{:S(2)}) collective-permute-start(bf16[64,2176]{1,0:T(8,128)(2,1)S(1)} %concatenate.14), channel_id=1, source_target_pairs={{0,8},{1,9},{2,10},{3,11},{4,12},{5,13},{6,14},{7,15},{8,0},{9,1},... | collective-permute-start | bytes 835592 | tf_op jit(solution)/shard_map/ppermute | solution.py:22
  5.8 10.3 %collective-permute-start.2 = (bf16[64,2176]{1,0:T(8,128)(2,1)S(1)}, bf16[64,2176]{1,0:T(8,128)(2,1)}, u32[]{:S(2)}, u32[]{:S(2)}) collective-permute-start(bf16[64,2176]{1,0:T(8,128)(2,1)S(1)} %concatenate.14), channel_id=1, source_target_pairs={{0,4},{1,5},{2,6},{3,7},{4,8},{5,9},{6,10},{7,11},{8,12},{9,13},{1... | collective-permute-start | bytes 835592 | tf_op jit(solution)/shard_map/ppermute | solution.py:22
  17.5 16.8 %collective-permute-start.4 = (bf16[256,2176]{1,0:T(8,128)(2,1)S(1)}, bf16[256,2176]{1,0:T(8,128)(2,1)S(1)}, u32[]{:S(2)}, u32[]{:S(2)}) collective-permute-start(bf16[256,2176]{1,0:T(8,128)(2,1)S(1)} %pad_maximum_fusion), channel_id=1, source_target_pairs={{0,1},{1,2},{2,3},{3,0},{4,5},{5,6},{6,7},{7,4},{8,9},{9,10},{10,1... | collective-permute-start | bytes 3342344 | tf_op jit(solution)/shard_map/ppermute | solution.py:22
  19.2 15.6 %collective-permute-start.3 = (bf16[256,2176]{1,0:T(8,128)(2,1)S(1)}, bf16[256,2176]{1,0:T(8,128)(2,1)S(1)}, u32[]{:S(2)}, u32[]{:S(2)}) collective-permute-start(bf16[256,2176]{1,0:T(8,128)(2,1)S(1)} %pad_maximum_fusion), channel_id=1, source_target_pairs={{0,3},{1,0},{2,1},{3,2},{4,7},{5,4},{6,5},{7,6},{8,11},{9,8},{10,9... | collective-permute-start | bytes 3342344 | tf_op jit(solution)/shard_map/ppermute | solution.py:22
  34.3 12.4 %collective-permute-start.5 = (bf16[128,2176]{1,0:T(8,128)(2,1)S(1)}, bf16[128,2176]{1,0:T(8,128)(2,1)S(1)}, u32[]{:S(2)}, u32[]{:S(2)}) collective-permute-start(bf16[128,2176]{1,0:T(8,128)(2,1)S(1)} %slice.159), channel_id=1, source_target_pairs={{0,1},{1,2},{2,3},{3,0},{4,5},{5,6},{6,7},{7,4},{8,9},{9,10},{10,1... | collective-permute-start | bytes 1671176 | tf_op jit(solution)/shard_map/ppermute | solution.py:22
  34.8 12.9 %collective-permute-start.8 = (bf16[128,2176]{1,0:T(8,128)(2,1)S(1)}, bf16[128,2176]{1,0:T(8,128)(2,1)S(1)}, u32[]{:S(2)}, u32[]{:S(2)}) collective-permute-start(bf16[128,2176]{1,0:T(8,128)(2,1)S(1)} %slice.173), channel_id=1, source_target_pairs={{0,3},{1,0},{2,1},{3,2},{4,7},{5,4},{6,5},{7,6},{8,11},{9,8},{10,9... | collective-permute-start | bytes 1671176 | tf_op jit(solution)/shard_map/ppermute | solution.py:22
  37.8 5.0 %slice-start = ((s8[6291456]{0:T(1024)(128)(4,1)}), s8[4194304]{0:T(1024)(128)(4,1)S(1)}, s32[]{:S(2)}) async-start(s8[6291456]{0:T(1024)(128)(4,1)} %bitcast.56), calls=%async_computation | async-start | bytes 8388608
  38.0 4.7 %slice-start.1 = ((s8[6291456]{0:T(1024)(128)(4,1)}), s8[2097152]{0:T(1024)(128)(4,1)S(1)}, s32[]{:S(2)}) async-start(s8[6291456]{0:T(1024)(128)(4,1)} %bitcast.56), calls=%async_computation.1 | async-start | bytes 4194304
  48.6 10.6 %collective-permute-start.6 = (bf16[128,2048]{1,0:T(8,128)(2,1)S(1)}, bf16[128,2048]{1,0:T(8,128)(2,1)S(1)}, u32[]{:S(2)}, u32[]{:S(2)}) collective-permute-start(bf16[128,2048]{1,0:T(8,128)(2,1)S(1)} %fusion.56), channel_id=1, source_target_pairs={{0,1},{1,2},{2,3},{3,0},{4,5},{5,6},{6,7},{7,4},{8,9},{9,10},{10,1... | collective-permute-start | bytes 1572872 | tf_op jit(solution)/shard_map/ppermute | solution.py:22
  50.5 10.0 %collective-permute-start.9 = (bf16[128,2048]{1,0:T(8,128)(2,1)S(1)}, bf16[128,2048]{1,0:T(8,128)(2,1)S(1)}, u32[]{:S(2)}, u32[]{:S(2)}) collective-permute-start(bf16[128,2048]{1,0:T(8,128)(2,1)S(1)} %fusion.68), channel_id=1, source_target_pairs={{0,3},{1,0},{2,1},{3,2},{4,7},{5,4},{6,5},{7,6},{8,11},{9,8},{10,9... | collective-permute-start | bytes 1572872 | tf_op jit(solution)/shard_map/ppermute | solution.py:22
  59.4 16.1 %collective-permute-start.7 = (bf16[256,2048]{1,0:T(8,128)(2,1)S(1)}, bf16[256,2048]{1,0:T(8,128)(2,1)S(1)}, u32[]{:S(2)}, u32[]{:S(2)}) collective-permute-start(bf16[256,2048]{1,0:T(8,128)(2,1)S(1)} %pad_maximum_fusion.1), channel_id=1, source_target_pairs={{0,1},{1,2},{2,3},{3,0},{4,5},{5,6},{6,7},{7,4},{8,9},{9,10},{10,1... | collective-permute-start | bytes 3145736 | tf_op jit(solution)/shard_map/ppermute | solution.py:22
  60.7 19.8 %collective-permute-start.10 = (bf16[256,2048]{1,0:T(8,128)(2,1)S(1)}, bf16[256,2048]{1,0:T(8,128)(2,1)S(1)}, u32[]{:S(2)}, u32[]{:S(2)}) collective-permute-start(bf16[256,2048]{1,0:T(8,128)(2,1)S(1)} %pad_maximum_fusion.2), channel_id=1, source_target_pairs={{0,3},{1,0},{2,1},{3,2},{4,7},{5,4},{6,5},{7,6},{8,11},{9,8},{10,9... | collective-permute-start | bytes 3145736 | tf_op jit(solution)/shard_map/ppermute | solution.py:22
  81.2 10.5 %collective-permute-start.11 = (bf16[64,2048]{1,0:T(8,128)(2,1)S(1)}, bf16[64,2048]{1,0:T(8,128)(2,1)S(1)}, u32[]{:S(2)}, u32[]{:S(2)}) collective-permute-start(bf16[64,2048]{1,0:T(8,128)(2,1)S(1)} %get-tuple-element.17), channel_id=1, source_target_pairs={{0,4},{1,5},{2,6},{3,7},{4,8},{5,9},{6,10},{7,11},{8,12},{9,13},{1... | collective-permute-start | bytes 786440 | tf_op jit(solution)/shard_map/ppermute | solution.py:22
  81.3 10.4 %collective-permute-start.12 = (bf16[64,2048]{1,0:T(8,128)(2,1)S(1)}, bf16[64,2048]{1,0:T(8,128)(2,1)S(1)}, u32[]{:S(2)}, u32[]{:S(2)}) collective-permute-start(bf16[64,2048]{1,0:T(8,128)(2,1)S(1)} %get-tuple-element.19), channel_id=1, source_target_pairs={{0,8},{1,9},{2,10},{3,11},{4,12},{5,13},{6,14},{7,15},{8,0},{9,1},... | collective-permute-start | bytes 786440 | tf_op jit(solution)/shard_map/ppermute | solution.py:22
  81.4 11.2 %collective-permute-start.13 = (bf16[64,2048]{1,0:T(8,128)(2,1)S(1)}, bf16[64,2048]{1,0:T(8,128)(2,1)S(1)}, u32[]{:S(2)}, u32[]{:S(2)}) collective-permute-start(bf16[64,2048]{1,0:T(8,128)(2,1)S(1)} %get-tuple-element.18), channel_id=1, source_target_pairs={{0,12},{1,13},{2,14},{3,15},{4,0},{5,1},{6,2},{7,3},{8,4},{9,5},{1... | collective-permute-start | bytes 786440 | tf_op jit(solution)/shard_map/ppermute | solution.py:22

commit v5 on v4

--- a/solution.py
+++ b/solution.py
@@ -23,14 +23,16 @@
 
 
 def scatter_ring(own, right, far_a, far_b, left, axis):
+    cut = far_a.shape[0]
     got_a = shift(far_a.astype(jnp.bfloat16), axis, 1)
     got_b = shift(far_b.astype(jnp.bfloat16), axis, -1)
-    cut = far_a.shape[0]
-    to_right = jnp.concatenate([right[:cut] + got_a.astype(jnp.float32), right[cut:]], axis=0)
-    to_left = jnp.concatenate([left[:cut], left[cut:] + got_b.astype(jnp.float32)], axis=0)
-    from_left = shift(to_right.astype(jnp.bfloat16), axis, 1)
-    from_right = shift(to_left.astype(jnp.bfloat16), axis, -1)
-    return own + from_left.astype(jnp.float32) + from_right.astype(jnp.float32)
+    right_early = shift(right[cut:].astype(jnp.bfloat16), axis, 1)
+    left_early = shift(left[:cut].astype(jnp.bfloat16), axis, -1)
+    right_late = shift((right[:cut] + got_a.astype(jnp.float32)).astype(jnp.bfloat16), axis, 1)
+    left_late = shift((left[cut:] + got_b.astype(jnp.float32)).astype(jnp.bfloat16), axis, -1)
+    from_left = jnp.concatenate([right_late, right_early], axis=0).astype(jnp.float32)
+    from_right = jnp.concatenate([left_early, left_late], axis=0).astype(jnp.float32)
+    return own + from_left + from_right
 
 
 def gather_direct(block, stage):
@@ -79,11 +81,15 @@
     payload = jnp.concatenate([hidden_in, high, low, extra], axis=1)
     first = gather_direct(payload, 0)
     first, mine_first = lax.optimization_barrier((first, gate_column(first, me, width)))
-    right = shift(first, 1, -1)
-    left = shift(first, 1, 1)
     cut = first.shape[0] // 2
-    far_a = shift(left[:cut], 1, 1)
-    far_b = shift(right[cut:], 1, -1)
+    right_a = shift(first[:cut], 1, -1)
+    right_b = shift(first[cut:], 1, -1)
+    left_a = shift(first[:cut], 1, 1)
+    left_b = shift(first[cut:], 1, 1)
+    far_a = shift(left_a, 1, 1)
+    far_b = shift(right_b, 1, -1)
+    right = jnp.concatenate([right_a, right_b], axis=0)
+    left = jnp.concatenate([left_a, left_b], axis=0)
     pieces = [expert_rows(first, me, width, w_in[0], w_out[0], mine_first)]
     pieces += [expert_rows(p, me, width, w_in[0], w_out[0]) for p in (right, far_a, far_b, left)]
     stage = scatter_ring(*pieces, 1)

time: 94.2 us -> 91.2 us (0.968)
  the two profiles are of different devices: /device:TPU:64 before, /device:TPU:0 now
where the time goes in v5:
time: 91.2 us
  waiting for transfers between devices  46.5 us (51%)
  starting transfers between devices  26.9 us (29%)
  matrix products  11.9 us (13%)
  other arithmetic  3.87 us (4%)
  local copies, waits for them, and re-layouts  1.72 us (2%)
    ppermute x18, waiting for transfers between devices, shift(): return lax.ppermute(tree, ('dp', 'expert'), pairs)  46.5 us
    ppermute x18, starting transfers between devices, shift(): return lax.ppermute(tree, ('dp', 'expert'), pairs)  26.9 us
    dot_general x5, matrix products, expert_rows(): jnp.dot(rows[:, :width], w_in, preferred_element_type=jnp.float32)  7.31 us
    dot_general x5, matrix products, expert_rows(): jnp.dot(inner, w_out, preferred_element_type=jnp.float32)  4.62 us
  transfers between devices with their start and end apart: 18, of which 14 were waited for; matrix products, arithmetic and copies ran while one was open for 13% of the time, Pallas kernels for 0%

profile of v5, /device:TPU:0, one launch (start us, length us, event | category | flops | bytes accessed | tf_op | source)
XLA Modules:
  0.0 91.2 jit_solution(8651122299868453438)
XLA Ops:
  1.1 1.1 %concatenate.18 = bf16[64,2176]{1,0:T(8,128)(2,1)S(1)} concatenate(bf16[64,2048]{1,0:T(8,128)(2,1)} %param.5, bf16[64,16]{1,0:T(8,128)(2,1)S(1)} %copy.8, bf16[64,16]{1,0:T(8,128)(2,1)S(1)} %copy.9, bf16[64,96]{1,0:T(8,128)(2,1)S(1)} %broadcast_in_dim.66), dimensions={1} | concatenate | bytes 557056 | tf_op jit(solution)/shard_map/concatenate | solution.py:81
  2.2 2.5 %collective-permute-start.1 = (bf16[64,2176]{1,0:T(8,128)(2,1)S(1)}, bf16[64,2176]{1,0:T(8,128)(2,1)}, u32[]{:S(2)}, u32[]{:S(2)}) collective-permute-start(bf16[64,2176]{1,0:T(8,128)(2,1)S(1)} %concatenate.18), channel_id=1, source_target_pairs={{0,8},{1,9},{2,10},{3,11},{4,12},{5,13},{6,14},{7,15},{8,0},{9,1},... | collective-permute-start | bytes 835592 | tf_op jit(solution)/shard_map/ppermute | solution.py:22
  4.7 1.4 %collective-permute-start = (bf16[64,2176]{1,0:T(8,128)(2,1)S(1)}, bf16[64,2176]{1,0:T(8,128)(2,1)}, u32[]{:S(2)}, u32[]{:S(2)}) collective-permute-start(bf16[64,2176]{1,0:T(8,128)(2,1)S(1)} %concatenate.18), channel_id=1, source_target_pairs={{0,12},{1,13},{2,14},{3,15},{4,0},{5,1},{6,2},{7,3},{8,4},{9,5},{1... | collective-permute-start | bytes 835592 | tf_op jit(solution)/shard_map/ppermute | solution.py:22
  6.2 6.9 %collective-permute-done.2 = bf16[64,2176]{1,0:T(8,128)(2,1)} collective-permute-done((bf16[64,2176]{1,0:T(8,128)(2,1)S(1)}, bf16[64,2176]{1,0:T(8,128)(2,1)}, u32[]{:S(2)}, u32[]{:S(2)}) %collective-permute-start.2) | collective-permute-done | bytes 278560 | tf_op jit(solution)/shard_map/ppermute | solution.py:22
  14.0 1.4 %pad_maximum_fusion = bf16[256,2176]{1,0:T(8,128)(2,1)S(1)} fusion(bf16[64,2176]{1,0:T(8,128)(2,1)} %collective-permute-done.2, bf16[64,2176]{1,0:T(8,128)(2,1)} %collective-permute-done.1, bf16[64,2176]{1,0:T(8,128)(2,1)} %collective-permute-done, bf16[64,2176]{1,0:T(8,128)(2,1)S(1)} %concatenate.18), kind=kLoop, calls=%fused_computation.38 | loop fusion | flops 4456448 | bytes 2228224 | tf_op jit(solution)/shard_map/concatenate | solution.py:42
  15.7 3.2 %collective-permute-start.3 = (bf16[128,2176]{1,0:T(8,128)(2,1)S(1)}, bf16[128,2176]{1,0:T(8,128)(2,1)S(1)}, u32[]{:S(2)}, u32[]{:S(2)}) collective-permute-start(bf16[128,2176]{1,0:T(8,128)(2,1)S(1)} %get-tuple-element.16), channel_id=1, source_target_pairs={{0,3},{1,0},{2,1},{3,2},{4,7},{5,4},{6,5},{7,6},{8,11},{9,8},{10,9... | collective-permute-start | bytes 1671176 | tf_op jit(solution)/shard_map/ppermute | solution.py:22
  18.9 3.2 %collective-permute-start.4 = (bf16[128,2176]{1,0:T(8,128)(2,1)S(1)}, bf16[128,2176]{1,0:T(8,128)(2,1)S(1)}, u32[]{:S(2)}, u32[]{:S(2)}) collective-permute-start(bf16[128,2176]{1,0:T(8,128)(2,1)S(1)} %get-tuple-element.15), channel_id=1, source_target_pairs={{0,3},{1,0},{2,1},{3,2},{4,7},{5,4},{6,5},{7,6},{8,11},{9,8},{10,9... | collective-permute-start | bytes 1671176 | tf_op jit(solution)/shard_map/ppermute | solution.py:22
  22.2 4.3 %collective-permute-done.5 = bf16[128,2176]{1,0:T(8,128)(2,1)S(1)} collective-permute-done((bf16[128,2176]{1,0:T(8,128)(2,1)S(1)}, bf16[128,2176]{1,0:T(8,128)(2,1)S(1)}, u32[]{:S(2)}, u32[]{:S(2)}) %collective-permute-start.5) | collective-permute-done | bytes 557088 | tf_op jit(solution)/shard_map/ppermute | solution.py:22
  26.5 5.9 %collective-permute-done.10 = bf16[128,2176]{1,0:T(8,128)(2,1)S(1)} collective-permute-done((bf16[128,2176]{1,0:T(8,128)(2,1)S(1)}, bf16[128,2176]{1,0:T(8,128)(2,1)S(1)}, u32[]{:S(2)}, u32[]{:S(2)}) %collective-permute-start.10) | collective-permute-done | bytes 557088 | tf_op jit(solution)/shard_map/ppermute | solution.py:22
  32.5 1.8 %fusion.2 = f32[256,1536]{1,0:T(8,128)S(1)} fusion(bf16[1,2048,1536]{2,1,0:T(8,128)(2,1)S(1)} %copy-done.1, bf16[256,2176]{1,0:T(8,128)(2,1)S(1)} %constant_dynamic-update-slice_fusion.2), kind=kOutput, calls=%fused_computation.2 | convolution fusion | flops 1610612736 | bytes 8912896 | tf_op jit(solution)/shard_map/dot_general | solution.py:64
  34.3 1.4 %collective-permute-start.12 = (bf16[128,2176]{1,0:T(8,128)(2,1)S(1)}, bf16[128,2176]{1,0:T(8,128)(2,1)S(1)}, u32[]{:S(2)}, u32[]{:S(2)}) collective-permute-start(bf16[128,2176]{1,0:T(8,128)(2,1)S(1)} %collective-permute-done.4), channel_id=1, source_target_pairs={{0,3},{1,0},{2,1},{3,2},{4,7},{5,4},{6,5},{7,6},{8,11},{9,8},{10,9... | collective-permute-start | bytes 1671176 | tf_op jit(solution)/shard_map/ppermute | solution.py:22
  35.7 1.8 %fusion.6 = f32[256,1536]{1,0:T(8,128)S(1)} fusion(bf16[1,2048,1536]{2,1,0:T(8,128)(2,1)S(1)} %copy-done.1, bf16[256,2176]{1,0:T(8,128)(2,1)S(1)} %constant_dynamic-update-slice_fusion), kind=kOutput, calls=%fused_computation.6 | convolution fusion | flops 1610612736 | bytes 8912896 | tf_op jit(solution)/shard_map/dot_general | solution.py:64
  38.5 1.0 %fusion.44 = f32[256,2048]{1,0:T(8,128)S(1)} fusion(bf16[1,768,2048]{2,1,0:T(8,128)(2,1)S(1)} %copy-done, f32[256]{0:T(256)S(1)} %get-tuple-element.11, f32[256,1536]{1,0:T(8,128)S(1)} %fusion.2), kind=kOutput, calls=%fused_computation.28 | convolution fusion | flops 808058880 | bytes 6816768 | tf_op jit(solution)/shard_map/dot_general | solution.py:66
  39.6 2.8 %collective-permute-start.11 = (bf16[128,2048]{1,0:T(8,128)(2,1)S(1)}, bf16[128,2048]{1,0:T(8,128)(2,1)S(1)}, u32[]{:S(2)}, u32[]{:S(2)}) collective-permute-start(bf16[128,2048]{1,0:T(8,128)(2,1)S(1)} %slice.248), channel_id=1, source_target_pairs={{0,3},{1,0},{2,1},{3,2},{4,7},{5,4},{6,5},{7,6},{8,11},{9,8},{10,9... | collective-permute-start | bytes 1572872 | tf_op jit(solution)/shard_map/ppermute | solution.py:22
  42.4 1.5 %collective-permute-done.12 = bf16[128,2176]{1,0:T(8,128)(2,1)S(1)} collective-permute-done((bf16[128,2176]{1,0:T(8,128)(2,1)S(1)}, bf16[128,2176]{1,0:T(8,128)(2,1)S(1)}, u32[]{:S(2)}, u32[]{:S(2)}) %collective-permute-start.12) | collective-permute-done | bytes 557088 | tf_op jit(solution)/shard_map/ppermute | solution.py:22
  43.9 1.0 %fusion = f32[128,1536]{1,0:T(8,128)S(1)} fusion(bf16[1,2048,1536]{2,1,0:T(8,128)(2,1)S(1)} %copy-done.1, bf16[128,2176]{1,0:T(8,128)(2,1)S(1)} %collective-permute-done.12), kind=kOutput, calls=%fused_computation | convolution fusion | flops 805306368 | bytes 7602176 | tf_op jit(solution)/shard_map/dot_general | solution.py:64
  44.9 3.4 %collective-permute-done.6 = bf16[128,2176]{1,0:T(8,128)(2,1)S(1)} collective-permute-done((bf16[128,2176]{1,0:T(8,128)(2,1)S(1)}, bf16[128,2176]{1,0:T(8,128)(2,1)S(1)}, u32[]{:S(2)}, u32[]{:S(2)}) %collective-permute-start.6) | collective-permute-done | bytes 557088 | tf_op jit(solution)/shard_map/ppermute | solution.py:22
  49.2 1.0 %fusion.4 = f32[128,1536]{1,0:T(8,128)S(1)} fusion(bf16[1,2048,1536]{2,1,0:T(8,128)(2,1)S(1)} %copy-done.1, bf16[128,2176]{1,0:T(8,128)(2,1)S(1)} %collective-permute-done.6), kind=kOutput, calls=%fused_computation.4 | convolution fusion | flops 805306368 | bytes 7602176 | tf_op jit(solution)/shard_map/dot_general | solution.py:64
  50.8 2.1 %collective-permute-start.7 = (bf16[128,2048]{1,0:T(8,128)(2,1)S(1)}, bf16[128,2048]{1,0:T(8,128)(2,1)S(1)}, u32[]{:S(2)}, u32[]{:S(2)}) collective-permute-start(bf16[128,2048]{1,0:T(8,128)(2,1)S(1)} %fusion.56), channel_id=1, source_target_pairs={{0,1},{1,2},{2,3},{3,0},{4,5},{5,6},{6,7},{7,4},{8,9},{9,10},{10,1... | collective-permute-start | bytes 1572872 | tf_op jit(solution)/shard_map/ppermute | solution.py:22
  52.9 1.0 %fusion.35 = f32[256,2048]{1,0:T(8,128)S(1)} fusion(bf16[1,768,2048]{2,1,0:T(8,128)(2,1)S(1)} %copy-done, f32[256]{0:T(256)S(1)} %get-tuple-element.12, f32[256,1536]{1,0:T(8,128)S(1)} %fusion.6), kind=kOutput, calls=%fused_computation.25 | convolution fusion | flops 808058880 | bytes 6816768 | tf_op jit(solution)/shard_map/dot_general | solution.py:66
  54.1 4.3 %collective-permute-done.13 = bf16[128,2048]{1,0:T(8,128)(2,1)S(1)} collective-permute-done((bf16[128,2048]{1,0:T(8,128)(2,1)S(1)}, bf16[128,2048]{1,0:T(8,128)(2,1)S(1)}, u32[]{:S(2)}, u32[]{:S(2)}) %collective-permute-start.13) | collective-permute-done | bytes 524320 | tf_op jit(solution)/shard_map/ppermute | solution.py:22
  58.5 1.3 %collective-permute-start.14 = (bf16[128,2048]{1,0:T(8,128)(2,1)S(1)}, bf16[128,2048]{1,0:T(8,128)(2,1)S(1)}, u32[]{:S(2)}, u32[]{:S(2)}) collective-permute-start(bf16[128,2048]{1,0:T(8,128)(2,1)S(1)} %fusion.71), channel_id=1, source_target_pairs={{0,3},{1,0},{2,1},{3,2},{4,7},{5,4},{6,5},{7,6},{8,11},{9,8},{10,9... | collective-permute-start | bytes 1572872 | tf_op jit(solution)/shard_map/ppermute | solution.py:22
  59.8 1.5 %collective-permute-done.7 = bf16[128,2048]{1,0:T(8,128)(2,1)S(1)} collective-permute-done((bf16[128,2048]{1,0:T(8,128)(2,1)S(1)}, bf16[128,2048]{1,0:T(8,128)(2,1)S(1)}, u32[]{:S(2)}, u32[]{:S(2)}) %collective-permute-start.7) | collective-permute-done | bytes 524320 | tf_op jit(solution)/shard_map/ppermute | solution.py:22
  62.3 1.8 %fusion.8 = f32[256,1536]{1,0:T(8,128)S(1)} fusion(bf16[1,2048,1536]{2,1,0:T(8,128)(2,1)S(1)} %copy-done.1, bf16[256,2176]{1,0:T(8,128)(2,1)S(1)} %pad_maximum_fusion), kind=kOutput, calls=%fused_computation.8 | convolution fusion | flops 1610612736 | bytes 8912896 | tf_op jit(solution)/shard_map/dot_general | solution.py:64
  64.1 2.8 %collective-permute-done.9 = bf16[128,2048]{1,0:T(8,128)(2,1)S(1)} collective-permute-done((bf16[128,2048]{1,0:T(8,128)(2,1)S(1)}, bf16[128,2048]{1,0:T(8,128)(2,1)S(1)}, u32[]{:S(2)}, u32[]{:S(2)}) %collective-permute-start.9) | collective-permute-done | bytes 524320 | tf_op jit(solution)/shard_map/ppermute | solution.py:22
  67.7 4.8 %collective-permute-done.8 = bf16[128,2048]{1,0:T(8,128)(2,1)S(1)} collective-permute-done((bf16[128,2048]{1,0:T(8,128)(2,1)S(1)}, bf16[128,2048]{1,0:T(8,128)(2,1)S(1)}, u32[]{:S(2)}, u32[]{:S(2)}) %collective-permute-start.8) | collective-permute-done | bytes 524320 | tf_op jit(solution)/shard_map/ppermute | solution.py:22
  72.5 1.3 %fusion.105 = (bf16[256,2048]{1,0:T(8,128)(2,1)S(1)}, f32[256,2048]{1,0:T(8,128)S(1)}) fusion(bf16[128,2048]{1,0:T(8,128)(2,1)S(1)} %collective-permute-done.14, bf16[128,2048]{1,0:T(8,128)(2,1)S(1)} %collective-permute-done.11, bf16[128,2048]{1,0:T(8,128)(2,1)S(1)} %collective-permute-done.9, bf16[128,2048]{1,0:T(8,128)(2,1)S(1)} %collective-permute-done.8, ...), kind=kOutput, calls=%fused_computation.89 | convolution fusion | flops 813826048 | bytes 9962496 | tf_op jit(solution)/shard_map/dot_general | solution.py:66
  73.9 6.0 %collective-permute-start.17 = (bf16[64,2048]{1,0:T(8,128)(2,1)S(1)}, bf16[64,2048]{1,0:T(8,128)(2,1)S(1)}, u32[]{:S(2)}, u32[]{:S(2)}) collective-permute-start(bf16[64,2048]{1,0:T(8,128)(2,1)S(1)} %get-tuple-element.18), channel_id=1, source_target_pairs={{0,12},{1,13},{2,14},{3,15},{4,0},{5,1},{6,2},{7,3},{8,4},{9,5},{1... | collective-permute-start | bytes 786440 | tf_op jit(solution)/shard_map/ppermute | solution.py:22
  79.9 1.0 %collective-permute-start.15 = (bf16[64,2048]{1,0:T(8,128)(2,1)S(1)}, bf16[64,2048]{1,0:T(8,128)(2,1)S(1)}, u32[]{:S(2)}, u32[]{:S(2)}) collective-permute-start(bf16[64,2048]{1,0:T(8,128)(2,1)S(1)} %get-tuple-element.17), channel_id=1, source_target_pairs={{0,4},{1,5},{2,6},{3,7},{4,8},{5,9},{6,10},{7,11},{8,12},{9,13},{1... | collective-permute-start | bytes 786440 | tf_op jit(solution)/shard_map/ppermute | solution.py:22
  80.9 5.7 %collective-permute-done.17 = bf16[64,2048]{1,0:T(8,128)(2,1)S(1)} collective-permute-done((bf16[64,2048]{1,0:T(8,128)(2,1)S(1)}, bf16[64,2048]{1,0:T(8,128)(2,1)S(1)}, u32[]{:S(2)}, u32[]{:S(2)}) %collective-permute-start.17) | collective-permute-done | bytes 262176 | tf_op jit(solution)/shard_map/ppermute | solution.py:22
  86.6 1.3 %collective-permute-done.16 = bf16[64,2048]{1,0:T(8,128)(2,1)S(1)} collective-permute-done((bf16[64,2048]{1,0:T(8,128)(2,1)S(1)}, bf16[64,2048]{1,0:T(8,128)(2,1)S(1)}, u32[]{:S(2)}, u32[]{:S(2)}) %collective-permute-start.16) | collective-permute-done | bytes 262176 | tf_op jit(solution)/shard_map/ppermute | solution.py:22
  87.9 2.4 %collective-permute-done.15 = bf16[64,2048]{1,0:T(8,128)(2,1)S(1)} collective-permute-done((bf16[64,2048]{1,0:T(8,128)(2,1)S(1)}, bf16[64,2048]{1,0:T(8,128)(2,1)S(1)}, u32[]{:S(2)}, u32[]{:S(2)}) %collective-permute-start.15) | collective-permute-done | bytes 262176 | tf_op jit(solution)/shard_map/ppermute | solution.py:22
  (40 shorter events, 8.2 us)
Async XLA Ops:
  0.0 38.5 %copy-start = (bf16[1,768,2048]{2,1,0:T(8,128)(2,1)S(1)}, bf16[1,768,2048]{2,1,0:T(8,128)(2,1)}, u32[]{:S(2)}) copy-start(bf16[1,768,2048]{2,1,0:T(8,128)(2,1)} %param.9) | copy-start | bytes 9437188
  2.1 10.9 %collective-permute-start.2 = (bf16[64,2176]{1,0:T(8,128)(2,1)S(1)}, bf16[64,2176]{1,0:T(8,128)(2,1)}, u32[]{:S(2)}, u32[]{:S(2)}) collective-permute-start(bf16[64,2176]{1,0:T(8,128)(2,1)S(1)} %concatenate.18), channel_id=1, source_target_pairs={{0,4},{1,5},{2,6},{3,7},{4,8},{5,9},{6,10},{7,11},{8,12},{9,13},{1... | collective-permute-start | bytes 835592 | tf_op jit(solution)/shard_map/ppermute | solution.py:22
  2.2 10.8 %collective-permute-start.1 = (bf16[64,2176]{1,0:T(8,128)(2,1)S(1)}, bf16[64,2176]{1,0:T(8,128)(2,1)}, u32[]{:S(2)}, u32[]{:S(2)}) collective-permute-start(bf16[64,2176]{1,0:T(8,128)(2,1)S(1)} %concatenate.18), channel_id=1, source_target_pairs={{0,8},{1,9},{2,10},{3,11},{4,12},{5,13},{6,14},{7,15},{8,0},{9,1},... | collective-permute-start | bytes 835592 | tf_op jit(solution)/shard_map/ppermute | solution.py:22
  4.7 9.2 %collective-permute-start = (bf16[64,2176]{1,0:T(8,128)(2,1)S(1)}, bf16[64,2176]{1,0:T(8,128)(2,1)}, u32[]{:S(2)}, u32[]{:S(2)}) collective-permute-start(bf16[64,2176]{1,0:T(8,128)(2,1)S(1)} %concatenate.18), channel_id=1, source_target_pairs={{0,12},{1,13},{2,14},{3,15},{4,0},{5,1},{6,2},{7,3},{8,4},{9,5},{1... | collective-permute-start | bytes 835592 | tf_op jit(solution)/shard_map/ppermute | solution.py:22
  14.0 18.5 %copy-start.1 = (bf16[1,2048,1536]{2,1,0:T(8,128)(2,1)S(1)}, bf16[1,2048,1536]{2,1,0:T(8,128)(2,1)}, u32[]{:S(2)}) copy-start(bf16[1,2048,1536]{2,1,0:T(8,128)(2,1)} %param.8) | copy-start | bytes 18874372
  15.6 10.8 %collective-permute-start.5 = (bf16[128,2176]{1,0:T(8,128)(2,1)S(1)}, bf16[128,2176]{1,0:T(8,128)(2,1)S(1)}, u32[]{:S(2)}, u32[]{:S(2)}) collective-permute-start(bf16[128,2176]{1,0:T(8,128)(2,1)S(1)} %get-tuple-element.16), channel_id=1, source_target_pairs={{0,1},{1,2},{2,3},{3,0},{4,5},{5,6},{6,7},{7,4},{8,9},{9,10},{10,1... | collective-permute-start | bytes 1671176 | tf_op jit(solution)/shard_map/ppermute | solution.py:22
  15.7 10.8 %collective-permute-start.3 = (bf16[128,2176]{1,0:T(8,128)(2,1)S(1)}, bf16[128,2176]{1,0:T(8,128)(2,1)S(1)}, u32[]{:S(2)}, u32[]{:S(2)}) collective-permute-start(bf16[128,2176]{1,0:T(8,128)(2,1)S(1)} %get-tuple-element.16), channel_id=1, source_target_pairs={{0,3},{1,0},{2,1},{3,2},{4,7},{5,4},{6,5},{7,6},{8,11},{9,8},{10,9... | collective-permute-start | bytes 1671176 | tf_op jit(solution)/shard_map/ppermute | solution.py:22
  18.9 13.5 %collective-permute-start.10 = (bf16[128,2176]{1,0:T(8,128)(2,1)S(1)}, bf16[128,2176]{1,0:T(8,128)(2,1)S(1)}, u32[]{:S(2)}, u32[]{:S(2)}) collective-permute-start(bf16[128,2176]{1,0:T(8,128)(2,1)S(1)} %get-tuple-element.15), channel_id=1, source_target_pairs={{0,1},{1,2},{2,3},{3,0},{4,5},{5,6},{6,7},{7,4},{8,9},{9,10},{10,1... | collective-permute-start | bytes 1671176 | tf_op jit(solution)/shard_map/ppermute | solution.py:22
  18.9 15.3 %collective-permute-start.4 = (bf16[128,2176]{1,0:T(8,128)(2,1)S(1)}, bf16[128,2176]{1,0:T(8,128)(2,1)S(1)}, u32[]{:S(2)}, u32[]{:S(2)}) collective-permute-start(bf16[128,2176]{1,0:T(8,128)(2,1)S(1)} %get-tuple-element.15), channel_id=1, source_target_pairs={{0,3},{1,0},{2,1},{3,2},{4,7},{5,4},{6,5},{7,6},{8,11},{9,8},{10,9... | collective-permute-start | bytes 1671176 | tf_op jit(solution)/shard_map/ppermute | solution.py:22
  34.3 9.6 %collective-permute-start.12 = (bf16[128,2176]{1,0:T(8,128)(2,1)S(1)}, bf16[128,2176]{1,0:T(8,128)(2,1)S(1)}, u32[]{:S(2)}, u32[]{:S(2)}) collective-permute-start(bf16[128,2176]{1,0:T(8,128)(2,1)S(1)} %collective-permute-done.4), channel_id=1, source_target_pairs={{0,3},{1,0},{2,1},{3,2},{4,7},{5,4},{6,5},{7,6},{8,11},{9,8},{10,9... | collective-permute-start | bytes 1671176 | tf_op jit(solution)/shard_map/ppermute | solution.py:22
  37.5 10.8 %collective-permute-start.6 = (bf16[128,2176]{1,0:T(8,128)(2,1)S(1)}, bf16[128,2176]{1,0:T(8,128)(2,1)S(1)}, u32[]{:S(2)}, u32[]{:S(2)}) collective-permute-start(bf16[128,2176]{1,0:T(8,128)(2,1)S(1)} %collective-permute-done.5), channel_id=1, source_target_pairs={{0,1},{1,2},{2,3},{3,0},{4,5},{5,6},{6,7},{7,4},{8,9},{9,10},{10,1... | collective-permute-start | bytes 1671176 | tf_op jit(solution)/shard_map/ppermute | solution.py:22
  39.6 24.4 %collective-permute-start.11 = (bf16[128,2048]{1,0:T(8,128)(2,1)S(1)}, bf16[128,2048]{1,0:T(8,128)(2,1)S(1)}, u32[]{:S(2)}, u32[]{:S(2)}) collective-permute-start(bf16[128,2048]{1,0:T(8,128)(2,1)S(1)} %slice.248), channel_id=1, source_target_pairs={{0,3},{1,0},{2,1},{3,2},{4,7},{5,4},{6,5},{7,6},{8,11},{9,8},{10,9... | collective-permute-start | bytes 1572872 | tf_op jit(solution)/shard_map/ppermute | solution.py:22
  49.1 9.3 %collective-permute-start.13 = (bf16[128,2048]{1,0:T(8,128)(2,1)S(1)}, bf16[128,2048]{1,0:T(8,128)(2,1)S(1)}, u32[]{:S(2)}, u32[]{:S(2)}) collective-permute-start(bf16[128,2048]{1,0:T(8,128)(2,1)S(1)} %fusion.68), channel_id=1, source_target_pairs={{0,3},{1,0},{2,1},{3,2},{4,7},{5,4},{6,5},{7,6},{8,11},{9,8},{10,9... | collective-permute-start | bytes 1572872 | tf_op jit(solution)/shard_map/ppermute | solution.py:22
  50.8 10.5 %collective-permute-start.7 = (bf16[128,2048]{1,0:T(8,128)(2,1)S(1)}, bf16[128,2048]{1,0:T(8,128)(2,1)S(1)}, u32[]{:S(2)}, u32[]{:S(2)}) collective-permute-start(bf16[128,2048]{1,0:T(8,128)(2,1)S(1)} %fusion.56), channel_id=1, source_target_pairs={{0,1},{1,2},{2,3},{3,0},{4,5},{5,6},{6,7},{7,4},{8,9},{9,10},{10,1... | collective-permute-start | bytes 1572872 | tf_op jit(solution)/shard_map/ppermute | solution.py:22
  54.0 12.9 %collective-permute-start.9 = (bf16[128,2048]{1,0:T(8,128)(2,1)S(1)}, bf16[128,2048]{1,0:T(8,128)(2,1)S(1)}, u32[]{:S(2)}, u32[]{:S(2)}) collective-permute-start(bf16[128,2048]{1,0:T(8,128)(2,1)S(1)} %slice.249), channel_id=1, source_target_pairs={{0,1},{1,2},{2,3},{3,0},{4,5},{5,6},{6,7},{7,4},{8,9},{9,10},{10,1... | collective-permute-start | bytes 1572872 | tf_op jit(solution)/shard_map/ppermute | solution.py:22
  58.5 9.3 %collective-permute-start.14 = (bf16[128,2048]{1,0:T(8,128)(2,1)S(1)}, bf16[128,2048]{1,0:T(8,128)(2,1)S(1)}, u32[]{:S(2)}, u32[]{:S(2)}) collective-permute-start(bf16[128,2048]{1,0:T(8,128)(2,1)S(1)} %fusion.71), channel_id=1, source_target_pairs={{0,3},{1,0},{2,1},{3,2},{4,7},{5,4},{6,5},{7,6},{8,11},{9,8},{10,9... | collective-permute-start | bytes 1572872 | tf_op jit(solution)/shard_map/ppermute | solution.py:22
  61.4 11.1 %collective-permute-start.8 = (bf16[128,2048]{1,0:T(8,128)(2,1)S(1)}, bf16[128,2048]{1,0:T(8,128)(2,1)S(1)}, u32[]{:S(2)}, u32[]{:S(2)}) collective-permute-start(bf16[128,2048]{1,0:T(8,128)(2,1)S(1)} %fusion.73), channel_id=1, source_target_pairs={{0,1},{1,2},{2,3},{3,0},{4,5},{5,6},{6,7},{7,4},{8,9},{9,10},{10,1... | collective-permute-start | bytes 1572872 | tf_op jit(solution)/shard_map/ppermute | solution.py:22
  73.9 12.7 %collective-permute-start.17 = (bf16[64,2048]{1,0:T(8,128)(2,1)S(1)}, bf16[64,2048]{1,0:T(8,128)(2,1)S(1)}, u32[]{:S(2)}, u32[]{:S(2)}) collective-permute-start(bf16[64,2048]{1,0:T(8,128)(2,1)S(1)} %get-tuple-element.18), channel_id=1, source_target_pairs={{0,12},{1,13},{2,14},{3,15},{4,0},{5,1},{6,2},{7,3},{8,4},{9,5},{1... | collective-permute-start | bytes 786440 | tf_op jit(solution)/shard_map/ppermute | solution.py:22
  79.9 8.0 %collective-permute-start.16 = (bf16[64,2048]{1,0:T(8,128)(2,1)S(1)}, bf16[64,2048]{1,0:T(8,128)(2,1)S(1)}, u32[]{:S(2)}, u32[]{:S(2)}) collective-permute-start(bf16[64,2048]{1,0:T(8,128)(2,1)S(1)} %get-tuple-element.19), channel_id=1, source_target_pairs={{0,8},{1,9},{2,10},{3,11},{4,12},{5,13},{6,14},{7,15},{8,0},{9,1},... | collective-permute-start | bytes 786440 | tf_op jit(solution)/shard_map/ppermute | solution.py:22
  79.9 10.4 %collective-permute-start.15 = (bf16[64,2048]{1,0:T(8,128)(2,1)S(1)}, bf16[64,2048]{1,0:T(8,128)(2,1)S(1)}, u32[]{:S(2)}, u32[]{:S(2)}) collective-permute-start(bf16[64,2048]{1,0:T(8,128)(2,1)S(1)} %get-tuple-element.17), channel_id=1, source_target_pairs={{0,4},{1,5},{2,6},{3,7},{4,8},{5,9},{6,10},{7,11},{8,12},{9,13},{1... | collective-permute-start | bytes 786440 | tf_op jit(solution)/shard_map/ppermute | solution.py:22

commit v6 on v5

--- a/solution.py
+++ b/solution.py
@@ -24,8 +24,8 @@
 
 def scatter_ring(own, right, far_a, far_b, left, axis):
     cut = far_a.shape[0]
-    got_a = shift(far_a.astype(jnp.bfloat16), axis, 1)
-    got_b = shift(far_b.astype(jnp.bfloat16), axis, -1)
+    got_a = shift_two(far_a.astype(jnp.bfloat16), axis, 1)
+    got_b = shift_two(far_b.astype(jnp.bfloat16), axis, -1)
     right_early = shift(right[cut:].astype(jnp.bfloat16), axis, 1)
     left_early = shift(left[:cut].astype(jnp.bfloat16), axis, -1)
     right_late = shift((right[:cut] + got_a.astype(jnp.float32)).astype(jnp.bfloat16), axis, 1)
@@ -35,11 +35,9 @@
     return own + from_left + from_right
 
 
-def gather_direct(block, stage):
-    right = shift(block, stage, -1)
-    far = shift(block, stage, 2)
-    left = shift(block, stage, 1)
-    return jnp.concatenate([block, right, far, left], axis=0)
+def shift_two(block, stage, step):
+    cut = block.shape[0] // 2
+    return jnp.concatenate([shift(block[:cut], stage, step), shift(block[cut:], stage, step)], axis=0)
 
 
 def scatter_direct(parts, stage):
@@ -55,6 +53,14 @@
     high = rows[:, width:width + count].astype(jnp.float32)
     low = rows[:, width + count:width + 2 * count].astype(jnp.float32)
     return jnp.sum(jnp.where(experts[None, :] == me, high + low, jnp.float32(0.0)), axis=1)
+
+
+def gate_column_dot(rows, me, width):
+    count = SIDE * SIDE
+    pick = (jnp.arange(count, dtype=jnp.int32) == me).astype(jnp.float32)
+    high = rows[:, width:width + count].astype(jnp.float32)
+    low = rows[:, width + count:width + 2 * count].astype(jnp.float32)
+    return jnp.dot(high + low, pick, precision=lax.Precision.HIGHEST)
 
 
 def expert_rows(rows, me, width, w_in, w_out, mine=None):
@@ -79,18 +85,24 @@
     low = (table - high.astype(jnp.float32)).astype(jnp.bfloat16)
     extra = jnp.zeros((count, PAD - 2 * SIDE * SIDE), jnp.bfloat16)
     payload = jnp.concatenate([hidden_in, high, low, extra], axis=1)
-    first = gather_direct(payload, 0)
-    first, mine_first = lax.optimization_barrier((first, gate_column(first, me, width)))
-    cut = first.shape[0] // 2
-    right_a = shift(first[:cut], 1, -1)
-    right_b = shift(first[cut:], 1, -1)
-    left_a = shift(first[:cut], 1, 1)
-    left_b = shift(first[cut:], 1, 1)
+    right_one = shift(payload, 0, -1)
+    far_one = shift(payload, 0, 2)
+    left_one = shift(payload, 0, 1)
+    first_a = jnp.concatenate([payload, right_one], axis=0)
+    first_b = jnp.concatenate([far_one, left_one], axis=0)
+    first_a, mine_a = lax.optimization_barrier((first_a, gate_column(first_a, me, width)))
+    first_b, mine_b = lax.optimization_barrier((first_b, gate_column_dot(first_b, me, width)))
+    right_a = shift(first_a, 1, -1)
+    right_b = shift(first_b, 1, -1)
+    left_a = shift(first_a, 1, 1)
+    left_b = shift(first_b, 1, 1)
     far_a = shift(left_a, 1, 1)
     far_b = shift(right_b, 1, -1)
     right = jnp.concatenate([right_a, right_b], axis=0)
     left = jnp.concatenate([left_a, left_b], axis=0)
-    pieces = [expert_rows(first, me, width, w_in[0], w_out[0], mine_first)]
+    own_a = expert_rows(first_a, me, width, w_in[0], w_out[0], mine_a)
+    own_b = expert_rows(first_b, me, width, w_in[0], w_out[0], mine_b)
+    pieces = [jnp.concatenate([own_a, own_b], axis=0)]
     pieces += [expert_rows(p, me, width, w_in[0], w_out[0]) for p in (right, far_a, far_b, left)]
     stage = scatter_ring(*pieces, 1)
     return scatter_direct(stage.reshape(SIDE, count, width), 0).astype(jnp.bfloat16)
@@ -104,6 +116,4 @@
         P("expert", None, None),
         P("expert", None, None),
     )
-    return jax.shard_map(
-        layer, mesh=mesh, in_specs=placed, out_specs=P(("dp", "expert"), None), check_vma=False
-    )
+    return jax.shard_map(layer, mesh=mesh, in_specs=placed, out_specs=P(("dp", "expert"), None), check_vma=False)

time: 91.2 us -> 91.8 us (level)
  the two profiles are of different devices: /device:TPU:0 before, /device:TPU:64 now
where the time goes in v6:
time: 91.8 us; the launch traced here: 90.8 us
  starting transfers between devices  33.5 us (36%)
  waiting for transfers between devices  33.5 us (36%)
  matrix products  15 us (16%)
  other arithmetic  4.9 us (5%)
  local copies, waits for them, and re-layouts  3.68 us (4%)
    ppermute x20, waiting for transfers between devices, shift(): return lax.ppermute(tree, ('dp', 'expert'), pairs)  33.5 us
    ppermute x20, starting transfers between devices, shift(): return lax.ppermute(tree, ('dp', 'expert'), pairs)  33.5 us
    dot_general x6, matrix products, expert_rows(): jnp.dot(rows[:, :width], w_in, preferred_element_type=jnp.float32)  10.3 us
    dot_general x6, matrix products, expert_rows(): jnp.dot(inner, w_out, preferred_element_type=jnp.float32)  4.5 us
  transfers between devices with their start and end apart: 20, of which 14 were waited for; matrix products, arithmetic and copies ran while one was open for 20% of the time, Pallas kernels for 0%

profile of v6, /device:TPU:64, one launch (start us, length us, event | category | flops | bytes accessed | tf_op | source)
XLA Modules:
  0.0 90.8 jit_solution(10111541720063142748)
XLA Ops:
  1.1 1.1 %concatenate.30 = bf16[64,2176]{1,0:T(8,128)(2,1)S(1)} concatenate(bf16[64,2048]{1,0:T(8,128)(2,1)} %param.5, bf16[64,16]{1,0:T(8,128)(2,1)S(1)} %copy.8, bf16[64,16]{1,0:T(8,128)(2,1)S(1)} %copy.9, bf16[64,96]{1,0:T(8,128)(2,1)S(1)} %broadcast_in_dim.67), dimensions={1} | concatenate | bytes 557056 | tf_op jit(solution)/shard_map/concatenate | solution.py:87
  2.1 2.8 %collective-permute-start = (bf16[64,2176]{1,0:T(8,128)(2,1)S(1)}, bf16[64,2176]{1,0:T(8,128)(2,1)}, u32[]{:S(2)}, u32[]{:S(2)}) collective-permute-start(bf16[64,2176]{1,0:T(8,128)(2,1)S(1)} %concatenate.30), channel_id=1, source_target_pairs={{0,12},{1,13},{2,14},{3,15},{4,0},{5,1},{6,2},{7,3},{8,4},{9,5},{1... | collective-permute-start | bytes 835592 | tf_op jit(solution)/shard_map/ppermute | solution.py:22
  6.7 5.4 %collective-permute-done = bf16[64,2176]{1,0:T(8,128)(2,1)} collective-permute-done((bf16[64,2176]{1,0:T(8,128)(2,1)S(1)}, bf16[64,2176]{1,0:T(8,128)(2,1)}, u32[]{:S(2)}, u32[]{:S(2)}) %collective-permute-start) | collective-permute-done | bytes 278560 | tf_op jit(solution)/shard_map/ppermute | solution.py:22
  13.0 1.0 %pad_maximum_fusion = bf16[128,2176]{1,0:T(8,128)(2,1)S(1)} fusion(bf16[64,2176]{1,0:T(8,128)(2,1)} %collective-permute-done, bf16[64,2176]{1,0:T(8,128)(2,1)S(1)} %concatenate.30), kind=kLoop, calls=%fused_computation.60 | loop fusion | flops 1114112 | bytes 1114112 | tf_op jit(solution)/shard_map/concatenate | solution.py:91
  14.0 3.1 %collective-permute-start.3 = (bf16[128,2176]{1,0:T(8,128)(2,1)S(1)}, bf16[128,2176]{1,0:T(8,128)(2,1)S(1)}, u32[]{:S(2)}, u32[]{:S(2)}) collective-permute-start(bf16[128,2176]{1,0:T(8,128)(2,1)S(1)} %pad_maximum_fusion), channel_id=1, source_target_pairs={{0,3},{1,0},{2,1},{3,2},{4,7},{5,4},{6,5},{7,6},{8,11},{9,8},{10,9... | collective-permute-start | bytes 1671176 | tf_op jit(solution)/shard_map/ppermute | solution.py:22
  17.1 1.0 %constant_dynamic-update-slice_fusion.1 = bf16[128,2176]{1,0:T(8,128)(2,1)S(1)} fusion(bf16[64,2176]{1,0:T(8,128)(2,1)} %collective-permute-done.1), kind=kLoop, calls=%fused_computation.101 | loop fusion | bytes 557056
  18.1 1.0 %constant_dynamic-update-slice_fusion = bf16[128,2176]{1,0:T(8,128)(2,1)S(1)} fusion(bf16[128,2176]{1,0:T(8,128)(2,1)S(1)} %constant_dynamic-update-slice_fusion.1, bf16[64,2176]{1,0:T(8,128)(2,1)} %collective-permute-done.2), kind=kLoop, calls=%fused_computation.100 | loop fusion | bytes 557056 | tf_op jit(solution)/shard_map/concatenate | solution.py:92
  19.3 3.3 %collective-permute-start.4 = (bf16[128,2176]{1,0:T(8,128)(2,1)S(1)}, bf16[128,2176]{1,0:T(8,128)(2,1)S(1)}, u32[]{:S(2)}, u32[]{:S(2)}) collective-permute-start(bf16[128,2176]{1,0:T(8,128)(2,1)S(1)} %constant_dynamic-update-slice_fusion), channel_id=1, source_target_pairs={{0,3},{1,0},{2,1},{3,2},{4,7},{5,4},{6,5},{7,6},{8,11},{9,8},{10,9... | collective-permute-start | bytes 1671176 | tf_op jit(solution)/shard_map/ppermute | solution.py:22
  22.6 3.8 %fusion.10 = f32[128,1536]{1,0:T(8,128)S(1)} fusion(bf16[1,2048,1536]{2,1,0:T(8,128)(2,1)} %param.8, bf16[128,2176]{1,0:T(8,128)(2,1)S(1)} %pad_maximum_fusion), kind=kOutput, calls=%fused_computation.10 | convolution fusion | flops 805306368 | bytes 7602176 | tf_op jit(solution)/shard_map/dot_general | solution.py:70
  26.4 1.0 %fusion.8 = f32[128,1536]{1,0:T(8,128)S(1)} fusion(bf16[1,2048,1536]{2,1,0:T(8,128)(2,1)S(1)} %copy-done.1, bf16[128,2176]{1,0:T(8,128)(2,1)S(1)} %constant_dynamic-update-slice_fusion), kind=kOutput, calls=%fused_computation.8 | convolution fusion | flops 805306368 | bytes 7602176 | tf_op jit(solution)/shard_map/dot_general | solution.py:70
  27.9 2.2 %collective-permute-done.4 = bf16[128,2176]{1,0:T(8,128)(2,1)S(1)} collective-permute-done((bf16[128,2176]{1,0:T(8,128)(2,1)S(1)}, bf16[128,2176]{1,0:T(8,128)(2,1)S(1)}, u32[]{:S(2)}, u32[]{:S(2)}) %collective-permute-start.4) | collective-permute-done | bytes 557088 | tf_op jit(solution)/shard_map/ppermute | solution.py:22
  30.2 1.8 %fusion.6 = f32[256,1536]{1,0:T(8,128)S(1)} fusion(bf16[1,2048,1536]{2,1,0:T(8,128)(2,1)S(1)} %copy-done.1, bf16[256,2176]{1,0:T(8,128)(2,1)S(1)} %constant_dynamic-update-slice_fusion.2), kind=kOutput, calls=%fused_computation.6 | convolution fusion | flops 1610612736 | bytes 8912896 | tf_op jit(solution)/shard_map/dot_general | solution.py:70
  32.0 1.8 %collective-permute-done.11 = bf16[128,2176]{1,0:T(8,128)(2,1)S(1)} collective-permute-done((bf16[128,2176]{1,0:T(8,128)(2,1)S(1)}, bf16[128,2176]{1,0:T(8,128)(2,1)S(1)}, u32[]{:S(2)}, u32[]{:S(2)}) %collective-permute-start.11) | collective-permute-done | bytes 557088 | tf_op jit(solution)/shard_map/ppermute | solution.py:22
  34.1 1.8 %fusion.2 = f32[256,1536]{1,0:T(8,128)S(1)} fusion(bf16[1,2048,1536]{2,1,0:T(8,128)(2,1)S(1)} %copy-done.1, bf16[256,2176]{1,0:T(8,128)(2,1)S(1)} %constant_dynamic-update-slice_fusion.4), kind=kOutput, calls=%fused_computation.2 | convolution fusion | flops 1610612736 | bytes 8912896 | tf_op jit(solution)/shard_map/dot_general | solution.py:70
  36.0 1.0 %fusion.30 = f32[256,2048]{1,0:T(8,128)S(1)} fusion(bf16[1,768,2048]{2,1,0:T(8,128)(2,1)S(1)} %copy-done, f32[256]{0:T(256)S(1)} %get-tuple-element.16, f32[256,1536]{1,0:T(8,128)S(1)} %fusion.6), kind=kOutput, calls=%fused_computation.26 | convolution fusion | flops 808058880 | bytes 6816768 | tf_op jit(solution)/shard_map/dot_general | solution.py:72
  38.0 2.7 %collective-permute-start.13 = (bf16[128,2176]{1,0:T(8,128)(2,1)S(1)}, bf16[128,2176]{1,0:T(8,128)(2,1)S(1)}, u32[]{:S(2)}, u32[]{:S(2)}) collective-permute-start(bf16[128,2176]{1,0:T(8,128)(2,1)S(1)} %collective-permute-done.4), channel_id=1, source_target_pairs={{0,3},{1,0},{2,1},{3,2},{4,7},{5,4},{6,5},{7,6},{8,11},{9,8},{10,9... | collective-permute-start | bytes 1671176 | tf_op jit(solution)/shard_map/ppermute | solution.py:22
  40.7 1.0 %fusion.39 = f32[256,2048]{1,0:T(8,128)S(1)} fusion(bf16[1,768,2048]{2,1,0:T(8,128)(2,1)S(1)} %copy-done, f32[256]{0:T(256)S(1)} %get-tuple-element.15, f32[256,1536]{1,0:T(8,128)S(1)} %fusion.2), kind=kOutput, calls=%fused_computation.29 | convolution fusion | flops 808058880 | bytes 6816768 | tf_op jit(solution)/shard_map/dot_general | solution.py:72
  41.8 1.8 %collective-permute-start.12 = (bf16[128,2048]{1,0:T(8,128)(2,1)S(1)}, bf16[128,2048]{1,0:T(8,128)(2,1)S(1)}, u32[]{:S(2)}, u32[]{:S(2)}) collective-permute-start(bf16[128,2048]{1,0:T(8,128)(2,1)S(1)} %slice.322), channel_id=1, source_target_pairs={{0,3},{1,0},{2,1},{3,2},{4,7},{5,4},{6,5},{7,6},{8,11},{9,8},{10,9... | collective-permute-start | bytes 1572872 | tf_op jit(solution)/shard_map/ppermute | solution.py:22
  43.6 3.1 %collective-permute-done.6 = bf16[128,2176]{1,0:T(8,128)(2,1)S(1)} collective-permute-done((bf16[128,2176]{1,0:T(8,128)(2,1)S(1)}, bf16[128,2176]{1,0:T(8,128)(2,1)S(1)}, u32[]{:S(2)}, u32[]{:S(2)}) %collective-permute-start.6) | collective-permute-done | bytes 557088 | tf_op jit(solution)/shard_map/ppermute | solution.py:22
  46.8 1.0 %fusion.4 = f32[128,1536]{1,0:T(8,128)S(1)} fusion(bf16[1,2048,1536]{2,1,0:T(8,128)(2,1)S(1)} %copy-done.1, bf16[128,2176]{1,0:T(8,128)(2,1)S(1)} %collective-permute-done.6), kind=kOutput, calls=%fused_computation.4 | convolution fusion | flops 805306368 | bytes 7602176 | tf_op jit(solution)/shard_map/dot_general | solution.py:70
  48.8 2.1 %collective-permute-start.7 = (bf16[64,2048]{1,0:T(8,128)(2,1)S(1)}, bf16[64,2048]{1,0:T(8,128)(2,1)S(1)}, u32[]{:S(2)}, u32[]{:S(2)}) collective-permute-start(bf16[64,2048]{1,0:T(8,128)(2,1)S(1)} %get-tuple-element.24), channel_id=1, source_target_pairs={{0,1},{1,2},{2,3},{3,0},{4,5},{5,6},{6,7},{7,4},{8,9},{9,10},{10,1... | collective-permute-start | bytes 786440 | tf_op jit(solution)/shard_map/ppermute | solution.py:22
  50.9 1.4 %collective-permute-start.8 = (bf16[64,2048]{1,0:T(8,128)(2,1)S(1)}, bf16[64,2048]{1,0:T(8,128)(2,1)S(1)}, u32[]{:S(2)}, u32[]{:S(2)}) collective-permute-start(bf16[64,2048]{1,0:T(8,128)(2,1)S(1)} %get-tuple-element.25), channel_id=1, source_target_pairs={{0,1},{1,2},{2,3},{3,0},{4,5},{5,6},{6,7},{7,4},{8,9},{9,10},{10,1... | collective-permute-start | bytes 786440 | tf_op jit(solution)/shard_map/ppermute | solution.py:22
  52.3 1.0 %fusion = f32[128,1536]{1,0:T(8,128)S(1)} fusion(bf16[1,2048,1536]{2,1,0:T(8,128)(2,1)S(1)} %copy-done.1, bf16[128,2176]{1,0:T(8,128)(2,1)S(1)} %collective-permute-done.13), kind=kOutput, calls=%fused_computation | convolution fusion | flops 805306368 | bytes 7602176 | tf_op jit(solution)/shard_map/dot_general | solution.py:70
  53.9 1.9 %collective-permute-start.14 = (bf16[64,2048]{1,0:T(8,128)(2,1)S(1)}, bf16[64,2048]{1,0:T(8,128)(2,1)S(1)}, u32[]{:S(2)}, u32[]{:S(2)}) collective-permute-start(bf16[64,2048]{1,0:T(8,128)(2,1)S(1)} %get-tuple-element.26), channel_id=1, source_target_pairs={{0,3},{1,0},{2,1},{3,2},{4,7},{5,4},{6,5},{7,6},{8,11},{9,8},{10,9... | collective-permute-start | bytes 786440 | tf_op jit(solution)/shard_map/ppermute | solution.py:22
  56.7 2.0 %collective-permute-start.15 = (bf16[64,2048]{1,0:T(8,128)(2,1)S(1)}, bf16[64,2048]{1,0:T(8,128)(2,1)S(1)}, u32[]{:S(2)}, u32[]{:S(2)}) collective-permute-start(bf16[64,2048]{1,0:T(8,128)(2,1)S(1)} %get-tuple-element.27), channel_id=1, source_target_pairs={{0,3},{1,0},{2,1},{3,2},{4,7},{5,4},{6,5},{7,6},{8,11},{9,8},{10,9... | collective-permute-start | bytes 786440 | tf_op jit(solution)/shard_map/ppermute | solution.py:22
  60.4 2.8 %collective-permute-done.15 = bf16[64,2048]{1,0:T(8,128)(2,1)S(1)} collective-permute-done((bf16[64,2048]{1,0:T(8,128)(2,1)S(1)}, bf16[64,2048]{1,0:T(8,128)(2,1)S(1)}, u32[]{:S(2)}, u32[]{:S(2)}) %collective-permute-start.15) | collective-permute-done | bytes 262176 | tf_op jit(solution)/shard_map/ppermute | solution.py:22
  63.4 3.2 %collective-permute-start.16 = (bf16[128,2048]{1,0:T(8,128)(2,1)S(1)}, bf16[128,2048]{1,0:T(8,128)(2,1)S(1)}, u32[]{:S(2)}, u32[]{:S(2)}) collective-permute-start(bf16[128,2048]{1,0:T(8,128)(2,1)S(1)} %fusion.82), channel_id=1, source_target_pairs={{0,3},{1,0},{2,1},{3,2},{4,7},{5,4},{6,5},{7,6},{8,11},{9,8},{10,9... | collective-permute-start | bytes 1572872 | tf_op jit(solution)/shard_map/ppermute | solution.py:22
  67.8 2.3 %collective-permute-done.9 = bf16[128,2048]{1,0:T(8,128)(2,1)S(1)} collective-permute-done((bf16[128,2048]{1,0:T(8,128)(2,1)S(1)}, bf16[128,2048]{1,0:T(8,128)(2,1)S(1)}, u32[]{:S(2)}, u32[]{:S(2)}) %collective-permute-start.9) | collective-permute-done | bytes 524320 | tf_op jit(solution)/shard_map/ppermute | solution.py:22
  70.1 6.3 %collective-permute-done.16 = bf16[128,2048]{1,0:T(8,128)(2,1)S(1)} collective-permute-done((bf16[128,2048]{1,0:T(8,128)(2,1)S(1)}, bf16[128,2048]{1,0:T(8,128)(2,1)S(1)}, u32[]{:S(2)}, u32[]{:S(2)}) %collective-permute-start.16) | collective-permute-done | bytes 524320 | tf_op jit(solution)/shard_map/ppermute | solution.py:22
  77.1 5.7 %collective-permute-start.18 = (bf16[64,2048]{1,0:T(8,128)(2,1)S(1)}, bf16[64,2048]{1,0:T(8,128)(2,1)S(1)}, u32[]{:S(2)}, u32[]{:S(2)}) collective-permute-start(bf16[64,2048]{1,0:T(8,128)(2,1)S(1)} %get-tuple-element.23), channel_id=1, source_target_pairs={{0,8},{1,9},{2,10},{3,11},{4,12},{5,13},{6,14},{7,15},{8,0},{9,1},... | collective-permute-start | bytes 786440 | tf_op jit(solution)/shard_map/ppermute | solution.py:22
  82.9 2.9 %collective-permute-done.17 = bf16[64,2048]{1,0:T(8,128)(2,1)S(1)} collective-permute-done((bf16[64,2048]{1,0:T(8,128)(2,1)S(1)}, bf16[64,2048]{1,0:T(8,128)(2,1)S(1)}, u32[]{:S(2)}, u32[]{:S(2)}) %collective-permute-start.17) | collective-permute-done | bytes 262176 | tf_op jit(solution)/shard_map/ppermute | solution.py:22
  85.8 4.3 %collective-permute-done.18 = bf16[64,2048]{1,0:T(8,128)(2,1)S(1)} collective-permute-done((bf16[64,2048]{1,0:T(8,128)(2,1)S(1)}, bf16[64,2048]{1,0:T(8,128)(2,1)S(1)}, u32[]{:S(2)}, u32[]{:S(2)}) %collective-permute-start.18) | collective-permute-done | bytes 262176 | tf_op jit(solution)/shard_map/ppermute | solution.py:22
  (51 shorter events, 12.9 us)
Async XLA Ops:
  0.0 36.0 %copy-start = (bf16[1,768,2048]{2,1,0:T(8,128)(2,1)S(1)}, bf16[1,768,2048]{2,1,0:T(8,128)(2,1)}, u32[]{:S(2)}) copy-start(bf16[1,768,2048]{2,1,0:T(8,128)(2,1)} %param.9) | copy-start | bytes 9437188
  2.1 9.9 %collective-permute-start = (bf16[64,2176]{1,0:T(8,128)(2,1)S(1)}, bf16[64,2176]{1,0:T(8,128)(2,1)}, u32[]{:S(2)}, u32[]{:S(2)}) collective-permute-start(bf16[64,2176]{1,0:T(8,128)(2,1)S(1)} %concatenate.30), channel_id=1, source_target_pairs={{0,12},{1,13},{2,14},{3,15},{4,0},{5,1},{6,2},{7,3},{8,4},{9,5},{1... | collective-permute-start | bytes 835592 | tf_op jit(solution)/shard_map/ppermute | solution.py:22
  5.0 12.2 %collective-permute-start.1 = (bf16[64,2176]{1,0:T(8,128)(2,1)S(1)}, bf16[64,2176]{1,0:T(8,128)(2,1)}, u32[]{:S(2)}, u32[]{:S(2)}) collective-permute-start(bf16[64,2176]{1,0:T(8,128)(2,1)S(1)} %concatenate.30), channel_id=1, source_target_pairs={{0,8},{1,9},{2,10},{3,11},{4,12},{5,13},{6,14},{7,15},{8,0},{9,1},... | collective-permute-start | bytes 835592 | tf_op jit(solution)/shard_map/ppermute | solution.py:22
  5.8 12.3 %collective-permute-start.2 = (bf16[64,2176]{1,0:T(8,128)(2,1)S(1)}, bf16[64,2176]{1,0:T(8,128)(2,1)}, u32[]{:S(2)}, u32[]{:S(2)}) collective-permute-start(bf16[64,2176]{1,0:T(8,128)(2,1)S(1)} %concatenate.30), channel_id=1, source_target_pairs={{0,4},{1,5},{2,6},{3,7},{4,8},{5,9},{6,10},{7,11},{8,12},{9,13},{1... | collective-permute-start | bytes 835592 | tf_op jit(solution)/shard_map/ppermute | solution.py:22
  14.0 13.4 %collective-permute-start.3 = (bf16[128,2176]{1,0:T(8,128)(2,1)S(1)}, bf16[128,2176]{1,0:T(8,128)(2,1)S(1)}, u32[]{:S(2)}, u32[]{:S(2)}) collective-permute-start(bf16[128,2176]{1,0:T(8,128)(2,1)S(1)} %pad_maximum_fusion), channel_id=1, source_target_pairs={{0,3},{1,0},{2,1},{3,2},{4,7},{5,4},{6,5},{7,6},{8,11},{9,8},{10,9... | collective-permute-start | bytes 1671176 | tf_op jit(solution)/shard_map/ppermute | solution.py:22
  17.1 10.7 %collective-permute-start.5 = (bf16[128,2176]{1,0:T(8,128)(2,1)S(1)}, bf16[128,2176]{1,0:T(8,128)(2,1)S(1)}, u32[]{:S(2)}, u32[]{:S(2)}) collective-permute-start(bf16[128,2176]{1,0:T(8,128)(2,1)S(1)} %pad_maximum_fusion), channel_id=1, source_target_pairs={{0,1},{1,2},{2,3},{3,0},{4,5},{5,6},{6,7},{7,4},{8,9},{9,10},{10,1... | collective-permute-start | bytes 1671176 | tf_op jit(solution)/shard_map/ppermute | solution.py:22
  19.3 7.1 %copy-start.1 = (bf16[1,2048,1536]{2,1,0:T(8,128)(2,1)S(1)}, bf16[1,2048,1536]{2,1,0:T(8,128)(2,1)}, u32[]{:S(2)}) copy-start(bf16[1,2048,1536]{2,1,0:T(8,128)(2,1)} %param.8) | copy-start | bytes 18874372
  19.3 10.8 %collective-permute-start.4 = (bf16[128,2176]{1,0:T(8,128)(2,1)S(1)}, bf16[128,2176]{1,0:T(8,128)(2,1)S(1)}, u32[]{:S(2)}, u32[]{:S(2)}) collective-permute-start(bf16[128,2176]{1,0:T(8,128)(2,1)S(1)} %constant_dynamic-update-slice_fusion), channel_id=1, source_target_pairs={{0,3},{1,0},{2,1},{3,2},{4,7},{5,4},{6,5},{7,6},{8,11},{9,8},{10,9... | collective-permute-start | bytes 1671176 | tf_op jit(solution)/shard_map/ppermute | solution.py:22
  22.6 11.2 %collective-permute-start.11 = (bf16[128,2176]{1,0:T(8,128)(2,1)S(1)}, bf16[128,2176]{1,0:T(8,128)(2,1)S(1)}, u32[]{:S(2)}, u32[]{:S(2)}) collective-permute-start(bf16[128,2176]{1,0:T(8,128)(2,1)S(1)} %constant_dynamic-update-slice_fusion), channel_id=1, source_target_pairs={{0,1},{1,2},{2,3},{3,0},{4,5},{5,6},{6,7},{7,4},{8,9},{9,10},{10,1... | collective-permute-start | bytes 1671176 | tf_op jit(solution)/shard_map/ppermute | solution.py:22
  35.9 10.8 %collective-permute-start.6 = (bf16[128,2176]{1,0:T(8,128)(2,1)S(1)}, bf16[128,2176]{1,0:T(8,128)(2,1)S(1)}, u32[]{:S(2)}, u32[]{:S(2)}) collective-permute-start(bf16[128,2176]{1,0:T(8,128)(2,1)S(1)} %collective-permute-done.5), channel_id=1, source_target_pairs={{0,1},{1,2},{2,3},{3,0},{4,5},{5,6},{6,7},{7,4},{8,9},{9,10},{10,1... | collective-permute-start | bytes 1671176 | tf_op jit(solution)/shard_map/ppermute | solution.py:22
  37.1 30.7 %collective-permute-start.10 = (bf16[128,2048]{1,0:T(8,128)(2,1)S(1)}, bf16[128,2048]{1,0:T(8,128)(2,1)S(1)}, u32[]{:S(2)}, u32[]{:S(2)}) collective-permute-start(bf16[128,2048]{1,0:T(8,128)(2,1)S(1)} %slice.323), channel_id=1, source_target_pairs={{0,1},{1,2},{2,3},{3,0},{4,5},{5,6},{6,7},{7,4},{8,9},{9,10},{10,1... | collective-permute-start | bytes 1572872 | tf_op jit(solution)/shard_map/ppermute | solution.py:22
  38.0 10.0 %collective-permute-start.13 = (bf16[128,2176]{1,0:T(8,128)(2,1)S(1)}, bf16[128,2176]{1,0:T(8,128)(2,1)S(1)}, u32[]{:S(2)}, u32[]{:S(2)}) collective-permute-start(bf16[128,2176]{1,0:T(8,128)(2,1)S(1)} %collective-permute-done.4), channel_id=1, source_target_pairs={{0,3},{1,0},{2,1},{3,2},{4,7},{5,4},{6,5},{7,6},{8,11},{9,8},{10,9... | collective-permute-start | bytes 1671176 | tf_op jit(solution)/shard_map/ppermute | solution.py:22
  41.8 26.0 %collective-permute-start.12 = (bf16[128,2048]{1,0:T(8,128)(2,1)S(1)}, bf16[128,2048]{1,0:T(8,128)(2,1)S(1)}, u32[]{:S(2)}, u32[]{:S(2)}) collective-permute-start(bf16[128,2048]{1,0:T(8,128)(2,1)S(1)} %slice.322), channel_id=1, source_target_pairs={{0,3},{1,0},{2,1},{3,2},{4,7},{5,4},{6,5},{7,6},{8,11},{9,8},{10,9... | collective-permute-start | bytes 1572872 | tf_op jit(solution)/shard_map/ppermute | solution.py:22
  48.8 7.9 %collective-permute-start.7 = (bf16[64,2048]{1,0:T(8,128)(2,1)S(1)}, bf16[64,2048]{1,0:T(8,128)(2,1)S(1)}, u32[]{:S(2)}, u32[]{:S(2)}) collective-permute-start(bf16[64,2048]{1,0:T(8,128)(2,1)S(1)} %get-tuple-element.24), channel_id=1, source_target_pairs={{0,1},{1,2},{2,3},{3,0},{4,5},{5,6},{6,7},{7,4},{8,9},{9,10},{10,1... | collective-permute-start | bytes 786440 | tf_op jit(solution)/shard_map/ppermute | solution.py:22
  50.9 8.6 %collective-permute-start.8 = (bf16[64,2048]{1,0:T(8,128)(2,1)S(1)}, bf16[64,2048]{1,0:T(8,128)(2,1)S(1)}, u32[]{:S(2)}, u32[]{:S(2)}) collective-permute-start(bf16[64,2048]{1,0:T(8,128)(2,1)S(1)} %get-tuple-element.25), channel_id=1, source_target_pairs={{0,1},{1,2},{2,3},{3,0},{4,5},{5,6},{6,7},{7,4},{8,9},{9,10},{10,1... | collective-permute-start | bytes 786440 | tf_op jit(solution)/shard_map/ppermute | solution.py:22
  53.9 6.4 %collective-permute-start.14 = (bf16[64,2048]{1,0:T(8,128)(2,1)S(1)}, bf16[64,2048]{1,0:T(8,128)(2,1)S(1)}, u32[]{:S(2)}, u32[]{:S(2)}) collective-permute-start(bf16[64,2048]{1,0:T(8,128)(2,1)S(1)} %get-tuple-element.26), channel_id=1, source_target_pairs={{0,3},{1,0},{2,1},{3,2},{4,7},{5,4},{6,5},{7,6},{8,11},{9,8},{10,9... | collective-permute-start | bytes 786440 | tf_op jit(solution)/shard_map/ppermute | solution.py:22
  56.7 6.5 %collective-permute-start.15 = (bf16[64,2048]{1,0:T(8,128)(2,1)S(1)}, bf16[64,2048]{1,0:T(8,128)(2,1)S(1)}, u32[]{:S(2)}, u32[]{:S(2)}) collective-permute-start(bf16[64,2048]{1,0:T(8,128)(2,1)S(1)} %get-tuple-element.27), channel_id=1, source_target_pairs={{0,3},{1,0},{2,1},{3,2},{4,7},{5,4},{6,5},{7,6},{8,11},{9,8},{10,9... | collective-permute-start | bytes 786440 | tf_op jit(solution)/shard_map/ppermute | solution.py:22
  59.7 10.5 %collective-permute-start.9 = (bf16[128,2048]{1,0:T(8,128)(2,1)S(1)}, bf16[128,2048]{1,0:T(8,128)(2,1)S(1)}, u32[]{:S(2)}, u32[]{:S(2)}) collective-permute-start(bf16[128,2048]{1,0:T(8,128)(2,1)S(1)} %fusion.84), channel_id=1, source_target_pairs={{0,1},{1,2},{2,3},{3,0},{4,5},{5,6},{6,7},{7,4},{8,9},{9,10},{10,1... | collective-permute-start | bytes 1572872 | tf_op jit(solution)/shard_map/ppermute | solution.py:22
  63.4 13.1 %collective-permute-start.16 = (bf16[128,2048]{1,0:T(8,128)(2,1)S(1)}, bf16[128,2048]{1,0:T(8,128)(2,1)S(1)}, u32[]{:S(2)}, u32[]{:S(2)}) collective-permute-start(bf16[128,2048]{1,0:T(8,128)(2,1)S(1)} %fusion.82), channel_id=1, source_target_pairs={{0,3},{1,0},{2,1},{3,2},{4,7},{5,4},{6,5},{7,6},{8,11},{9,8},{10,9... | collective-permute-start | bytes 1572872 | tf_op jit(solution)/shard_map/ppermute | solution.py:22
  77.0 8.7 %collective-permute-start.17 = (bf16[64,2048]{1,0:T(8,128)(2,1)S(1)}, bf16[64,2048]{1,0:T(8,128)(2,1)S(1)}, u32[]{:S(2)}, u32[]{:S(2)}) collective-permute-start(bf16[64,2048]{1,0:T(8,128)(2,1)S(1)} %get-tuple-element.21), channel_id=1, source_target_pairs={{0,4},{1,5},{2,6},{3,7},{4,8},{5,9},{6,10},{7,11},{8,12},{9,13},{1... | collective-permute-start | bytes 786440 | tf_op jit(solution)/shard_map/ppermute | solution.py:22
  77.1 12.9 %collective-permute-start.18 = (bf16[64,2048]{1,0:T(8,128)(2,1)S(1)}, bf16[64,2048]{1,0:T(8,128)(2,1)S(1)}, u32[]{:S(2)}, u32[]{:S(2)}) collective-permute-start(bf16[64,2048]{1,0:T(8,128)(2,1)S(1)} %get-tuple-element.23), channel_id=1, source_target_pairs={{0,8},{1,9},{2,10},{3,11},{4,12},{5,13},{6,14},{7,15},{8,0},{9,1},... | collective-permute-start | bytes 786440 | tf_op jit(solution)/shard_map/ppermute | solution.py:22
  82.9 7.2 %collective-permute-start.19 = (bf16[64,2048]{1,0:T(8,128)(2,1)S(1)}, bf16[64,2048]{1,0:T(8,128)(2,1)S(1)}, u32[]{:S(2)}, u32[]{:S(2)}) collective-permute-start(bf16[64,2048]{1,0:T(8,128)(2,1)S(1)} %get-tuple-element.22), channel_id=1, source_target_pairs={{0,12},{1,13},{2,14},{3,15},{4,0},{5,1},{6,2},{7,3},{8,4},{9,5},{1... | collective-permute-start | bytes 786440 | tf_op jit(solution)/shard_map/ppermute | solution.py:22

commit v7 on v6

--- a/solution.py
+++ b/solution.py
@@ -24,8 +24,8 @@
 
 def scatter_ring(own, right, far_a, far_b, left, axis):
     cut = far_a.shape[0]
-    got_a = shift_two(far_a.astype(jnp.bfloat16), axis, 1)
-    got_b = shift_two(far_b.astype(jnp.bfloat16), axis, -1)
+    got_a = shift(far_a.astype(jnp.bfloat16), axis, 1)
+    got_b = shift(far_b.astype(jnp.bfloat16), axis, -1)
     right_early = shift(right[cut:].astype(jnp.bfloat16), axis, 1)
     left_early = shift(left[:cut].astype(jnp.bfloat16), axis, -1)
     right_late = shift((right[:cut] + got_a.astype(jnp.float32)).astype(jnp.bfloat16), axis, 1)
@@ -33,11 +33,6 @@
     from_left = jnp.concatenate([right_late, right_early], axis=0).astype(jnp.float32)
     from_right = jnp.concatenate([left_early, left_late], axis=0).astype(jnp.float32)
     return own + from_left + from_right
-
-
-def shift_two(block, stage, step):
-    cut = block.shape[0] // 2
-    return jnp.concatenate([shift(block[:cut], stage, step), shift(block[cut:], stage, step)], axis=0)
 
 
 def scatter_direct(parts, stage):
@@ -103,7 +98,10 @@
     own_a = expert_rows(first_a, me, width, w_in[0], w_out[0], mine_a)
     own_b = expert_rows(first_b, me, width, w_in[0], w_out[0], mine_b)
     pieces = [jnp.concatenate([own_a, own_b], axis=0)]
-    pieces += [expert_rows(p, me, width, w_in[0], w_out[0]) for p in (right, far_a, far_b, left)]
+    cut = far_a.shape[0]
+    far = expert_rows(jnp.concatenate([far_a, far_b], axis=0), me, width, w_in[0], w_out[0])
+    pieces += [expert_rows(right, me, width, w_in[0], w_out[0]), far[:cut], far[cut:]]
+    pieces += [expert_rows(left, me, width, w_in[0], w_out[0])]
     stage = scatter_ring(*pieces, 1)
     return scatter_direct(stage.reshape(SIDE, count, width), 0).astype(jnp.bfloat16)
 
@@ -116,4 +114,6 @@
         P("expert", None, None),
         P("expert", None, None),
     )
-    return jax.shard_map(layer, mesh=mesh, in_specs=placed, out_specs=P(("dp", "expert"), None), check_vma=False)
+    return jax.shard_map(
+        layer, mesh=mesh, in_specs=placed, out_specs=P(("dp", "expert"), None), check_vma=False
+    )

time: 91.8 us -> 87.1 us (0.949)
  the two profiles are of different devices: /device:TPU:64 before, /device:TPU:104 now
where the time goes in v7:
time: 87.1 us; the launch traced here: 86.8 us
  waiting for transfers between devices  36.6 us (42%)
  starting transfers between devices  26.7 us (31%)
  matrix products  14.7 us (17%)
  other arithmetic  4.76 us (5%)
  local copies, waits for them, and re-layouts  3.79 us (4%)
    ppermute x18, waiting for transfers between devices, shift(): return lax.ppermute(tree, ('dp', 'expert'), pairs)  36.6 us
    ppermute x18, starting transfers between devices, shift(): return lax.ppermute(tree, ('dp', 'expert'), pairs)  26.7 us
    dot_general x5, matrix products, expert_rows(): jnp.dot(rows[:, :width], w_in, preferred_element_type=jnp.float32)  10.1 us
    dot_general x5, matrix products, expert_rows(): jnp.dot(inner, w_out, preferred_element_type=jnp.float32)  4.41 us
  transfers between devices with their start and end apart: 18, of which 12 were waited for; matrix products, arithmetic and copies ran while one was open for 19% of the time, Pallas kernels for 0%

profile of v7, /device:TPU:104, one launch (start us, length us, event | category | flops | bytes accessed | tf_op | source)
XLA Modules:
  0.0 86.8 jit_solution(3276253760996654241)
XLA Ops:
  1.1 1.1 %concatenate.27 = bf16[64,2176]{1,0:T(8,128)(2,1)S(1)} concatenate(bf16[64,2048]{1,0:T(8,128)(2,1)} %param.5, bf16[64,16]{1,0:T(8,128)(2,1)S(1)} %copy.8, bf16[64,16]{1,0:T(8,128)(2,1)S(1)} %copy.9, bf16[64,96]{1,0:T(8,128)(2,1)S(1)} %broadcast_in_dim.61), dimensions={1} | concatenate | bytes 557056 | tf_op jit(solution)/shard_map/concatenate | solution.py:82
  2.1 2.8 %collective-permute-start = (bf16[64,2176]{1,0:T(8,128)(2,1)S(1)}, bf16[64,2176]{1,0:T(8,128)(2,1)}, u32[]{:S(2)}, u32[]{:S(2)}) collective-permute-start(bf16[64,2176]{1,0:T(8,128)(2,1)S(1)} %concatenate.27), channel_id=1, source_target_pairs={{0,12},{1,13},{2,14},{3,15},{4,0},{5,1},{6,2},{7,3},{8,4},{9,5},{1... | collective-permute-start | bytes 835592 | tf_op jit(solution)/shard_map/ppermute | solution.py:22
  6.7 5.4 %collective-permute-done = bf16[64,2176]{1,0:T(8,128)(2,1)} collective-permute-done((bf16[64,2176]{1,0:T(8,128)(2,1)S(1)}, bf16[64,2176]{1,0:T(8,128)(2,1)}, u32[]{:S(2)}, u32[]{:S(2)}) %collective-permute-start) | collective-permute-done | bytes 278560 | tf_op jit(solution)/shard_map/ppermute | solution.py:22
  12.1 1.0 %select_reduce_fusion.3 = f32[128]{0:T(128)S(1)} fusion(bf16[64,2176]{1,0:T(8,128)(2,1)} %collective-permute-done, bf16[64,2176]{1,0:T(8,128)(2,1)S(1)} %concatenate.27, pred[16]{0:T(512)(128)(4,1)S(1)} %iota_compare_fusion.1), kind=kLoop, calls=%fused_computation.80 | loop fusion | flops 22400 | bytes 557584 | tf_op jit(solution)/shard_map/reduce_sum | solution.py:50
  13.0 1.0 %pad_maximum_fusion = bf16[128,2176]{1,0:T(8,128)(2,1)S(1)} fusion(bf16[64,2176]{1,0:T(8,128)(2,1)} %collective-permute-done, bf16[64,2176]{1,0:T(8,128)(2,1)S(1)} %concatenate.27), kind=kLoop, calls=%fused_computation.55 | loop fusion | flops 1114112 | bytes 1114112 | tf_op jit(solution)/shard_map/concatenate | solution.py:86
  14.0 1.7 %collective-permute-start.5 = (bf16[128,2176]{1,0:T(8,128)(2,1)S(1)}, bf16[128,2176]{1,0:T(8,128)(2,1)S(1)}, u32[]{:S(2)}, u32[]{:S(2)}) collective-permute-start(bf16[128,2176]{1,0:T(8,128)(2,1)S(1)} %pad_maximum_fusion), channel_id=1, source_target_pairs={{0,1},{1,2},{2,3},{3,0},{4,5},{5,6},{6,7},{7,4},{8,9},{9,10},{10,1... | collective-permute-start | bytes 1671176 | tf_op jit(solution)/shard_map/ppermute | solution.py:22
  16.2 1.0 %constant_dynamic-update-slice_fusion.1 = bf16[128,2176]{1,0:T(8,128)(2,1)S(1)} fusion(bf16[64,2176]{1,0:T(8,128)(2,1)} %collective-permute-done.1), kind=kLoop, calls=%fused_computation.88 | loop fusion | bytes 557056
  17.1 1.3 %collective-permute-done.2 = bf16[64,2176]{1,0:T(8,128)(2,1)} collective-permute-done((bf16[64,2176]{1,0:T(8,128)(2,1)S(1)}, bf16[64,2176]{1,0:T(8,128)(2,1)}, u32[]{:S(2)}, u32[]{:S(2)}) %collective-permute-start.2) | collective-permute-done | bytes 278560 | tf_op jit(solution)/shard_map/ppermute | solution.py:22
  18.4 1.0 %constant_dynamic-update-slice_fusion = bf16[128,2176]{1,0:T(8,128)(2,1)S(1)} fusion(bf16[128,2176]{1,0:T(8,128)(2,1)S(1)} %constant_dynamic-update-slice_fusion.1, bf16[64,2176]{1,0:T(8,128)(2,1)} %collective-permute-done.2), kind=kLoop, calls=%fused_computation.87 | loop fusion | bytes 557056 | tf_op jit(solution)/shard_map/concatenate | solution.py:87
  20.1 1.6 %collective-permute-start.11 = (bf16[128,2176]{1,0:T(8,128)(2,1)S(1)}, bf16[128,2176]{1,0:T(8,128)(2,1)S(1)}, u32[]{:S(2)}, u32[]{:S(2)}) collective-permute-start(bf16[128,2176]{1,0:T(8,128)(2,1)S(1)} %constant_dynamic-update-slice_fusion), channel_id=1, source_target_pairs={{0,1},{1,2},{2,3},{3,0},{4,5},{5,6},{6,7},{7,4},{8,9},{9,10},{10,1... | collective-permute-start | bytes 1671176 | tf_op jit(solution)/shard_map/ppermute | solution.py:22
  21.7 3.8 %fusion.8 = f32[128,1536]{1,0:T(8,128)S(1)} fusion(bf16[1,2048,1536]{2,1,0:T(8,128)(2,1)} %param.8, bf16[128,2176]{1,0:T(8,128)(2,1)S(1)} %pad_maximum_fusion), kind=kOutput, calls=%fused_computation.8 | convolution fusion | flops 805306368 | bytes 7602176 | tf_op jit(solution)/shard_map/dot_general | solution.py:65
  25.5 1.0 %fusion.6 = f32[128,1536]{1,0:T(8,128)S(1)} fusion(bf16[1,2048,1536]{2,1,0:T(8,128)(2,1)S(1)} %copy-done.1, bf16[128,2176]{1,0:T(8,128)(2,1)S(1)} %constant_dynamic-update-slice_fusion), kind=kOutput, calls=%fused_computation.6 | convolution fusion | flops 805306368 | bytes 7602176 | tf_op jit(solution)/shard_map/dot_general | solution.py:65
  26.5 1.6 %collective-permute-start.6 = (bf16[128,2176]{1,0:T(8,128)(2,1)S(1)}, bf16[128,2176]{1,0:T(8,128)(2,1)S(1)}, u32[]{:S(2)}, u32[]{:S(2)}) collective-permute-start(bf16[128,2176]{1,0:T(8,128)(2,1)S(1)} %collective-permute-done.5), channel_id=1, source_target_pairs={{0,1},{1,2},{2,3},{3,0},{4,5},{5,6},{6,7},{7,4},{8,9},{9,10},{10,1... | collective-permute-start | bytes 1671176 | tf_op jit(solution)/shard_map/ppermute | solution.py:22
  28.1 3.1 %collective-permute-done.4 = bf16[128,2176]{1,0:T(8,128)(2,1)S(1)} collective-permute-done((bf16[128,2176]{1,0:T(8,128)(2,1)S(1)}, bf16[128,2176]{1,0:T(8,128)(2,1)S(1)}, u32[]{:S(2)}, u32[]{:S(2)}) %collective-permute-start.4) | collective-permute-done | bytes 557088 | tf_op jit(solution)/shard_map/ppermute | solution.py:22
  31.8 1.8 %fusion.4 = f32[256,1536]{1,0:T(8,128)S(1)} fusion(bf16[1,2048,1536]{2,1,0:T(8,128)(2,1)S(1)} %copy-done.1, bf16[256,2176]{1,0:T(8,128)(2,1)S(1)} %constant_dynamic-update-slice_fusion.2), kind=kOutput, calls=%fused_computation.4 | convolution fusion | flops 1610612736 | bytes 8912896 | tf_op jit(solution)/shard_map/dot_general | solution.py:65
  33.7 1.8 %fusion = f32[256,1536]{1,0:T(8,128)S(1)} fusion(bf16[1,2048,1536]{2,1,0:T(8,128)(2,1)S(1)} %copy-done.1, bf16[256,2176]{1,0:T(8,128)(2,1)S(1)} %constant_dynamic-update-slice_fusion.6), kind=kOutput, calls=%fused_computation | convolution fusion | flops 1610612736 | bytes 8912896 | tf_op jit(solution)/shard_map/dot_general | solution.py:65
  36.1 4.6 %collective-permute-done.7 = bf16[128,2176]{1,0:T(8,128)(2,1)S(1)} collective-permute-done((bf16[128,2176]{1,0:T(8,128)(2,1)S(1)}, bf16[128,2176]{1,0:T(8,128)(2,1)S(1)}, u32[]{:S(2)}, u32[]{:S(2)}) %collective-permute-start.7) | collective-permute-done | bytes 557088 | tf_op jit(solution)/shard_map/ppermute | solution.py:22
  41.1 1.8 %fusion.2 = f32[256,1536]{1,0:T(8,128)S(1)} fusion(bf16[1,2048,1536]{2,1,0:T(8,128)(2,1)S(1)} %copy-done.1, bf16[256,2176]{1,0:T(8,128)(2,1)S(1)} %constant_dynamic-update-slice_fusion.4), kind=kOutput, calls=%fused_computation.2 | convolution fusion | flops 1610612736 | bytes 8912896 | tf_op jit(solution)/shard_map/dot_general | solution.py:65
  42.9 1.0 %fusion.38 = bf16[256,2048]{1,0:T(8,128)(2,1)S(1)} fusion(bf16[1,768,2048]{2,1,0:T(8,128)(2,1)S(1)} %copy-done, f32[256]{0:T(256)S(1)} %get-tuple-element.15, f32[256,1536]{1,0:T(8,128)S(1)} %fusion.2), kind=kOutput, calls=%fused_computation.26 | convolution fusion | flops 808583168 | bytes 5768192 | tf_op jit(solution)/shard_map/dot_general | solution.py:67
  44.0 1.4 %collective-permute-start.8 = (bf16[128,2048]{1,0:T(8,128)(2,1)S(1)}, bf16[128,2048]{1,0:T(8,128)(2,1)S(1)}, u32[]{:S(2)}, u32[]{:S(2)}) collective-permute-start(bf16[128,2048]{1,0:T(8,128)(2,1)S(1)} %get-tuple-element.23), channel_id=1, source_target_pairs={{0,1},{1,2},{2,3},{3,0},{4,5},{5,6},{6,7},{7,4},{8,9},{9,10},{10,1... | collective-permute-start | bytes 1572872 | tf_op jit(solution)/shard_map/ppermute | solution.py:22
  45.4 1.1 %fusion.26 = f32[256,2048]{1,0:T(8,128)S(1)} fusion(bf16[1,768,2048]{2,1,0:T(8,128)(2,1)S(1)} %copy-done, f32[256]{0:T(256)S(1)} %get-tuple-element.14, f32[256,1536]{1,0:T(8,128)S(1)} %fusion.4), kind=kOutput, calls=%fused_computation.22 | convolution fusion | flops 808058880 | bytes 6816768 | tf_op jit(solution)/shard_map/dot_general | solution.py:67
  46.5 2.7 %collective-permute-start.10 = (bf16[128,2048]{1,0:T(8,128)(2,1)S(1)}, bf16[128,2048]{1,0:T(8,128)(2,1)S(1)}, u32[]{:S(2)}, u32[]{:S(2)}) collective-permute-start(bf16[128,2048]{1,0:T(8,128)(2,1)S(1)} %slice.280), channel_id=1, source_target_pairs={{0,1},{1,2},{2,3},{3,0},{4,5},{5,6},{6,7},{7,4},{8,9},{9,10},{10,1... | collective-permute-start | bytes 1572872 | tf_op jit(solution)/shard_map/ppermute | solution.py:22
  49.2 1.1 %fusion.47 = f32[256,2048]{1,0:T(8,128)S(1)} fusion(bf16[1,768,2048]{2,1,0:T(8,128)(2,1)S(1)} %copy-done, f32[256]{0:T(256)S(1)} %get-tuple-element.13, f32[256,1536]{1,0:T(8,128)S(1)} %fusion), kind=kOutput, calls=%fused_computation.29 | convolution fusion | flops 808058880 | bytes 6816768 | tf_op jit(solution)/shard_map/dot_general | solution.py:67
  50.4 1.4 %collective-permute-start.12 = (bf16[128,2048]{1,0:T(8,128)(2,1)S(1)}, bf16[128,2048]{1,0:T(8,128)(2,1)S(1)}, u32[]{:S(2)}, u32[]{:S(2)}) collective-permute-start(bf16[128,2048]{1,0:T(8,128)(2,1)S(1)} %slice.279), channel_id=1, source_target_pairs={{0,3},{1,0},{2,1},{3,2},{4,7},{5,4},{6,5},{7,6},{8,11},{9,8},{10,9... | collective-permute-start | bytes 1572872 | tf_op jit(solution)/shard_map/ppermute | solution.py:22
  51.8 1.5 %collective-permute-done.8 = bf16[128,2048]{1,0:T(8,128)(2,1)S(1)} collective-permute-done((bf16[128,2048]{1,0:T(8,128)(2,1)S(1)}, bf16[128,2048]{1,0:T(8,128)(2,1)S(1)}, u32[]{:S(2)}, u32[]{:S(2)}) %collective-permute-start.8) | collective-permute-done | bytes 524320 | tf_op jit(solution)/shard_map/ppermute | solution.py:22
  53.4 1.5 %collective-permute-start.9 = (bf16[128,2048]{1,0:T(8,128)(2,1)S(1)}, bf16[128,2048]{1,0:T(8,128)(2,1)S(1)}, u32[]{:S(2)}, u32[]{:S(2)}) collective-permute-start(bf16[128,2048]{1,0:T(8,128)(2,1)S(1)} %fusion.69), channel_id=1, source_target_pairs={{0,1},{1,2},{2,3},{3,0},{4,5},{5,6},{6,7},{7,4},{8,9},{9,10},{10,1... | collective-permute-start | bytes 1572872 | tf_op jit(solution)/shard_map/ppermute | solution.py:22
  54.9 3.5 %collective-permute-done.13 = bf16[128,2048]{1,0:T(8,128)(2,1)S(1)} collective-permute-done((bf16[128,2048]{1,0:T(8,128)(2,1)S(1)}, bf16[128,2048]{1,0:T(8,128)(2,1)S(1)}, u32[]{:S(2)}, u32[]{:S(2)}) %collective-permute-start.13) | collective-permute-done | bytes 524320 | tf_op jit(solution)/shard_map/ppermute | solution.py:22
  60.1 3.9 %collective-permute-done.12 = bf16[128,2048]{1,0:T(8,128)(2,1)S(1)} collective-permute-done((bf16[128,2048]{1,0:T(8,128)(2,1)S(1)}, bf16[128,2048]{1,0:T(8,128)(2,1)S(1)}, u32[]{:S(2)}, u32[]{:S(2)}) %collective-permute-start.12) | collective-permute-done | bytes 524320 | tf_op jit(solution)/shard_map/ppermute | solution.py:22
  64.5 5.1 %collective-permute-done.14 = bf16[128,2048]{1,0:T(8,128)(2,1)S(1)} collective-permute-done((bf16[128,2048]{1,0:T(8,128)(2,1)S(1)}, bf16[128,2048]{1,0:T(8,128)(2,1)S(1)}, u32[]{:S(2)}, u32[]{:S(2)}) %collective-permute-start.14) | collective-permute-done | bytes 524320 | tf_op jit(solution)/shard_map/ppermute | solution.py:22
  70.4 8.5 %collective-permute-start.16 = (bf16[64,2048]{1,0:T(8,128)(2,1)S(1)}, bf16[64,2048]{1,0:T(8,128)(2,1)S(1)}, u32[]{:S(2)}, u32[]{:S(2)}) collective-permute-start(bf16[64,2048]{1,0:T(8,128)(2,1)S(1)} %get-tuple-element.22), channel_id=1, source_target_pairs={{0,8},{1,9},{2,10},{3,11},{4,12},{5,13},{6,14},{7,15},{8,0},{9,1},... | collective-permute-start | bytes 786440 | tf_op jit(solution)/shard_map/ppermute | solution.py:22
  78.9 2.9 %collective-permute-done.15 = bf16[64,2048]{1,0:T(8,128)(2,1)S(1)} collective-permute-done((bf16[64,2048]{1,0:T(8,128)(2,1)S(1)}, bf16[64,2048]{1,0:T(8,128)(2,1)S(1)}, u32[]{:S(2)}, u32[]{:S(2)}) %collective-permute-start.15) | collective-permute-done | bytes 262176 | tf_op jit(solution)/shard_map/ppermute | solution.py:22
  81.8 4.3 %collective-permute-done.16 = bf16[64,2048]{1,0:T(8,128)(2,1)S(1)} collective-permute-done((bf16[64,2048]{1,0:T(8,128)(2,1)S(1)}, bf16[64,2048]{1,0:T(8,128)(2,1)S(1)}, u32[]{:S(2)}, u32[]{:S(2)}) %collective-permute-start.16) | collective-permute-done | bytes 262176 | tf_op jit(solution)/shard_map/ppermute | solution.py:22
  (45 shorter events, 9.6 us)
Async XLA Ops:
  0.0 42.9 %copy-start = (bf16[1,768,2048]{2,1,0:T(8,128)(2,1)S(1)}, bf16[1,768,2048]{2,1,0:T(8,128)(2,1)}, u32[]{:S(2)}) copy-start(bf16[1,768,2048]{2,1,0:T(8,128)(2,1)} %param.9) | copy-start | bytes 9437188
  2.1 9.9 %collective-permute-start = (bf16[64,2176]{1,0:T(8,128)(2,1)S(1)}, bf16[64,2176]{1,0:T(8,128)(2,1)}, u32[]{:S(2)}, u32[]{:S(2)}) collective-permute-start(bf16[64,2176]{1,0:T(8,128)(2,1)S(1)} %concatenate.27), channel_id=1, source_target_pairs={{0,12},{1,13},{2,14},{3,15},{4,0},{5,1},{6,2},{7,3},{8,4},{9,5},{1... | collective-permute-start | bytes 835592 | tf_op jit(solution)/shard_map/ppermute | solution.py:22
  5.0 11.2 %collective-permute-start.1 = (bf16[64,2176]{1,0:T(8,128)(2,1)S(1)}, bf16[64,2176]{1,0:T(8,128)(2,1)}, u32[]{:S(2)}, u32[]{:S(2)}) collective-permute-start(bf16[64,2176]{1,0:T(8,128)(2,1)S(1)} %concatenate.27), channel_id=1, source_target_pairs={{0,8},{1,9},{2,10},{3,11},{4,12},{5,13},{6,14},{7,15},{8,0},{9,1},... | collective-permute-start | bytes 835592 | tf_op jit(solution)/shard_map/ppermute | solution.py:22
  5.8 12.6 %collective-permute-start.2 = (bf16[64,2176]{1,0:T(8,128)(2,1)S(1)}, bf16[64,2176]{1,0:T(8,128)(2,1)}, u32[]{:S(2)}, u32[]{:S(2)}) collective-permute-start(bf16[64,2176]{1,0:T(8,128)(2,1)S(1)} %concatenate.27), channel_id=1, source_target_pairs={{0,4},{1,5},{2,6},{3,7},{4,8},{5,9},{6,10},{7,11},{8,12},{9,13},{1... | collective-permute-start | bytes 835592 | tf_op jit(solution)/shard_map/ppermute | solution.py:22
  14.0 12.4 %collective-permute-start.5 = (bf16[128,2176]{1,0:T(8,128)(2,1)S(1)}, bf16[128,2176]{1,0:T(8,128)(2,1)S(1)}, u32[]{:S(2)}, u32[]{:S(2)}) collective-permute-start(bf16[128,2176]{1,0:T(8,128)(2,1)S(1)} %pad_maximum_fusion), channel_id=1, source_target_pairs={{0,1},{1,2},{2,3},{3,0},{4,5},{5,6},{6,7},{7,4},{8,9},{9,10},{10,1... | collective-permute-start | bytes 1671176 | tf_op jit(solution)/shard_map/ppermute | solution.py:22
  15.7 16.0 %collective-permute-start.3 = (bf16[128,2176]{1,0:T(8,128)(2,1)S(1)}, bf16[128,2176]{1,0:T(8,128)(2,1)S(1)}, u32[]{:S(2)}, u32[]{:S(2)}) collective-permute-start(bf16[128,2176]{1,0:T(8,128)(2,1)S(1)} %pad_maximum_fusion), channel_id=1, source_target_pairs={{0,3},{1,0},{2,1},{3,2},{4,7},{5,4},{6,5},{7,6},{8,11},{9,8},{10,9... | collective-permute-start | bytes 1671176 | tf_op jit(solution)/shard_map/ppermute | solution.py:22
  19.6 5.9 %copy-start.1 = (bf16[1,2048,1536]{2,1,0:T(8,128)(2,1)S(1)}, bf16[1,2048,1536]{2,1,0:T(8,128)(2,1)}, u32[]{:S(2)}) copy-start(bf16[1,2048,1536]{2,1,0:T(8,128)(2,1)} %param.8) | copy-start | bytes 18874372
  19.6 11.6 %collective-permute-start.4 = (bf16[128,2176]{1,0:T(8,128)(2,1)S(1)}, bf16[128,2176]{1,0:T(8,128)(2,1)S(1)}, u32[]{:S(2)}, u32[]{:S(2)}) collective-permute-start(bf16[128,2176]{1,0:T(8,128)(2,1)S(1)} %constant_dynamic-update-slice_fusion), channel_id=1, source_target_pairs={{0,3},{1,0},{2,1},{3,2},{4,7},{5,4},{6,5},{7,6},{8,11},{9,8},{10,9... | collective-permute-start | bytes 1671176 | tf_op jit(solution)/shard_map/ppermute | solution.py:22
  20.1 13.6 %collective-permute-start.11 = (bf16[128,2176]{1,0:T(8,128)(2,1)S(1)}, bf16[128,2176]{1,0:T(8,128)(2,1)S(1)}, u32[]{:S(2)}, u32[]{:S(2)}) collective-permute-start(bf16[128,2176]{1,0:T(8,128)(2,1)S(1)} %constant_dynamic-update-slice_fusion), channel_id=1, source_target_pairs={{0,1},{1,2},{2,3},{3,0},{4,5},{5,6},{6,7},{7,4},{8,9},{9,10},{10,1... | collective-permute-start | bytes 1671176 | tf_op jit(solution)/shard_map/ppermute | solution.py:22
  26.5 9.6 %collective-permute-start.6 = (bf16[128,2176]{1,0:T(8,128)(2,1)S(1)}, bf16[128,2176]{1,0:T(8,128)(2,1)S(1)}, u32[]{:S(2)}, u32[]{:S(2)}) collective-permute-start(bf16[128,2176]{1,0:T(8,128)(2,1)S(1)} %collective-permute-done.5), channel_id=1, source_target_pairs={{0,1},{1,2},{2,3},{3,0},{4,5},{5,6},{6,7},{7,4},{8,9},{9,10},{10,1... | collective-permute-start | bytes 1671176 | tf_op jit(solution)/shard_map/ppermute | solution.py:22
  31.2 9.5 %collective-permute-start.7 = (bf16[128,2176]{1,0:T(8,128)(2,1)S(1)}, bf16[128,2176]{1,0:T(8,128)(2,1)S(1)}, u32[]{:S(2)}, u32[]{:S(2)}) collective-permute-start(bf16[128,2176]{1,0:T(8,128)(2,1)S(1)} %collective-permute-done.4), channel_id=1, source_target_pairs={{0,3},{1,0},{2,1},{3,2},{4,7},{5,4},{6,5},{7,6},{8,11},{9,8},{10,9... | collective-permute-start | bytes 1671176 | tf_op jit(solution)/shard_map/ppermute | solution.py:22
  44.0 9.3 %collective-permute-start.8 = (bf16[128,2048]{1,0:T(8,128)(2,1)S(1)}, bf16[128,2048]{1,0:T(8,128)(2,1)S(1)}, u32[]{:S(2)}, u32[]{:S(2)}) collective-permute-start(bf16[128,2048]{1,0:T(8,128)(2,1)S(1)} %get-tuple-element.23), channel_id=1, source_target_pairs={{0,1},{1,2},{2,3},{3,0},{4,5},{5,6},{6,7},{7,4},{8,9},{9,10},{10,1... | collective-permute-start | bytes 1572872 | tf_op jit(solution)/shard_map/ppermute | solution.py:22
  46.5 13.6 %collective-permute-start.10 = (bf16[128,2048]{1,0:T(8,128)(2,1)S(1)}, bf16[128,2048]{1,0:T(8,128)(2,1)S(1)}, u32[]{:S(2)}, u32[]{:S(2)}) collective-permute-start(bf16[128,2048]{1,0:T(8,128)(2,1)S(1)} %slice.280), channel_id=1, source_target_pairs={{0,1},{1,2},{2,3},{3,0},{4,5},{5,6},{6,7},{7,4},{8,9},{9,10},{10,1... | collective-permute-start | bytes 1572872 | tf_op jit(solution)/shard_map/ppermute | solution.py:22
  49.2 9.2 %collective-permute-start.13 = (bf16[128,2048]{1,0:T(8,128)(2,1)S(1)}, bf16[128,2048]{1,0:T(8,128)(2,1)S(1)}, u32[]{:S(2)}, u32[]{:S(2)}) collective-permute-start(bf16[128,2048]{1,0:T(8,128)(2,1)S(1)} %get-tuple-element.24), channel_id=1, source_target_pairs={{0,3},{1,0},{2,1},{3,2},{4,7},{5,4},{6,5},{7,6},{8,11},{9,8},{10,9... | collective-permute-start | bytes 1572872 | tf_op jit(solution)/shard_map/ppermute | solution.py:22
  50.4 13.7 %collective-permute-start.12 = (bf16[128,2048]{1,0:T(8,128)(2,1)S(1)}, bf16[128,2048]{1,0:T(8,128)(2,1)S(1)}, u32[]{:S(2)}, u32[]{:S(2)}) collective-permute-start(bf16[128,2048]{1,0:T(8,128)(2,1)S(1)} %slice.279), channel_id=1, source_target_pairs={{0,3},{1,0},{2,1},{3,2},{4,7},{5,4},{6,5},{7,6},{8,11},{9,8},{10,9... | collective-permute-start | bytes 1572872 | tf_op jit(solution)/shard_map/ppermute | solution.py:22
  53.4 11.1 %collective-permute-start.9 = (bf16[128,2048]{1,0:T(8,128)(2,1)S(1)}, bf16[128,2048]{1,0:T(8,128)(2,1)S(1)}, u32[]{:S(2)}, u32[]{:S(2)}) collective-permute-start(bf16[128,2048]{1,0:T(8,128)(2,1)S(1)} %fusion.69), channel_id=1, source_target_pairs={{0,1},{1,2},{2,3},{3,0},{4,5},{5,6},{6,7},{7,4},{8,9},{9,10},{10,1... | collective-permute-start | bytes 1572872 | tf_op jit(solution)/shard_map/ppermute | solution.py:22
  58.6 11.1 %collective-permute-start.14 = (bf16[128,2048]{1,0:T(8,128)(2,1)S(1)}, bf16[128,2048]{1,0:T(8,128)(2,1)S(1)}, u32[]{:S(2)}, u32[]{:S(2)}) collective-permute-start(bf16[128,2048]{1,0:T(8,128)(2,1)S(1)} %fusion.66), channel_id=1, source_target_pairs={{0,3},{1,0},{2,1},{3,2},{4,7},{5,4},{6,5},{7,6},{8,11},{9,8},{10,9... | collective-permute-start | bytes 1572872 | tf_op jit(solution)/shard_map/ppermute | solution.py:22
  70.3 11.5 %collective-permute-start.15 = (bf16[64,2048]{1,0:T(8,128)(2,1)S(1)}, bf16[64,2048]{1,0:T(8,128)(2,1)S(1)}, u32[]{:S(2)}, u32[]{:S(2)}) collective-permute-start(bf16[64,2048]{1,0:T(8,128)(2,1)S(1)} %get-tuple-element.20), channel_id=1, source_target_pairs={{0,4},{1,5},{2,6},{3,7},{4,8},{5,9},{6,10},{7,11},{8,12},{9,13},{1... | collective-permute-start | bytes 786440 | tf_op jit(solution)/shard_map/ppermute | solution.py:22
  70.4 15.6 %collective-permute-start.16 = (bf16[64,2048]{1,0:T(8,128)(2,1)S(1)}, bf16[64,2048]{1,0:T(8,128)(2,1)S(1)}, u32[]{:S(2)}, u32[]{:S(2)}) collective-permute-start(bf16[64,2048]{1,0:T(8,128)(2,1)S(1)} %get-tuple-element.22), channel_id=1, source_target_pairs={{0,8},{1,9},{2,10},{3,11},{4,12},{5,13},{6,14},{7,15},{8,0},{9,1},... | collective-permute-start | bytes 786440 | tf_op jit(solution)/shard_map/ppermute | solution.py:22
  78.9 7.2 %collective-permute-start.17 = (bf16[64,2048]{1,0:T(8,128)(2,1)S(1)}, bf16[64,2048]{1,0:T(8,128)(2,1)S(1)}, u32[]{:S(2)}, u32[]{:S(2)}) collective-permute-start(bf16[64,2048]{1,0:T(8,128)(2,1)S(1)} %get-tuple-element.21), channel_id=1, source_target_pairs={{0,12},{1,13},{2,14},{3,15},{4,0},{5,1},{6,2},{7,3},{8,4},{9,5},{1... | collective-permute-start | bytes 786440 | tf_op jit(solution)/shard_map/ppermute | solution.py:22

commit v8 on v6

--- a/solution.py
+++ b/solution.py
@@ -24,8 +24,8 @@
 
 def scatter_ring(own, right, far_a, far_b, left, axis):
     cut = far_a.shape[0]
-    got_a = shift_two(far_a.astype(jnp.bfloat16), axis, 1)
-    got_b = shift_two(far_b.astype(jnp.bfloat16), axis, -1)
+    got_a = shift(far_a.astype(jnp.bfloat16), axis, 1)
+    got_b = shift(far_b.astype(jnp.bfloat16), axis, -1)
     right_early = shift(right[cut:].astype(jnp.bfloat16), axis, 1)
     left_early = shift(left[:cut].astype(jnp.bfloat16), axis, -1)
     right_late = shift((right[:cut] + got_a.astype(jnp.float32)).astype(jnp.bfloat16), axis, 1)
@@ -33,11 +33,6 @@
     from_left = jnp.concatenate([right_late, right_early], axis=0).astype(jnp.float32)
     from_right = jnp.concatenate([left_early, left_late], axis=0).astype(jnp.float32)
     return own + from_left + from_right
-
-
-def shift_two(block, stage, step):
-    cut = block.shape[0] // 2
-    return jnp.concatenate([shift(block[:cut], stage, step), shift(block[cut:], stage, step)], axis=0)
 
 
 def scatter_direct(parts, stage):

time: 91.8 us -> 84.6 us (0.922)
  starting transfers between devices: 33.5 us -> 27.8 us
  waiting for transfers between devices: 33.5 us -> 31.4 us
    ppermute x20 -> x18, starting transfers between devices: 33.5 us -> 27.8 us  [shift(): return lax.ppermute(tree, ('dp', 'expert'), pairs)]
    ppermute x20 -> x18, waiting for transfers between devices: 33.5 us -> 31.4 us  [shift(): return lax.ppermute(tree, ('dp', 'expert'), pairs)]
  transfers between devices with their start and end apart: 20 -> 18, of which waited for: 14 -> 13; matrix products, arithmetic and copies ran while one was open for 20% -> 24% of each run, Pallas kernels for 0% -> 0%
where the time goes in v8:
time: 84.6 us; the launch traced here: 83 us
  waiting for transfers between devices  31.4 us (37%)
  starting transfers between devices  27.8 us (33%)
  matrix products  15.1 us (18%)
  other arithmetic  4.87 us (6%)
  local copies, waits for them, and re-layouts  3.61 us (4%)
    ppermute x18, waiting for transfers between devices, shift(): return lax.ppermute(tree, ('dp', 'expert'), pairs)  31.4 us
    ppermute x18, starting transfers between devices, shift(): return lax.ppermute(tree, ('dp', 'expert'), pairs)  27.8 us
    dot_general x6, matrix products, expert_rows(): jnp.dot(rows[:, :width], w_in, preferred_element_type=jnp.float32)  10.3 us
    dot_general x6, matrix products, expert_rows(): jnp.dot(inner, w_out, preferred_element_type=jnp.float32)  4.6 us
  transfers between devices with their start and end apart: 18, of which 13 were waited for; matrix products, arithmetic and copies ran while one was open for 24% of the time, Pallas kernels for 0%

profile of v8, /device:TPU:64, one launch (start us, length us, event | category | flops | bytes accessed | tf_op | source)
XLA Modules:
  0.0 83.0 jit_solution(8380994023080797148)
XLA Ops:
  1.1 1.1 %concatenate.24 = bf16[64,2176]{1,0:T(8,128)(2,1)S(1)} concatenate(bf16[64,2048]{1,0:T(8,128)(2,1)} %param.5, bf16[64,16]{1,0:T(8,128)(2,1)S(1)} %copy.8, bf16[64,16]{1,0:T(8,128)(2,1)S(1)} %copy.9, bf16[64,96]{1,0:T(8,128)(2,1)S(1)} %broadcast_in_dim.67), dimensions={1} | concatenate | bytes 557056 | tf_op jit(solution)/shard_map/concatenate | solution.py:82
  2.1 2.8 %collective-permute-start = (bf16[64,2176]{1,0:T(8,128)(2,1)S(1)}, bf16[64,2176]{1,0:T(8,128)(2,1)}, u32[]{:S(2)}, u32[]{:S(2)}) collective-permute-start(bf16[64,2176]{1,0:T(8,128)(2,1)S(1)} %concatenate.24), channel_id=1, source_target_pairs={{0,12},{1,13},{2,14},{3,15},{4,0},{5,1},{6,2},{7,3},{8,4},{9,5},{1... | collective-permute-start | bytes 835592 | tf_op jit(solution)/shard_map/ppermute | solution.py:22
  5.8 0.9 %collective-permute-start.2 = (bf16[64,2176]{1,0:T(8,128)(2,1)S(1)}, bf16[64,2176]{1,0:T(8,128)(2,1)}, u32[]{:S(2)}, u32[]{:S(2)}) collective-permute-start(bf16[64,2176]{1,0:T(8,128)(2,1)S(1)} %concatenate.24), channel_id=1, source_target_pairs={{0,4},{1,5},{2,6},{3,7},{4,8},{5,9},{6,10},{7,11},{8,12},{9,13},{1... | collective-permute-start | bytes 835592 | tf_op jit(solution)/shard_map/ppermute | solution.py:22
  6.7 5.4 %collective-permute-done = bf16[64,2176]{1,0:T(8,128)(2,1)} collective-permute-done((bf16[64,2176]{1,0:T(8,128)(2,1)S(1)}, bf16[64,2176]{1,0:T(8,128)(2,1)}, u32[]{:S(2)}, u32[]{:S(2)}) %collective-permute-start) | collective-permute-done | bytes 278560 | tf_op jit(solution)/shard_map/ppermute | solution.py:22
  12.1 1.0 %select_reduce_fusion.4 = f32[128]{0:T(128)S(1)} fusion(bf16[64,2176]{1,0:T(8,128)(2,1)} %collective-permute-done, bf16[64,2176]{1,0:T(8,128)(2,1)S(1)} %concatenate.24, pred[16]{0:T(512)(128)(4,1)S(1)} %iota_compare_fusion.1), kind=kLoop, calls=%fused_computation.93 | loop fusion | flops 22400 | bytes 557584 | tf_op jit(solution)/shard_map/reduce_sum | solution.py:50
  13.0 1.0 %pad_maximum_fusion = bf16[128,2176]{1,0:T(8,128)(2,1)S(1)} fusion(bf16[64,2176]{1,0:T(8,128)(2,1)} %collective-permute-done, bf16[64,2176]{1,0:T(8,128)(2,1)S(1)} %concatenate.24), kind=kLoop, calls=%fused_computation.60 | loop fusion | flops 1114112 | bytes 1114112 | tf_op jit(solution)/shard_map/concatenate | solution.py:86
  14.0 3.1 %collective-permute-start.3 = (bf16[128,2176]{1,0:T(8,128)(2,1)S(1)}, bf16[128,2176]{1,0:T(8,128)(2,1)S(1)}, u32[]{:S(2)}, u32[]{:S(2)}) collective-permute-start(bf16[128,2176]{1,0:T(8,128)(2,1)S(1)} %pad_maximum_fusion), channel_id=1, source_target_pairs={{0,3},{1,0},{2,1},{3,2},{4,7},{5,4},{6,5},{7,6},{8,11},{9,8},{10,9... | collective-permute-start | bytes 1671176 | tf_op jit(solution)/shard_map/ppermute | solution.py:22
  17.1 1.0 %constant_dynamic-update-slice_fusion.1 = bf16[128,2176]{1,0:T(8,128)(2,1)S(1)} fusion(bf16[64,2176]{1,0:T(8,128)(2,1)} %collective-permute-done.1), kind=kLoop, calls=%fused_computation.101 | loop fusion | bytes 557056
  18.1 1.0 %constant_dynamic-update-slice_fusion = bf16[128,2176]{1,0:T(8,128)(2,1)S(1)} fusion(bf16[128,2176]{1,0:T(8,128)(2,1)S(1)} %constant_dynamic-update-slice_fusion.1, bf16[64,2176]{1,0:T(8,128)(2,1)} %collective-permute-done.2), kind=kLoop, calls=%fused_computation.100 | loop fusion | bytes 557056 | tf_op jit(solution)/shard_map/concatenate | solution.py:87
  19.3 3.3 %collective-permute-start.4 = (bf16[128,2176]{1,0:T(8,128)(2,1)S(1)}, bf16[128,2176]{1,0:T(8,128)(2,1)S(1)}, u32[]{:S(2)}, u32[]{:S(2)}) collective-permute-start(bf16[128,2176]{1,0:T(8,128)(2,1)S(1)} %constant_dynamic-update-slice_fusion), channel_id=1, source_target_pairs={{0,3},{1,0},{2,1},{3,2},{4,7},{5,4},{6,5},{7,6},{8,11},{9,8},{10,9... | collective-permute-start | bytes 1671176 | tf_op jit(solution)/shard_map/ppermute | solution.py:22
  22.6 3.8 %fusion.10 = f32[128,1536]{1,0:T(8,128)S(1)} fusion(bf16[1,2048,1536]{2,1,0:T(8,128)(2,1)} %param.8, bf16[128,2176]{1,0:T(8,128)(2,1)S(1)} %pad_maximum_fusion), kind=kOutput, calls=%fused_computation.10 | convolution fusion | flops 805306368 | bytes 7602176 | tf_op jit(solution)/shard_map/dot_general | solution.py:65
  26.4 1.0 %fusion.8 = f32[128,1536]{1,0:T(8,128)S(1)} fusion(bf16[1,2048,1536]{2,1,0:T(8,128)(2,1)S(1)} %copy-done.1, bf16[128,2176]{1,0:T(8,128)(2,1)S(1)} %constant_dynamic-update-slice_fusion), kind=kOutput, calls=%fused_computation.8 | convolution fusion | flops 805306368 | bytes 7602176 | tf_op jit(solution)/shard_map/dot_general | solution.py:65
  28.0 2.2 %collective-permute-done.4 = bf16[128,2176]{1,0:T(8,128)(2,1)S(1)} collective-permute-done((bf16[128,2176]{1,0:T(8,128)(2,1)S(1)}, bf16[128,2176]{1,0:T(8,128)(2,1)S(1)}, u32[]{:S(2)}, u32[]{:S(2)}) %collective-permute-start.4) | collective-permute-done | bytes 557088 | tf_op jit(solution)/shard_map/ppermute | solution.py:22
  30.2 1.8 %fusion.6 = f32[256,1536]{1,0:T(8,128)S(1)} fusion(bf16[1,2048,1536]{2,1,0:T(8,128)(2,1)S(1)} %copy-done.1, bf16[256,2176]{1,0:T(8,128)(2,1)S(1)} %constant_dynamic-update-slice_fusion.2), kind=kOutput, calls=%fused_computation.6 | convolution fusion | flops 1610612736 | bytes 8912896 | tf_op jit(solution)/shard_map/dot_general | solution.py:65
  32.0 1.8 %collective-permute-done.10 = bf16[128,2176]{1,0:T(8,128)(2,1)S(1)} collective-permute-done((bf16[128,2176]{1,0:T(8,128)(2,1)S(1)}, bf16[128,2176]{1,0:T(8,128)(2,1)S(1)}, u32[]{:S(2)}, u32[]{:S(2)}) %collective-permute-start.10) | collective-permute-done | bytes 557088 | tf_op jit(solution)/shard_map/ppermute | solution.py:22
  33.9 1.8 %fusion.2 = f32[256,1536]{1,0:T(8,128)S(1)} fusion(bf16[1,2048,1536]{2,1,0:T(8,128)(2,1)S(1)} %copy-done.1, bf16[256,2176]{1,0:T(8,128)(2,1)S(1)} %constant_dynamic-update-slice_fusion.4), kind=kOutput, calls=%fused_computation.2 | convolution fusion | flops 1610612736 | bytes 8912896 | tf_op jit(solution)/shard_map/dot_general | solution.py:65
  35.7 1.9 %collective-permute-start.12 = (bf16[128,2176]{1,0:T(8,128)(2,1)S(1)}, bf16[128,2176]{1,0:T(8,128)(2,1)S(1)}, u32[]{:S(2)}, u32[]{:S(2)}) collective-permute-start(bf16[128,2176]{1,0:T(8,128)(2,1)S(1)} %collective-permute-done.4), channel_id=1, source_target_pairs={{0,3},{1,0},{2,1},{3,2},{4,7},{5,4},{6,5},{7,6},{8,11},{9,8},{10,9... | collective-permute-start | bytes 1671176 | tf_op jit(solution)/shard_map/ppermute | solution.py:22
  37.9 1.1 %fusion.30 = f32[256,2048]{1,0:T(8,128)S(1)} fusion(bf16[1,768,2048]{2,1,0:T(8,128)(2,1)S(1)} %copy-done, f32[256]{0:T(256)S(1)} %get-tuple-element.16, f32[256,1536]{1,0:T(8,128)S(1)} %fusion.6), kind=kOutput, calls=%fused_computation.26 | convolution fusion | flops 808058880 | bytes 6816768 | tf_op jit(solution)/shard_map/dot_general | solution.py:67
  39.8 1.0 %fusion.4 = f32[128,1536]{1,0:T(8,128)S(1)} fusion(bf16[1,2048,1536]{2,1,0:T(8,128)(2,1)S(1)} %copy-done.1, bf16[128,2176]{1,0:T(8,128)(2,1)S(1)} %collective-permute-done.6), kind=kOutput, calls=%fused_computation.4 | convolution fusion | flops 805306368 | bytes 7602176 | tf_op jit(solution)/shard_map/dot_general | solution.py:65
  40.8 4.5 %collective-permute-done.12 = bf16[128,2176]{1,0:T(8,128)(2,1)S(1)} collective-permute-done((bf16[128,2176]{1,0:T(8,128)(2,1)S(1)}, bf16[128,2176]{1,0:T(8,128)(2,1)S(1)}, u32[]{:S(2)}, u32[]{:S(2)}) %collective-permute-start.12) | collective-permute-done | bytes 557088 | tf_op jit(solution)/shard_map/ppermute | solution.py:22
  46.2 1.0 %fusion = f32[128,1536]{1,0:T(8,128)S(1)} fusion(bf16[1,2048,1536]{2,1,0:T(8,128)(2,1)S(1)} %copy-done.1, bf16[128,2176]{1,0:T(8,128)(2,1)S(1)} %collective-permute-done.12), kind=kOutput, calls=%fused_computation | convolution fusion | flops 805306368 | bytes 7602176 | tf_op jit(solution)/shard_map/dot_general | solution.py:65
  47.8 3.3 %collective-permute-start.13 = (bf16[128,2048]{1,0:T(8,128)(2,1)S(1)}, bf16[128,2048]{1,0:T(8,128)(2,1)S(1)}, u32[]{:S(2)}, u32[]{:S(2)}) collective-permute-start(bf16[128,2048]{1,0:T(8,128)(2,1)S(1)} %fusion.78), channel_id=1, source_target_pairs={{0,3},{1,0},{2,1},{3,2},{4,7},{5,4},{6,5},{7,6},{8,11},{9,8},{10,9... | collective-permute-start | bytes 1572872 | tf_op jit(solution)/shard_map/ppermute | solution.py:22
  51.1 1.1 %fusion.39 = f32[256,2048]{1,0:T(8,128)S(1)} fusion(bf16[1,768,2048]{2,1,0:T(8,128)(2,1)S(1)} %copy-done, f32[256]{0:T(256)S(1)} %get-tuple-element.15, f32[256,1536]{1,0:T(8,128)S(1)} %fusion.2), kind=kOutput, calls=%fused_computation.29 | convolution fusion | flops 808058880 | bytes 6816768 | tf_op jit(solution)/shard_map/dot_general | solution.py:67
  52.3 1.9 %collective-permute-start.11 = (bf16[128,2048]{1,0:T(8,128)(2,1)S(1)}, bf16[128,2048]{1,0:T(8,128)(2,1)S(1)}, u32[]{:S(2)}, u32[]{:S(2)}) collective-permute-start(bf16[128,2048]{1,0:T(8,128)(2,1)S(1)} %slice.302), channel_id=1, source_target_pairs={{0,3},{1,0},{2,1},{3,2},{4,7},{5,4},{6,5},{7,6},{8,11},{9,8},{10,9... | collective-permute-start | bytes 1572872 | tf_op jit(solution)/shard_map/ppermute | solution.py:22
  54.2 2.4 %collective-permute-done.7 = bf16[128,2048]{1,0:T(8,128)(2,1)S(1)} collective-permute-done((bf16[128,2048]{1,0:T(8,128)(2,1)S(1)}, bf16[128,2048]{1,0:T(8,128)(2,1)S(1)}, u32[]{:S(2)}, u32[]{:S(2)}) %collective-permute-start.7) | collective-permute-done | bytes 524320 | tf_op jit(solution)/shard_map/ppermute | solution.py:22
  56.8 1.0 %collective-permute-done.13 = bf16[128,2048]{1,0:T(8,128)(2,1)S(1)} collective-permute-done((bf16[128,2048]{1,0:T(8,128)(2,1)S(1)}, bf16[128,2048]{1,0:T(8,128)(2,1)S(1)}, u32[]{:S(2)}, u32[]{:S(2)}) %collective-permute-start.13) | collective-permute-done | bytes 524320 | tf_op jit(solution)/shard_map/ppermute | solution.py:22
  57.9 3.8 %collective-permute-start.14 = (bf16[128,2048]{1,0:T(8,128)(2,1)S(1)}, bf16[128,2048]{1,0:T(8,128)(2,1)S(1)}, u32[]{:S(2)}, u32[]{:S(2)}) collective-permute-start(bf16[128,2048]{1,0:T(8,128)(2,1)S(1)} %fusion.82), channel_id=1, source_target_pairs={{0,3},{1,0},{2,1},{3,2},{4,7},{5,4},{6,5},{7,6},{8,11},{9,8},{10,9... | collective-permute-start | bytes 1572872 | tf_op jit(solution)/shard_map/ppermute | solution.py:22
  63.4 3.7 %collective-permute-done.8 = bf16[128,2048]{1,0:T(8,128)(2,1)S(1)} collective-permute-done((bf16[128,2048]{1,0:T(8,128)(2,1)S(1)}, bf16[128,2048]{1,0:T(8,128)(2,1)S(1)}, u32[]{:S(2)}, u32[]{:S(2)}) %collective-permute-start.8) | collective-permute-done | bytes 524320 | tf_op jit(solution)/shard_map/ppermute | solution.py:22
  67.2 1.9 %collective-permute-done.14 = bf16[128,2048]{1,0:T(8,128)(2,1)S(1)} collective-permute-done((bf16[128,2048]{1,0:T(8,128)(2,1)S(1)}, bf16[128,2048]{1,0:T(8,128)(2,1)S(1)}, u32[]{:S(2)}, u32[]{:S(2)}) %collective-permute-start.14) | collective-permute-done | bytes 524320 | tf_op jit(solution)/shard_map/ppermute | solution.py:22
  69.8 5.2 %collective-permute-start.16 = (bf16[64,2048]{1,0:T(8,128)(2,1)S(1)}, bf16[64,2048]{1,0:T(8,128)(2,1)S(1)}, u32[]{:S(2)}, u32[]{:S(2)}) collective-permute-start(bf16[64,2048]{1,0:T(8,128)(2,1)S(1)} %get-tuple-element.23), channel_id=1, source_target_pairs={{0,8},{1,9},{2,10},{3,11},{4,12},{5,13},{6,14},{7,15},{8,0},{9,1},... | collective-permute-start | bytes 786440 | tf_op jit(solution)/shard_map/ppermute | solution.py:22
  75.0 2.9 %collective-permute-done.15 = bf16[64,2048]{1,0:T(8,128)(2,1)S(1)} collective-permute-done((bf16[64,2048]{1,0:T(8,128)(2,1)S(1)}, bf16[64,2048]{1,0:T(8,128)(2,1)S(1)}, u32[]{:S(2)}, u32[]{:S(2)}) %collective-permute-start.15) | collective-permute-done | bytes 262176 | tf_op jit(solution)/shard_map/ppermute | solution.py:22
  77.9 4.3 %collective-permute-done.16 = bf16[64,2048]{1,0:T(8,128)(2,1)S(1)} collective-permute-done((bf16[64,2048]{1,0:T(8,128)(2,1)S(1)}, bf16[64,2048]{1,0:T(8,128)(2,1)S(1)}, u32[]{:S(2)}, u32[]{:S(2)}) %collective-permute-start.16) | collective-permute-done | bytes 262176 | tf_op jit(solution)/shard_map/ppermute | solution.py:22
  (45 shorter events, 9.0 us)
Async XLA Ops:
  0.0 37.9 %copy-start = (bf16[1,768,2048]{2,1,0:T(8,128)(2,1)S(1)}, bf16[1,768,2048]{2,1,0:T(8,128)(2,1)}, u32[]{:S(2)}) copy-start(bf16[1,768,2048]{2,1,0:T(8,128)(2,1)} %param.9) | copy-start | bytes 9437188
  2.1 9.9 %collective-permute-start = (bf16[64,2176]{1,0:T(8,128)(2,1)S(1)}, bf16[64,2176]{1,0:T(8,128)(2,1)}, u32[]{:S(2)}, u32[]{:S(2)}) collective-permute-start(bf16[64,2176]{1,0:T(8,128)(2,1)S(1)} %concatenate.24), channel_id=1, source_target_pairs={{0,12},{1,13},{2,14},{3,15},{4,0},{5,1},{6,2},{7,3},{8,4},{9,5},{1... | collective-permute-start | bytes 835592 | tf_op jit(solution)/shard_map/ppermute | solution.py:22
  5.0 12.2 %collective-permute-start.1 = (bf16[64,2176]{1,0:T(8,128)(2,1)S(1)}, bf16[64,2176]{1,0:T(8,128)(2,1)}, u32[]{:S(2)}, u32[]{:S(2)}) collective-permute-start(bf16[64,2176]{1,0:T(8,128)(2,1)S(1)} %concatenate.24), channel_id=1, source_target_pairs={{0,8},{1,9},{2,10},{3,11},{4,12},{5,13},{6,14},{7,15},{8,0},{9,1},... | collective-permute-start | bytes 835592 | tf_op jit(solution)/shard_map/ppermute | solution.py:22
  5.8 12.3 %collective-permute-start.2 = (bf16[64,2176]{1,0:T(8,128)(2,1)S(1)}, bf16[64,2176]{1,0:T(8,128)(2,1)}, u32[]{:S(2)}, u32[]{:S(2)}) collective-permute-start(bf16[64,2176]{1,0:T(8,128)(2,1)S(1)} %concatenate.24), channel_id=1, source_target_pairs={{0,4},{1,5},{2,6},{3,7},{4,8},{5,9},{6,10},{7,11},{8,12},{9,13},{1... | collective-permute-start | bytes 835592 | tf_op jit(solution)/shard_map/ppermute | solution.py:22
  14.0 13.9 %collective-permute-start.3 = (bf16[128,2176]{1,0:T(8,128)(2,1)S(1)}, bf16[128,2176]{1,0:T(8,128)(2,1)S(1)}, u32[]{:S(2)}, u32[]{:S(2)}) collective-permute-start(bf16[128,2176]{1,0:T(8,128)(2,1)S(1)} %pad_maximum_fusion), channel_id=1, source_target_pairs={{0,3},{1,0},{2,1},{3,2},{4,7},{5,4},{6,5},{7,6},{8,11},{9,8},{10,9... | collective-permute-start | bytes 1671176 | tf_op jit(solution)/shard_map/ppermute | solution.py:22
  17.1 10.7 %collective-permute-start.5 = (bf16[128,2176]{1,0:T(8,128)(2,1)S(1)}, bf16[128,2176]{1,0:T(8,128)(2,1)S(1)}, u32[]{:S(2)}, u32[]{:S(2)}) collective-permute-start(bf16[128,2176]{1,0:T(8,128)(2,1)S(1)} %pad_maximum_fusion), channel_id=1, source_target_pairs={{0,1},{1,2},{2,3},{3,0},{4,5},{5,6},{6,7},{7,4},{8,9},{9,10},{10,1... | collective-permute-start | bytes 1671176 | tf_op jit(solution)/shard_map/ppermute | solution.py:22
  19.3 7.1 %copy-start.1 = (bf16[1,2048,1536]{2,1,0:T(8,128)(2,1)S(1)}, bf16[1,2048,1536]{2,1,0:T(8,128)(2,1)}, u32[]{:S(2)}) copy-start(bf16[1,2048,1536]{2,1,0:T(8,128)(2,1)} %param.8) | copy-start | bytes 18874372
  19.3 10.8 %collective-permute-start.4 = (bf16[128,2176]{1,0:T(8,128)(2,1)S(1)}, bf16[128,2176]{1,0:T(8,128)(2,1)S(1)}, u32[]{:S(2)}, u32[]{:S(2)}) collective-permute-start(bf16[128,2176]{1,0:T(8,128)(2,1)S(1)} %constant_dynamic-update-slice_fusion), channel_id=1, source_target_pairs={{0,3},{1,0},{2,1},{3,2},{4,7},{5,4},{6,5},{7,6},{8,11},{9,8},{10,9... | collective-permute-start | bytes 1671176 | tf_op jit(solution)/shard_map/ppermute | solution.py:22
  22.6 11.2 %collective-permute-start.10 = (bf16[128,2176]{1,0:T(8,128)(2,1)S(1)}, bf16[128,2176]{1,0:T(8,128)(2,1)S(1)}, u32[]{:S(2)}, u32[]{:S(2)}) collective-permute-start(bf16[128,2176]{1,0:T(8,128)(2,1)S(1)} %constant_dynamic-update-slice_fusion), channel_id=1, source_target_pairs={{0,1},{1,2},{2,3},{3,0},{4,5},{5,6},{6,7},{7,4},{8,9},{9,10},{10,1... | collective-permute-start | bytes 1671176 | tf_op jit(solution)/shard_map/ppermute | solution.py:22
  27.9 11.9 %collective-permute-start.6 = (bf16[128,2176]{1,0:T(8,128)(2,1)S(1)}, bf16[128,2176]{1,0:T(8,128)(2,1)S(1)}, u32[]{:S(2)}, u32[]{:S(2)}) collective-permute-start(bf16[128,2176]{1,0:T(8,128)(2,1)S(1)} %collective-permute-done.5), channel_id=1, source_target_pairs={{0,1},{1,2},{2,3},{3,0},{4,5},{5,6},{6,7},{7,4},{8,9},{9,10},{10,1... | collective-permute-start | bytes 1671176 | tf_op jit(solution)/shard_map/ppermute | solution.py:22
  35.7 9.6 %collective-permute-start.12 = (bf16[128,2176]{1,0:T(8,128)(2,1)S(1)}, bf16[128,2176]{1,0:T(8,128)(2,1)S(1)}, u32[]{:S(2)}, u32[]{:S(2)}) collective-permute-start(bf16[128,2176]{1,0:T(8,128)(2,1)S(1)} %collective-permute-done.4), channel_id=1, source_target_pairs={{0,3},{1,0},{2,1},{3,2},{4,7},{5,4},{6,5},{7,6},{8,11},{9,8},{10,9... | collective-permute-start | bytes 1671176 | tf_op jit(solution)/shard_map/ppermute | solution.py:22
  39.0 23.9 %collective-permute-start.9 = (bf16[128,2048]{1,0:T(8,128)(2,1)S(1)}, bf16[128,2048]{1,0:T(8,128)(2,1)S(1)}, u32[]{:S(2)}, u32[]{:S(2)}) collective-permute-start(bf16[128,2048]{1,0:T(8,128)(2,1)S(1)} %slice.303), channel_id=1, source_target_pairs={{0,1},{1,2},{2,3},{3,0},{4,5},{5,6},{6,7},{7,4},{8,9},{9,10},{10,1... | collective-permute-start | bytes 1572872 | tf_op jit(solution)/shard_map/ppermute | solution.py:22
  46.1 10.5 %collective-permute-start.7 = (bf16[128,2048]{1,0:T(8,128)(2,1)S(1)}, bf16[128,2048]{1,0:T(8,128)(2,1)S(1)}, u32[]{:S(2)}, u32[]{:S(2)}) collective-permute-start(bf16[128,2048]{1,0:T(8,128)(2,1)S(1)} %fusion.66), channel_id=1, source_target_pairs={{0,1},{1,2},{2,3},{3,0},{4,5},{5,6},{6,7},{7,4},{8,9},{9,10},{10,1... | collective-permute-start | bytes 1572872 | tf_op jit(solution)/shard_map/ppermute | solution.py:22
  47.8 10.0 %collective-permute-start.13 = (bf16[128,2048]{1,0:T(8,128)(2,1)S(1)}, bf16[128,2048]{1,0:T(8,128)(2,1)S(1)}, u32[]{:S(2)}, u32[]{:S(2)}) collective-permute-start(bf16[128,2048]{1,0:T(8,128)(2,1)S(1)} %fusion.78), channel_id=1, source_target_pairs={{0,3},{1,0},{2,1},{3,2},{4,7},{5,4},{6,5},{7,6},{8,11},{9,8},{10,9... | collective-permute-start | bytes 1572872 | tf_op jit(solution)/shard_map/ppermute | solution.py:22
  52.3 11.2 %collective-permute-start.11 = (bf16[128,2048]{1,0:T(8,128)(2,1)S(1)}, bf16[128,2048]{1,0:T(8,128)(2,1)S(1)}, u32[]{:S(2)}, u32[]{:S(2)}) collective-permute-start(bf16[128,2048]{1,0:T(8,128)(2,1)S(1)} %slice.302), channel_id=1, source_target_pairs={{0,3},{1,0},{2,1},{3,2},{4,7},{5,4},{6,5},{7,6},{8,11},{9,8},{10,9... | collective-permute-start | bytes 1572872 | tf_op jit(solution)/shard_map/ppermute | solution.py:22
  56.7 10.5 %collective-permute-start.8 = (bf16[128,2048]{1,0:T(8,128)(2,1)S(1)}, bf16[128,2048]{1,0:T(8,128)(2,1)S(1)}, u32[]{:S(2)}, u32[]{:S(2)}) collective-permute-start(bf16[128,2048]{1,0:T(8,128)(2,1)S(1)} %fusion.84), channel_id=1, source_target_pairs={{0,1},{1,2},{2,3},{3,0},{4,5},{5,6},{6,7},{7,4},{8,9},{9,10},{10,1... | collective-permute-start | bytes 1572872 | tf_op jit(solution)/shard_map/ppermute | solution.py:22
  57.9 11.1 %collective-permute-start.14 = (bf16[128,2048]{1,0:T(8,128)(2,1)S(1)}, bf16[128,2048]{1,0:T(8,128)(2,1)S(1)}, u32[]{:S(2)}, u32[]{:S(2)}) collective-permute-start(bf16[128,2048]{1,0:T(8,128)(2,1)S(1)} %fusion.82), channel_id=1, source_target_pairs={{0,3},{1,0},{2,1},{3,2},{4,7},{5,4},{6,5},{7,6},{8,11},{9,8},{10,9... | collective-permute-start | bytes 1572872 | tf_op jit(solution)/shard_map/ppermute | solution.py:22
  69.7 8.2 %collective-permute-start.15 = (bf16[64,2048]{1,0:T(8,128)(2,1)S(1)}, bf16[64,2048]{1,0:T(8,128)(2,1)S(1)}, u32[]{:S(2)}, u32[]{:S(2)}) collective-permute-start(bf16[64,2048]{1,0:T(8,128)(2,1)S(1)} %get-tuple-element.21), channel_id=1, source_target_pairs={{0,4},{1,5},{2,6},{3,7},{4,8},{5,9},{6,10},{7,11},{8,12},{9,13},{1... | collective-permute-start | bytes 786440 | tf_op jit(solution)/shard_map/ppermute | solution.py:22
  69.8 12.4 %collective-permute-start.16 = (bf16[64,2048]{1,0:T(8,128)(2,1)S(1)}, bf16[64,2048]{1,0:T(8,128)(2,1)S(1)}, u32[]{:S(2)}, u32[]{:S(2)}) collective-permute-start(bf16[64,2048]{1,0:T(8,128)(2,1)S(1)} %get-tuple-element.23), channel_id=1, source_target_pairs={{0,8},{1,9},{2,10},{3,11},{4,12},{5,13},{6,14},{7,15},{8,0},{9,1},... | collective-permute-start | bytes 786440 | tf_op jit(solution)/shard_map/ppermute | solution.py:22
  75.0 7.2 %collective-permute-start.17 = (bf16[64,2048]{1,0:T(8,128)(2,1)S(1)}, bf16[64,2048]{1,0:T(8,128)(2,1)S(1)}, u32[]{:S(2)}, u32[]{:S(2)}) collective-permute-start(bf16[64,2048]{1,0:T(8,128)(2,1)S(1)} %get-tuple-element.22), channel_id=1, source_target_pairs={{0,12},{1,13},{2,14},{3,15},{4,0},{5,1},{6,2},{7,3},{8,4},{9,5},{1... | collective-permute-start | bytes 786440 | tf_op jit(solution)/shard_map/ppermute | solution.py:22
